TPU v7x, 128 devices: a whole 4x4x4 slice. The times are simulated.
128 devices in a mesh: dp: 16 (over x, y_lo, core), ctx: 8 (over z, y_hi).
Axes of the slice: x: 4, y: 4 (y_hi: 2, y_lo: 2; y = y_hi * 2 + y_lo), z: 4, core: 2. Of those that a mesh axis runs over, the one named last changes fastest.
Arguments:
- ids: int32 [2048], P('ctx'), may hold values from 0 to 511
- tags: int32 [2048], P('ctx'), may hold values from 0 to 3
- embed: bfloat16 [512, 4096], P(None, 'dp'), may hold values from -21 to 21
- gain: float32 [4096], P('dp'), may hold values from 0.5 to 1.5
- w_in: bfloat16 [3, 4096, 4096], P(None, None, 'dp'), may hold values from -0.125 to 0.125
- short_filt: float32 [3, 7, 4096], P(None, None, 'dp'), may hold values from -2.4 to 2.4
- mr_filt: float32 [128, 4096], P(None, 'dp'), may hold values from -0.9 to 0.9
- rates: float32 [4096], P('dp'), may hold values from 0.004 to 0.12
- w_out: bfloat16 [4096, 4096], P('dp'), may hold values from -0.125 to 0.125
- w_tag: bfloat16 [4096, 4], P('dp'), may hold values from -0.25 to 0.25
Outputs:
- loss: float32 [], replicated
- block_out: bfloat16 [2048, 4096], P('ctx', 'dp')
- d_embed: float32 [512, 4096], P('ctx', 'dp')
- d_gain: float32 [4096], P('dp')
- d_w_in: float32 [3, 4096, 4096], P(None, 'ctx', 'dp')
- d_short: float32 [3, 7, 4096], P(None, None, 'dp')
- d_mr: float32 [128, 4096], P(None, 'dp')
- d_rates: float32 [4096], P('dp')
- d_w_out: float32 [4096, 4096], P('dp', 'ctx')
- d_w_tag: float32 [4096, 4], P('dp')
All inputs are finite; a program needn't handle non-finite values.
Results may differ from a plain program's by a relative error of at most 0.025.
Values may be sent and summed in bfloat16 or wider, within the bound.
No kernel may reach another device: no remote copies, remote signals or barrier semaphores. Data moves between devices by JAX's collectives and lax.ppermute only.
A program may use at most 128 MiB of HBM per device.

v0:
```python
import jax
import jax.numpy as jnp
from jax import lax
from jax.sharding import PartitionSpec as P


def shifted(block, axis, distance):
    devices = range(lax.axis_size(axis))
    route = [(i - distance, i) for i in devices if i - distance in devices]
    return lax.ppermute(block, axis, route)


def short_filter(padded, filters, count):
    taps = filters.shape[1]
    total = jnp.zeros((count,) + padded.shape[1:], jnp.float32)
    for s in range(taps):
        total = total + filters[None, :, s, :] * padded[taps - 1 - s : taps - 1 - s + count].astype(
            jnp.float32
        )
    return total


def body(ids, tags, embed, gain, w_in, short_filt, mr_filt, rates, w_out, w_tag):
    f32 = jnp.float32
    high = lax.Precision.HIGHEST
    rows = ids.shape[0]
    width = w_in.shape[1]
    taps = short_filt.shape[1]
    span = mr_filt.shape[0]
    n_ctx = lax.axis_size("ctx")
    id_hot = (ids[:, None] == jnp.arange(embed.shape[0])[None, :]).astype(jnp.bfloat16)
    x0 = jnp.dot(id_hot, embed, preferred_element_type=f32)
    row_sq = lax.psum(jnp.sum(x0 * x0, axis=1), "dp")
    r = lax.rsqrt(row_sq / width + 1e-06)[:, None]
    u_slab = (x0 * r * gain[None, :]).astype(jnp.bfloat16)
    u = lax.all_gather(u_slab, "dp", axis=1, tiled=True)
    proj = jnp.einsum("td,jdc->tjc", u, w_in, preferred_element_type=f32).astype(jnp.bfloat16)
    head = shifted(proj[rows - (taps - 1) :], "ctx", 1)
    p_ext = jnp.concatenate([head, proj], axis=0)
    z = short_filter(p_ext, short_filt, rows)
    kv = (z[:, 1] * z[:, 2]).astype(jnp.bfloat16)
    kv_head = shifted(kv[rows - (span - 1) :], "ctx", 1)
    kv_ext = jnp.concatenate([kv_head, kv], axis=0)
    q = z[:, 0]
    k = z[:, 1]
    v = z[:, 2]
    lags = jnp.arange(span).astype(f32)[:, None]
    decay = jnp.exp(-rates[None, :] * lags)
    taps_eff = mr_filt * decay
    kv_wide = kv_ext.astype(f32)

    def forward_lag(s, total):
        start = span - 1 - s
        return total + taps_eff[s] * lax.dynamic_slice_in_dim(kv_wide, start, rows, 0)

    m = lax.fori_loop(0, span, forward_lag, jnp.zeros((rows, kv_wide.shape[1]), f32))
    h = (q * m).astype(jnp.bfloat16)
    y_part = jnp.dot(h, w_out, preferred_element_type=f32)
    y = lax.psum_scatter(y_part, "dp", scatter_dimension=1, tiled=True)
    block_out = (x0 + y).astype(jnp.bfloat16)
    logits = lax.psum(jnp.dot(block_out, w_tag, preferred_element_type=f32), "dp")
    top = jnp.max(logits, axis=1)
    lse = top + jnp.log(jnp.sum(jnp.exp(logits - top[:, None]), axis=1))
    tag_hot = (tags[:, None] == jnp.arange(w_tag.shape[1])[None, :]).astype(f32)
    loss_part = jnp.sum(lse - jnp.sum(logits * tag_hot, axis=1))
    dlog = jnp.exp(logits - lse[:, None]) - tag_hot
    dout = jnp.dot(dlog, w_tag.astype(f32).T, precision=high)
    tag_part = jnp.dot(block_out.astype(f32).T, dlog, precision=high)
    dy = dout.astype(jnp.bfloat16)
    dy_full = lax.all_gather(dy, "dp", axis=1, tiled=True)
    dh = lax.dot_general(dy_full, w_out, (((1,), (1,)), ((), ())), preferred_element_type=f32)
    out_part = lax.dot_general(h, dy_full, (((0,), (0,)), ((), ())), preferred_element_type=f32)
    d_w_out = lax.psum_scatter(
        out_part.astype(jnp.bfloat16), "ctx", scatter_dimension=1, tiled=True
    ).astype(jnp.float32)
    dq = dh * m
    dm = dh * q
    dm_tail = shifted(dm[: span - 1].astype(jnp.bfloat16), "ctx", -1).astype(jnp.float32)
    dm_ext = jnp.concatenate([dm, dm_tail], axis=0)

    def backward_lag(s, carry):
        total, corr = carry
        total = total + taps_eff[s] * lax.dynamic_slice_in_dim(dm_ext, s, rows, 0)
        lagged = lax.dynamic_slice_in_dim(kv_wide, span - 1 - s, rows, 0)
        corr = lax.dynamic_update_index_in_dim(corr, jnp.sum(dm * lagged, axis=0), s, 0)
        return (total, corr)

    dkv, corr = lax.fori_loop(
        0, span, backward_lag, (jnp.zeros_like(dm), jnp.zeros(mr_filt.shape, f32))
    )
    mr_part = corr * decay
    rate_part = -jnp.sum(lags * mr_filt * mr_part, axis=0)
    dz = jnp.stack([dq, dkv * v, dkv * k], axis=1)
    dz_tail = shifted(dz[: taps - 1], "ctx", -1)
    dz_ext = jnp.concatenate([dz, dz_tail], axis=0)
    dp = jnp.zeros_like(dz)
    shorts = []
    for s in range(taps):
        dp = dp + short_filt[None, :, s, :] * dz_ext[s : s + rows]
        shorts.append(jnp.sum(dz * p_ext[taps - 1 - s : taps - 1 - s + rows].astype(f32), axis=0))
    short_part = jnp.stack(shorts, axis=1)
    dpb = dp.astype(jnp.bfloat16)
    in_part = jnp.einsum("td,tjc->jdc", u, dpb, preferred_element_type=f32)
    d_w_in = lax.psum_scatter(
        in_part.astype(jnp.bfloat16), "ctx", scatter_dimension=1, tiled=True
    ).astype(jnp.float32)
    du_part = jnp.einsum("tjc,jdc->td", dpb, w_in, preferred_element_type=f32)
    du = lax.psum_scatter(
        du_part.astype(jnp.bfloat16), "dp", scatter_dimension=1, tiled=True
    ).astype(jnp.float32)
    gain_part = jnp.sum(du * x0 * r, axis=0)
    dn = du * gain[None, :]
    row_dot = lax.psum(jnp.sum(dn * x0, axis=1), "dp")[:, None] / width
    dx0 = dout + r * (dn - x0 * r * r * row_dot)
    embed_part = jnp.dot(id_hot.astype(f32).T, dx0, precision=high)
    d_embed = lax.psum_scatter(embed_part, "ctx", scatter_dimension=0, tiled=True)
    totals = (
        lax.psum(loss_part.astype(jnp.bfloat16), "ctx").astype(jnp.float32),
        lax.psum(gain_part.astype(jnp.bfloat16), "ctx").astype(jnp.float32),
        lax.psum(short_part.astype(jnp.bfloat16), "ctx").astype(jnp.float32),
        lax.psum(mr_part.astype(jnp.bfloat16), "ctx").astype(jnp.float32),
        lax.psum(rate_part.astype(jnp.bfloat16), "ctx").astype(jnp.float32),
        lax.psum(tag_part.astype(jnp.bfloat16), "ctx").astype(jnp.float32),
    )
    loss = totals[0] / (rows * n_ctx)
    return (
        loss,
        block_out,
        d_embed,
        totals[1],
        d_w_in,
        totals[2],
        totals[3],
        totals[4],
        d_w_out,
        totals[5],
    )


def solution(mesh):
    placed = (
        P("ctx"),
        P("ctx"),
        P(None, "dp"),
        P("dp"),
        P(None, None, "dp"),
        P(None, None, "dp"),
        P(None, "dp"),
        P("dp"),
        P("dp", None),
        P("dp", None),
    )
    return jax.shard_map(
        body,
        mesh=mesh,
        in_specs=placed,
        out_specs=(
            P(),
            P("ctx", "dp"),
            P("ctx", "dp"),
            P("dp"),
            P(None, "ctx", "dp"),
            P(None, None, "dp"),
            P(None, "dp"),
            P("dp"),
            P("dp", "ctx"),
            P("dp", None),
        ),
        check_vma=False,
    )
```

profile of v0, /device:TPU:0, one launch (start us, length us, event | category | flops | bytes accessed | tf_op | source)
XLA Modules:
  0.0 1189.9 jit_solution(6980538435493755328)
XLA Ops:
  7.2 1.5 multiply_reduce_fusion.1
  8.7 30.5 %psum.63 = f32[256]{0:T(256)S(1)} all-reduce(f32[256]{0:T(256)S(1)} %get-tuple-element.418), channel_id=1, replica_groups=mesh['dp'=16,'ctx'=8] {'dp'}, use_global_device_ids=true, to_apply=%region_1.0 | all-reduce | flops 256 | bytes 2048 | tf_op jit(solution)/shard_map/psum | solution.py:33
  39.2 1.4 multiply_convert_fusion.2
  41.8 32.2 %all-gather.3.cloned.1.call-done = bf16[256,4096]{0,1:T(8,128)(2,1)} async-done(((bf16[256,256]{0,1:T(8,128)(2,1)}), bf16[256,4096]{0,1:T(8,128)(2,1)}) %all-gather.3.cloned.1.call-update) | async-done | bytes 2097168 | tf_op jit(solution)/shard_map/all_gather | solution.py:36
  74.1 5.2 fusion.5
  79.3 4.9 collective-permute-start
  86.4 6.3 collective-permute-start.1
  94.9 107.1 %while.34 = (s32[]{:T(128)}, f32[256,256]{1,0:T(8,128)S(1)}, f32[128,256]{1,0:T(8,128)}, f32[383,256]{1,0:T(8,128)S(1)}, s32[]{:T(128)}, /*index=5*/s32[]{:T(128)}, s32[]{:T(128)}, s32[]{:T(128)}) while((s32[]{:T(128)}, f32[256,256]{1,0:T(8,128)S(1)}, f32[128,256]{1,0:T(8,128)}, f32[383,256]{1,0:T(8,128)S(1)}, s32[]{:T(128)}, ...), condition=%wide.region_3.0_spmd.clone, body=%wide.region_2.0_spmd.clone.sunk | while | flops 196615 | bytes 789661 | solution.py:56
  203.7 2.9 fusion.64
  206.6 70.1 %reduce-scatter.6.cloned.1.call-done = f32[256,256]{0,1:T(8,128)} async-done(((f32[256,4096]{0,1:T(8,128)}), f32[256,256]{0,1:T(8,128)}) %reduce-scatter.6.cloned.1.call-update) | async-done | bytes 262160 | tf_op jit(solution)/shard_map/reduce_scatter | solution.py:59
  277.9 27.8 %psum.64 = f32[256,4]{0,1:T(4,128)S(1)} all-reduce(f32[256,4]{0,1:T(4,128)S(1)} %fusion.65), channel_id=1, replica_groups=mesh['dp'=16,'ctx'=8] {'dp'}, use_global_device_ids=true, to_apply=%region_5.0 | all-reduce | flops 1024 | bytes 8192 | tf_op jit(solution)/shard_map/psum | solution.py:61
  307.0 1.8 fusion.63
  308.9 35.7 %all-gather.5.cloned.1.call-done = bf16[256,4096]{1,0:T(8,128)(2,1)} async-done(((bf16[256,256]{1,0:T(8,128)(2,1)}), bf16[256,4096]{1,0:T(8,128)(2,1)}) %all-gather.5.cloned.1.call-update) | async-done | bytes 2097168 | tf_op jit(solution)/shard_map/all_gather | solution.py:70
  344.6 3.0 multiply_bitcast_fusion.2
  349.6 6.7 collective-permute-done.2
  357.9 401.7 %while.35 = (s32[]{:T(128)}, f32[256,256]{1,0:T(8,128)S(1)}, f32[128,256]{1,0:T(8,128)}, f32[128,256]{1,0:T(8,128)}, f32[383,256]{1,0:T(8,128)}, /*index=5*/f32[...) while((s32[]{:T(128)}, f32[256,256]{1,0:T(8,128)S(1)}, ...), condition=%wide.region_13.14_spmd.clone, body=%wide.region_11.13_spmd.clone.sunk | while | flops 327431 | bytes 1317053 | solution.py:88
  359.7 1.3 dynamic_update_slice.13
  362.9 1.3 dynamic_update_slice.13
  369.1 1.3 dynamic_update_slice.13
  372.3 1.3 dynamic_update_slice.13
  381.7 1.3 dynamic_update_slice.13
  394.3 1.3 dynamic_update_slice.13
  397.4 1.3 dynamic_update_slice.13
  409.9 1.3 dynamic_update_slice.13
  419.4 1.3 dynamic_update_slice.13
  428.8 1.3 dynamic_update_slice.13
  441.3 1.3 dynamic_update_slice.13
  444.5 1.3 dynamic_update_slice.13
  457.0 1.3 dynamic_update_slice.13
  466.4 1.3 dynamic_update_slice.13
  469.6 1.3 dynamic_update_slice.13
  475.8 1.3 dynamic_update_slice.13
  479.0 1.3 dynamic_update_slice.13
  488.4 1.3 dynamic_update_slice.13
  491.5 1.3 dynamic_update_slice.13
  504.1 1.3 dynamic_update_slice.13
  507.2 1.3 dynamic_update_slice.13
  513.5 1.3 dynamic_update_slice.13
  516.6 1.3 dynamic_update_slice.13
  526.0 1.3 dynamic_update_slice.13
  535.5 1.3 dynamic_update_slice.13
  538.6 1.3 dynamic_update_slice.13
  551.1 1.3 dynamic_update_slice.13
  554.3 1.3 dynamic_update_slice.13
  563.7 1.3 dynamic_update_slice.13
  573.1 1.3 dynamic_update_slice.13
  582.5 1.3 dynamic_update_slice.13
  585.7 1.3 dynamic_update_slice.13
  763.1 6.0 collective-permute-done.3
  770.7 6.0 fusion.1
  778.5 3.6 convolution_convert_fusion.1
  782.2 6.2 fusion
  789.5 1.8 copy.31
  792.3 50.8 %reduce-scatter.8.cloned.1.call-done = bf16[256,256]{0,1:T(8,128)(2,1)} async-done(((bf16[256,4096]{0,1:T(8,128)(2,1)}), bf16[256,256]{0,1:T(8,128)(2,1)}) %reduce-scatter.8.cloned.1.call-update) | async-done | bytes 131088 | tf_op jit(solution)/shard_map/reduce_scatter | solution.py:108
  844.3 28.2 %psum.66 = f32[256]{0:T(256)S(1)} all-reduce(f32[256]{0:T(256)S(1)} %get-tuple-element.367), channel_id=1, replica_groups=mesh['dp'=16,'ctx'=8] {'dp'}, use_global_device_ids=true, to_apply=%region_16.17 | all-reduce | flops 256 | bytes 2048 | tf_op jit(solution)/shard_map/psum | solution.py:113
  872.5 2.5 fusion.40
  875.0 54.0 %all-reduce.3.cloned.1.call-done = bf16[128,256]{1,0:T(8,128)(2,1)} async-done(((bf16[128,256]{1,0:T(8,128)(2,1)}), bf16[128,256]{1,0:T(8,128)(2,1)}) %all-reduce.3.cloned.1.call-update) | async-done | bytes 65552 | tf_op jit(solution)/shard_map/psum | solution.py:121
  929.0 1.5 convert_element_type.156
  930.5 75.9 %reduce-scatter.14.cloned.1.call-done = bf16[256,512]{1,0:T(8,128)(2,1)} async-done(((bf16[256,4096]{1,0:T(8,128)(2,1)}), bf16[256,512]{1,0:T(8,128)(2,1)}) %reduce-scatter.14.cloned.1.call-update) | async-done | bytes 262160 | tf_op jit(solution)/shard_map/reduce_scatter | solution.py:73
  1006.4 1.8 convert_element_type.160
  1008.2 41.1 %all-reduce = (bf16[]{:T(256)}, bf16[3,7,256]{2,0,1:T(4,128)(2,1)S(1)}, bf16[256]{0:T(256)(128)(2,1)S(1)}, bf16[256]{0:T(256)(128)(2,1)S(1)}, bf16[256,4]{0,1:T(4,128)(2,1)S(1)}) all-reduce(bf16[]{:T(256)} %get-tuple-element.397, ...), channel_id=1, replica_groups=mesh['dp'=16,'ctx'=8] {'ctx'}, use_global_device_ids=true, to_apply=%region_10.0 | all-reduce | flops 6913 | bytes 27652 | tf_op jit(solution)/shard_map/psum | solution.py:118
  1052.4 55.7 %reduce-scatter.12.cloned.1.call-done = bf16[3,512,256]{1,2,0:T(8,128)(2,1)} async-done(((bf16[3,4096,256]{1,2,0:T(8,128)(2,1)}), bf16[3,512,256]{1,2,0:T(8,128)(2,1)}) %reduce-scatter.12.cloned.1.call-update) | async-done | bytes 786448 | tf_op jit(solution)/shard_map/reduce_scatter | solution.py:104
  1108.1 2.5 copy.35
  1110.6 71.3 %reduce-scatter.10.cloned.1.call-done = f32[64,256]{1,0:T(8,128)} async-done(((f32[512,256]{1,0:T(8,128)}), f32[64,256]{1,0:T(8,128)}) %reduce-scatter.10.cloned.1.call-update) | async-done | bytes 65552 | tf_op jit(solution)/shard_map/reduce_scatter | solution.py:116
  (751 shorter events, 488.7 us)
Async XLA Ops:
  7.2 196.5 %copy-start = (bf16[256,4096]{1,0:T(8,128)(2,1)S(1)}, bf16[256,4096]{1,0:T(8,128)(2,1)}, u32[]{:S(2)}) copy-start(bf16[256,4096]{1,0:T(8,128)(2,1)} %param.22) | copy-start | bytes 6291460
  7.2 66.9 %all-gather.3.cloned.1.call-start = ((), (), s32[]{:S(2)}) async-start(), calls=%async_computation.5 | async-start | bytes 2228224 | tf_op jit(solution)/shard_map/all_gather | solution.py:36
  8.7 268.1 %copy-start.5 = (f32[256,256]{0,1:T(8,128)}, f32[256,256]{0,1:T(8,128)S(1)}, u32[]{:S(2)}) copy-start(f32[256,256]{0,1:T(8,128)S(1)} %get-tuple-element.419) | copy-start | bytes 786436
  39.2 2.6 copy-start.24
  40.7 236.1 %reduce-scatter.6.cloned.1.call-start = ((), (), s32[]{:S(2)}) async-start(), calls=%async_computation.6 | async-start | bytes 4456448 | tf_op jit(solution)/shard_map/reduce_scatter | solution.py:59
  41.8 43.8 %copy-start.14 = (f32[3,256]{1,0:T(4,128)}, f32[3,256]{1,0:T(4,128)S(1)}, u32[]{:S(2)}) copy-start(f32[3,256]{1,0:T(4,128)S(1)} %get-tuple-element.426) | copy-start | bytes 9220
  41.8 43.8 %copy-start.16 = (f32[3,256]{1,0:T(4,128)}, f32[3,256]{1,0:T(4,128)S(1)}, u32[]{:S(2)}) copy-start(f32[3,256]{1,0:T(4,128)S(1)} %get-tuple-element.427) | copy-start | bytes 9220
  41.8 43.8 %copy-start.18 = (f32[3,256]{1,0:T(4,128)}, f32[3,256]{1,0:T(4,128)S(1)}, u32[]{:S(2)}) copy-start(f32[3,256]{1,0:T(4,128)S(1)} %get-tuple-element.422) | copy-start | bytes 9220
  41.8 43.8 %copy-start.20 = (f32[3,256]{1,0:T(4,128)}, f32[3,256]{1,0:T(4,128)S(1)}, u32[]{:S(2)}) copy-start(f32[3,256]{1,0:T(4,128)S(1)} %get-tuple-element.423) | copy-start | bytes 9220
  41.8 42.4 %copy-start.36 = (f32[256]{0:T(256)S(1)}, f32[256]{0:T(256)}, u32[]{:S(2)}) copy-start(f32[256]{0:T(256)} %param.21) | copy-start | bytes 3076
  79.3 13.4 %copy-start.9 = (f32[128,256]{1,0:T(8,128)S(1)}, f32[128,256]{1,0:T(8,128)}, u32[]{:S(2)}) copy-start(f32[128,256]{1,0:T(8,128)} %param.20) | copy-start | bytes 393220
  79.3 6.3 collective-permute-start
  84.2 10.6 copy-start.33
  84.3 10.6 copy-start.27
  84.3 1.3 copy-start.22
  85.6 0.7 copy-start.12
  86.3 6.4 copy-start.1
  86.4 7.6 collective-permute-start.1
  203.0 0.7 copy-start.7
  206.6 71.2 %copy-start.32 = (bf16[256,4]{0,1:T(4,128)(2,1)S(1)}, bf16[256,4]{0,1:T(4,128)(2,1)}, u32[]{:S(2)}) copy-start(bf16[256,4]{0,1:T(4,128)(2,1)} %param.23) | copy-start | bytes 6148
  206.6 138.0 %all-gather.5.cloned.1.call-start = ((), (), s32[]{:S(2)}) async-start(), calls=%async_computation.7 | async-start | bytes 2228224 | tf_op jit(solution)/shard_map/all_gather | solution.py:70
  307.0 40.6 %copy-start.29 = (f32[256]{0:T(256)}, f32[256]{0:T(256)S(1)}, u32[]{:S(2)}) copy-start(f32[256]{0:T(256)S(1)} %get-tuple-element.398) | copy-start | bytes 3076
  308.8 534.3 %reduce-scatter.8.cloned.1.call-start = ((), (), s32[]{:S(2)}) async-start(), calls=%async_computation.8 | async-start | bytes 2228224 | tf_op jit(solution)/shard_map/reduce_scatter | solution.py:108
  348.3 8.0 collective-permute-start.2
  759.6 9.6 copy-start.2
  759.6 9.7 copy-start.15
  759.6 9.7 copy-start.17
  759.6 9.7 copy-start.19
  759.6 9.7 copy-start.21
  759.6 9.7 copy-start.23
  760.7 8.5 copy-start.3
  761.8 7.3 collective-permute-start.3
  770.0 0.7 copy-start.6
  776.7 0.9 copy-start.10
  776.7 1.0 copy-start.11
  776.7 1.0 copy-start.28
  776.7 1.0 copy-start.34
  776.7 1.8 copy-start.8
  776.7 152.3 %all-reduce.3.cloned.1.call-start = ((), (), s32[]{:S(2)}) async-start(), calls=%async_computation.11 | async-start | bytes 131072 | tf_op jit(solution)/shard_map/psum | solution.py:121
  778.4 228.0 %reduce-scatter.14.cloned.1.call-start = ((), (), s32[]{:S(2)}) async-start(), calls=%async_computation.12 | async-start | bytes 2359296 | tf_op jit(solution)/shard_map/reduce_scatter | solution.py:73
  782.1 326.0 %reduce-scatter.12.cloned.1.call-start = ((), (), s32[]{:S(2)}) async-start(), calls=%async_computation.10 | async-start | bytes 7077888 | tf_op jit(solution)/shard_map/reduce_scatter | solution.py:104
  788.4 2.9 copy-start.30
  788.4 2.9 copy-start.31
  788.4 3.0 copy-start.4
  788.4 3.1 copy-start.13
  788.5 54.7 %copy-start.25 = (f32[256]{0:T(256)S(1)}, f32[256]{0:T(256)}, u32[]{:S(2)}) copy-start(f32[256]{0:T(256)} %copy-done.24) | copy-start | bytes 3076
  788.5 54.6 %copy-start.26 = (f32[256]{0:T(256)S(1)}, f32[256]{0:T(256)}, u32[]{:S(2)}) copy-start(f32[256]{0:T(256)} %param.17) | copy-start | bytes 3076
  788.5 84.0 %copy-start.35 = (s32[256]{0:T(256)S(1)}, s32[256]{0:T(256)}, u32[]{:S(2)}) copy-start(s32[256]{0:T(256)} %param.14) | copy-start | bytes 3076
  788.5 393.4 %reduce-scatter.10.cloned.1.call-start = ((), (), s32[]{:S(2)}) async-start(), calls=%async_computation.9 | async-start | bytes 589824 | tf_op jit(solution)/shard_map/reduce_scatter | solution.py:116
Sparse Core Ops, SparseCore 0:
  40.8 33.2 all-gather.2
  206.7 70.0 reduce-scatter.5
  309.0 35.6 all-gather.4
  776.8 66.2 reduce-scatter.7
  846.0 82.9 all-reduce.2
  932.6 73.7 reduce-scatter.13
  1010.3 97.7 reduce-scatter.11
  1112.2 69.6 reduce-scatter.9
where the time goes:
time: 1210 us; the launch traced here: 1190 us
  waiting for transfers between devices  460 us (38%)
  local copies, waits for them, and re-layouts  358 us (30%)
  other arithmetic  176 us (15%)
  blocking collectives  128 us (11%)
  matrix products  33.1 us (3%)
  between operations  16.5 us (1%)
  starting transfers between devices  14.3 us (1%)
    dynamic_update_slice x128, local copies, waits for them, and re-layouts, backward_lag(): lax.dynamic_update_index_in_dim(corr, jnp.sum(dm * lagged, axis=0), s, 0)  168 us
    add x128, other arithmetic, backward_lag(): total = total + taps_eff[s] * lax.dynamic_slice_in_dim(dm_ext, s, rows, 0)  143 us
    dynamic_slice x128, local copies, waits for them, and re-layouts, forward_lag(): taps_eff[s] * lax.dynamic_slice_in_dim(kv_wide, start, rows, 0)  90.3 us
    dynamic_slice x128, local copies, waits for them, and re-layouts, backward_lag(): total = total + taps_eff[s] * lax.dynamic_slice_in_dim(dm_ext, s, rows, 0)  89.7 us
    reduce_scatter x1, waiting for transfers between devices, body(): lax.psum_scatter(out_part.astype(jnp.bfloat16), 'ctx', scatter_dimension=...  75.9 us
    reduce_scatter x1, waiting for transfers between devices, body(): lax.psum_scatter(embed_part, 'ctx', scatter_dimension=0, tiled=True)  71.3 us
    reduce_scatter x1, waiting for transfers between devices, body(): y = lax.psum_scatter(y_part, 'dp', scatter_dimension=1, tiled=True)  70.1 us
    reduce_scatter x1, waiting for transfers between devices, body(): lax.psum_scatter(in_part.astype(jnp.bfloat16), 'ctx', scatter_dimension=1...  55.7 us
  transfers between devices with their start and end apart: 12, of which 12 were waited for; matrix products, arithmetic and copies ran while one was open for 2% of the time, Pallas kernels for 0%

commit v1 on v0

--- a/solution.py
+++ b/solution.py
@@ -2,6 +2,74 @@
 import jax.numpy as jnp
 from jax import lax
 from jax.sharding import PartitionSpec as P
+from jax.experimental import pallas as pl
+from jax.experimental.pallas import tpu as pltpu
+
+LANES = 128
+ROW_BLOCK = 64
+
+
+def medium_forward(kv_ext, taps_eff, rows):
+    span, width = taps_eff.shape
+
+    def kernel(kv_ref, g_ref, m_ref):
+        for rb in range(0, rows, ROW_BLOCK):
+            acc = jnp.zeros((ROW_BLOCK, LANES), jnp.float32)
+            for s in range(span):
+                start = span - 1 - s + rb
+                acc = acc + g_ref[s : s + 1, :] * kv_ref[start : start + ROW_BLOCK, :]
+            m_ref[rb : rb + ROW_BLOCK, :] = acc
+
+    ext = kv_ext.shape[0]
+    return pl.pallas_call(
+        kernel,
+        out_shape=jax.ShapeDtypeStruct((rows, width), jnp.float32),
+        grid=(width // LANES,),
+        in_specs=[
+            pl.BlockSpec((ext, LANES), lambda c: (0, c)),
+            pl.BlockSpec((span, LANES), lambda c: (0, c)),
+        ],
+        out_specs=pl.BlockSpec((rows, LANES), lambda c: (0, c)),
+    )(kv_ext, taps_eff)
+
+
+def medium_backward(dm_ext, kv_ext, taps_eff, rows):
+    span, width = taps_eff.shape
+
+    def kernel(dm_ref, kv_ref, g_ref, dkv_ref, corr_ref):
+        for rb in range(0, rows, ROW_BLOCK):
+            acc = jnp.zeros((ROW_BLOCK, LANES), jnp.float32)
+            for s in range(span):
+                acc = acc + g_ref[s : s + 1, :] * dm_ref[s + rb : s + rb + ROW_BLOCK, :]
+            dkv_ref[rb : rb + ROW_BLOCK, :] = acc
+        for s0 in range(0, span, 8):
+            parts = []
+            for s in range(s0, s0 + 8):
+                start = span - 1 - s
+                part = jnp.zeros((8, LANES), jnp.float32)
+                for rb in range(0, rows, 8):
+                    part = part + dm_ref[rb : rb + 8, :] * kv_ref[start + rb : start + rb + 8, :]
+                parts.append(jnp.sum(part, axis=0, keepdims=True))
+            corr_ref[s0 : s0 + 8, :] = jnp.concatenate(parts, axis=0)
+
+    ext = kv_ext.shape[0]
+    return pl.pallas_call(
+        kernel,
+        out_shape=(
+            jax.ShapeDtypeStruct((rows, width), jnp.float32),
+            jax.ShapeDtypeStruct((span, width), jnp.float32),
+        ),
+        grid=(width // LANES,),
+        in_specs=[
+            pl.BlockSpec((dm_ext.shape[0], LANES), lambda c: (0, c)),
+            pl.BlockSpec((ext, LANES), lambda c: (0, c)),
+            pl.BlockSpec((span, LANES), lambda c: (0, c)),
+        ],
+        out_specs=(
+            pl.BlockSpec((rows, LANES), lambda c: (0, c)),
+            pl.BlockSpec((span, LANES), lambda c: (0, c)),
+        ),
+    )(dm_ext, kv_ext, taps_eff)
 
 
 def shifted(block, axis, distance):
@@ -40,7 +108,7 @@
     z = short_filter(p_ext, short_filt, rows)
     kv = (z[:, 1] * z[:, 2]).astype(jnp.bfloat16)
     kv_head = shifted(kv[rows - (span - 1) :], "ctx", 1)
-    kv_ext = jnp.concatenate([kv_head, kv], axis=0)
+    kv_ext = jnp.concatenate([kv_head, kv, jnp.zeros((1,) + kv.shape[1:], kv.dtype)], axis=0)
     q = z[:, 0]
     k = z[:, 1]
     v = z[:, 2]
@@ -49,11 +117,7 @@
     taps_eff = mr_filt * decay
     kv_wide = kv_ext.astype(f32)
 
-    def forward_lag(s, total):
-        start = span - 1 - s
-        return total + taps_eff[s] * lax.dynamic_slice_in_dim(kv_wide, start, rows, 0)
-
-    m = lax.fori_loop(0, span, forward_lag, jnp.zeros((rows, kv_wide.shape[1]), f32))
+    m = medium_forward(kv_wide, taps_eff, rows)
     h = (q * m).astype(jnp.bfloat16)
     y_part = jnp.dot(h, w_out, preferred_element_type=f32)
     y = lax.psum_scatter(y_part, "dp", scatter_dimension=1, tiled=True)
@@ -76,18 +140,8 @@
     dq = dh * m
     dm = dh * q
     dm_tail = shifted(dm[: span - 1].astype(jnp.bfloat16), "ctx", -1).astype(jnp.float32)
-    dm_ext = jnp.concatenate([dm, dm_tail], axis=0)
-
-    def backward_lag(s, carry):
-        total, corr = carry
-        total = total + taps_eff[s] * lax.dynamic_slice_in_dim(dm_ext, s, rows, 0)
-        lagged = lax.dynamic_slice_in_dim(kv_wide, span - 1 - s, rows, 0)
-        corr = lax.dynamic_update_index_in_dim(corr, jnp.sum(dm * lagged, axis=0), s, 0)
-        return (total, corr)
-
-    dkv, corr = lax.fori_loop(
-        0, span, backward_lag, (jnp.zeros_like(dm), jnp.zeros(mr_filt.shape, f32))
-    )
+    dm_ext = jnp.concatenate([dm, dm_tail, jnp.zeros((1,) + dm.shape[1:], f32)], axis=0)
+    dkv, corr = medium_backward(dm_ext, kv_wide, taps_eff, rows)
     mr_part = corr * decay
     rate_part = -jnp.sum(lags * mr_filt * mr_part, axis=0)
     dz = jnp.stack([dq, dkv * v, dkv * k], axis=1)

time: 1210 us -> 690 us (0.57); the launches traced: 1190 us -> 689 us
  local copies, waits for them, and re-layouts: 358 us -> 12.1 us
  other arithmetic: 176 us -> 19.2 us
    dynamic_slice x256 -> x0, local copies, waits for them, and re-layouts: 180 us -> none  [the longest x128 90.3 us: forward_lag(): taps_eff[s] * lax.dynamic_slice_in_dim(kv_wide, start, rows, 0)]
    dynamic_update_slice x128 -> x0, local copies, waits for them, and re-layouts: 168 us -> none  [backward_lag(): lax.dynamic_update_index_in_dim(corr, jnp.sum(dm * lagged, axis=0), s, 0)]
    add x256 -> x0, other arithmetic: 157 us -> none  [the longest x128 143 us: backward_lag(): total = total + taps_eff[s] * lax.dynamic_slice_in_dim(dm_ext, s, rows, 0)]
  transfers between devices with their start and end apart: 12 -> 12, of which waited for: 12 -> 12; matrix products, arithmetic and copies ran while one was open for 2% -> 5% of each run, Pallas kernels for 0% -> 0%
where the time goes in v1:
time: 690 us; the launch traced here: 689 us
  waiting for transfers between devices  454 us (66%)
  blocking collectives  128 us (19%)
  matrix products  33.8 us (5%)
  other arithmetic  19.2 us (3%)
  between operations  16.4 us (2%)
  starting transfers between devices  13.7 us (2%)
  local copies, waits for them, and re-layouts  12.1 us (2%)
  Pallas kernels  11.3 us (2%)
    reduce_scatter x1, waiting for transfers between devices, body(): lax.psum_scatter(out_part.astype(jnp.bfloat16), 'ctx', scatter_dimension=...  75.9 us
    reduce_scatter x1, waiting for transfers between devices, body(): lax.psum_scatter(embed_part, 'ctx', scatter_dimension=0, tiled=True)  71.3 us
    reduce_scatter x1, waiting for transfers between devices, body(): y = lax.psum_scatter(y_part, 'dp', scatter_dimension=1, tiled=True)  69.7 us
    reduce_scatter x1, waiting for transfers between devices, body(): lax.psum_scatter(in_part.astype(jnp.bfloat16), 'ctx', scatter_dimension=1...  55.7 us
    psum x1, waiting for transfers between devices, body(): lax.psum(mr_part.astype(jnp.bfloat16), 'ctx').astype(jnp.float32)  54.3 us
    reduce_scatter x1, waiting for transfers between devices, body(): lax.psum_scatter(du_part.astype(jnp.bfloat16), 'dp', scatter_dimension=1,...  46.6 us
    psum x1, blocking collectives, body(): lax.psum(loss_part.astype(jnp.bfloat16), 'ctx').astype(jnp.float32)  41.1 us
    all_gather x1, waiting for transfers between devices, body(): dy_full = lax.all_gather(dy, 'dp', axis=1, tiled=True)  35.9 us
  transfers between devices with their start and end apart: 12, of which 12 were waited for; matrix products, arithmetic and copies ran while one was open for 5% of the time, Pallas kernels for 0%

profile of v1, /device:TPU:0, one launch (start us, length us, event | category | flops | bytes accessed | tf_op | source)
XLA Modules:
  0.0 688.6 jit_solution(17627525775846174425)
XLA Ops:
  7.2 1.5 multiply_reduce_fusion
  8.7 30.5 %psum.63 = f32[256]{0:T(256)S(1)} all-reduce(f32[256]{0:T(256)S(1)} %get-tuple-element.69), channel_id=1, replica_groups=mesh['dp'=16,'ctx'=8] {'dp'}, use_global_device_ids=true, to_apply=%region_1.0 | all-reduce | flops 256 | bytes 2048 | tf_op jit(solution)/shard_map/psum | solution.py:101
  39.2 1.4 multiply_convert_fusion.2
  40.7 1.0 fusion.62
  41.7 0.6 copy_bitcast_fusion.2
  42.3 0.6 copy_bitcast_fusion.4
  42.9 0.6 copy_bitcast_fusion
  43.5 30.5 %all-gather.3.cloned.1.call-done = bf16[256,4096]{0,1:T(8,128)(2,1)} async-done(((bf16[256,256]{0,1:T(8,128)(2,1)}), bf16[256,4096]{0,1:T(8,128)(2,1)}) %all-gather.3.cloned.1.call-update) | async-done | bytes 2097168 | tf_op jit(solution)/shard_map/all_gather | solution.py:104
  74.1 5.3 fusion.5
  79.4 4.9 collective-permute-start
  84.3 1.3 collective-permute-done
  85.7 0.7 fusion.13
  86.4 5.7 collective-permute-start.1
  92.2 0.8 fusion.53.g_ref
  92.9 0.1 pad.12.clone
  93.0 1.0 collective-permute-done.1
  94.0 0.9 maximum_convert_fusion.kv_ref
  94.9 4.7 shard_map.177
  99.6 1.0 multiply_convert_fusion
  100.6 0.6 copy-done.8
  101.3 2.9 fusion.64
  104.2 69.7 %reduce-scatter.6.cloned.1.call-done = f32[256,256]{0,1:T(8,128)} async-done(((f32[256,4096]{0,1:T(8,128)}), f32[256,256]{0,1:T(8,128)}) %reduce-scatter.6.cloned.1.call-update) | async-done | bytes 262160 | tf_op jit(solution)/shard_map/reduce_scatter | solution.py:123
  173.9 1.0 add_convert_fusion
  174.9 0.6 copy-done.7
  175.5 0.1 fusion.65
  175.7 27.9 %psum.64 = f32[256,4]{0,1:T(4,128)S(1)} all-reduce(f32[256,4]{0,1:T(4,128)S(1)} %fusion.65), channel_id=1, replica_groups=mesh['dp'=16,'ctx'=8] {'dp'}, use_global_device_ids=true, to_apply=%region_3.0 | all-reduce | flops 1024 | bytes 8192 | tf_op jit(solution)/shard_map/psum | solution.py:125
  203.6 0.7 select_reduce_fusion
  204.3 0.6 subtract_reduce_fusion
  205.0 1.8 fusion.63
  206.8 35.9 %all-gather.5.cloned.1.call-done = bf16[256,4096]{1,0:T(8,128)(2,1)} async-done(((bf16[256,256]{1,0:T(8,128)(2,1)}), bf16[256,4096]{1,0:T(8,128)(2,1)}) %all-gather.5.cloned.1.call-update) | async-done | bytes 2097168 | tf_op jit(solution)/shard_map/all_gather | solution.py:134
  242.7 2.3 multiply_bitcast_fusion.2
  245.0 1.3 collective-permute-start.2
  246.4 6.3 collective-permute-done.2
  252.7 0.9 maximum_maximum_fusion.dm_ref
  253.6 6.6 shard_map.178
  260.2 1.0 multiply_bitcast_fusion.1
  261.3 1.5 collective-permute-start.3
  262.8 5.8 collective-permute-done.3
  268.8 0.7 fusion.22
  269.5 5.9 fusion.1
  275.5 0.8 copy-done.11
  276.4 2.0 fusion.56
  278.5 3.7 convolution_convert_fusion.1
  282.2 6.1 fusion
  288.4 1.7 copy.34
  290.1 1.8 copy.31
  291.9 1.7 convolution_convert_fusion.2
  293.6 1.3 fusion.19
  295.0 46.6 %reduce-scatter.8.cloned.1.call-done = bf16[256,256]{0,1:T(8,128)(2,1)} async-done(((bf16[256,4096]{0,1:T(8,128)(2,1)}), bf16[256,256]{0,1:T(8,128)(2,1)}) %reduce-scatter.8.cloned.1.call-update) | async-done | bytes 131088 | tf_op jit(solution)/shard_map/reduce_scatter | solution.py:162
  341.6 1.1 fusion.43
  342.7 28.2 %psum.66 = f32[256]{0:T(256)S(1)} all-reduce(f32[256]{0:T(256)S(1)} %get-tuple-element.42), channel_id=1, replica_groups=mesh['dp'=16,'ctx'=8] {'dp'}, use_global_device_ids=true, to_apply=%region_11.0 | all-reduce | flops 256 | bytes 2048 | tf_op jit(solution)/shard_map/psum | solution.py:167
  371.0 2.4 fusion.40
  373.5 54.3 %all-reduce.3.cloned.1.call-done = bf16[128,256]{1,0:T(8,128)(2,1)} async-done(((bf16[128,256]{1,0:T(8,128)(2,1)}), bf16[128,256]{1,0:T(8,128)(2,1)}) %all-reduce.3.cloned.1.call-update) | async-done | bytes 65552 | tf_op jit(solution)/shard_map/psum | solution.py:175
  427.8 1.5 convert_element_type.156
  429.3 75.9 %reduce-scatter.14.cloned.1.call-done = bf16[256,512]{1,0:T(8,128)(2,1)} async-done(((bf16[256,4096]{1,0:T(8,128)(2,1)}), bf16[256,512]{1,0:T(8,128)(2,1)}) %reduce-scatter.14.cloned.1.call-update) | async-done | bytes 262160 | tf_op jit(solution)/shard_map/reduce_scatter | solution.py:137
  505.2 1.8 convert_element_type.160
  507.0 41.1 %all-reduce = (bf16[]{:T(256)}, bf16[3,7,256]{2,0,1:T(4,128)(2,1)S(1)}, bf16[256]{0:T(256)(128)(2,1)S(1)}, bf16[256]{0:T(256)(128)(2,1)S(1)}, bf16[256,4]{0,1:T(4,128)(2,1)S(1)}) all-reduce(bf16[]{:T(256)} %get-tuple-element.50, ...), channel_id=1, replica_groups=mesh['dp'=16,'ctx'=8] {'ctx'}, use_global_device_ids=true, to_apply=%region_8.0 | all-reduce | flops 6913 | bytes 27652 | tf_op jit(solution)/shard_map/psum | solution.py:172
  548.1 0.6 convert_element_type.150
  548.7 0.6 convert_element_type.158
  549.2 0.6 convert_element_type.162
  549.8 0.6 copy.36
  551.1 55.7 %reduce-scatter.12.cloned.1.call-done = bf16[3,512,256]{1,2,0:T(8,128)(2,1)} async-done(((bf16[3,4096,256]{1,2,0:T(8,128)(2,1)}), bf16[3,512,256]{1,2,0:T(8,128)(2,1)}) %reduce-scatter.12.cloned.1.call-update) | async-done | bytes 786448 | tf_op jit(solution)/shard_map/reduce_scatter | solution.py:158
  606.8 2.5 copy.35
  609.4 71.3 %reduce-scatter.10.cloned.1.call-done = f32[64,256]{1,0:T(8,128)} async-done(((f32[512,256]{1,0:T(8,128)}), f32[64,256]{1,0:T(8,128)}) %reduce-scatter.10.cloned.1.call-update) | async-done | bytes 65552 | tf_op jit(solution)/shard_map/reduce_scatter | solution.py:170
  (114 shorter events, 1.1 us)
Async XLA Ops:
  7.2 94.1 %copy-start = (bf16[256,4096]{1,0:T(8,128)(2,1)S(1)}, bf16[256,4096]{1,0:T(8,128)(2,1)}, u32[]{:S(2)}) copy-start(bf16[256,4096]{1,0:T(8,128)(2,1)} %param.18) | copy-start | bytes 6291460
  7.2 66.9 %all-gather.3.cloned.1.call-start = ((), (), s32[]{:S(2)}) async-start(), calls=%async_computation.5 | async-start | bytes 2228224 | tf_op jit(solution)/shard_map/all_gather | solution.py:104
  8.7 165.2 %copy-start.5 = (f32[256,256]{0,1:T(8,128)}, f32[256,256]{0,1:T(8,128)S(1)}, u32[]{:S(2)}) copy-start(f32[256,256]{0,1:T(8,128)S(1)} %get-tuple-element.70) | copy-start | bytes 786436
  39.2 4.3 copy-start.27
  40.7 133.2 %reduce-scatter.6.cloned.1.call-start = ((), (), s32[]{:S(2)}) async-start(), calls=%async_computation.6 | async-start | bytes 4456448 | tf_op jit(solution)/shard_map/reduce_scatter | solution.py:123
  42.3 43.3 %copy-start.13 = (f32[3,256]{1,0:T(4,128)}, f32[3,256]{1,0:T(4,128)S(1)}, u32[]{:S(2)}) copy-start(f32[3,256]{1,0:T(4,128)S(1)} %get-tuple-element.75) | copy-start | bytes 9220
  43.5 40.7 %copy-start.38 = (f32[256]{0:T(256)S(1)}, f32[256]{0:T(256)}, u32[]{:S(2)}) copy-start(f32[256]{0:T(256)} %param.17) | copy-start | bytes 3076
  74.1 11.6 %copy-start.15 = (f32[3,256]{1,0:T(4,128)S(1)}, f32[3,256]{1,0:T(4,128)}, u32[]{:S(2)}) copy-start(f32[3,256]{1,0:T(4,128)} %get-tuple-element.76) | copy-start | bytes 9220
  74.1 11.6 %copy-start.17 = (f32[3,256]{1,0:T(4,128)S(1)}, f32[3,256]{1,0:T(4,128)}, u32[]{:S(2)}) copy-start(f32[3,256]{1,0:T(4,128)} %get-tuple-element.77) | copy-start | bytes 9220
  74.1 11.6 %copy-start.19 = (f32[3,256]{1,0:T(4,128)S(1)}, f32[3,256]{1,0:T(4,128)}, u32[]{:S(2)}) copy-start(f32[3,256]{1,0:T(4,128)} %get-tuple-element.78) | copy-start | bytes 9220
  74.1 11.6 %copy-start.21 = (f32[3,256]{1,0:T(4,128)S(1)}, f32[3,256]{1,0:T(4,128)}, u32[]{:S(2)}) copy-start(f32[3,256]{1,0:T(4,128)} %get-tuple-element.73) | copy-start | bytes 9220
  74.1 11.6 %copy-start.23 = (f32[3,256]{1,0:T(4,128)S(1)}, f32[3,256]{1,0:T(4,128)}, u32[]{:S(2)}) copy-start(f32[3,256]{1,0:T(4,128)} %get-tuple-element.74) | copy-start | bytes 9220
  79.4 12.8 %copy-start.10 = (f32[128,256]{1,0:T(8,128)S(1)}, f32[128,256]{1,0:T(8,128)}, u32[]{:S(2)}) copy-start(f32[128,256]{1,0:T(8,128)} %param.16) | copy-start | bytes 393220
  79.4 6.3 collective-permute-start
  84.3 9.8 %copy-start.36 = (f32[128]{0:T(128)}, f32[128]{0:T(128)S(1)}, u32[]{:S(2)}) copy-start(f32[128]{0:T(128)S(1)} %iota_convert_fusion) | copy-start | bytes 1540
  84.3 9.7 %copy-start.28 = (f32[256]{0:T(256)}, f32[256]{0:T(256)S(1)}, u32[]{:S(2)}) copy-start(f32[256]{0:T(256)S(1)} %neg.7) | copy-start | bytes 3076
  84.3 9.7 %copy-start.25 = (f32[3,1,256]{2,0,1:T(4,128)}, f32[3,1,256]{2,0,1:T(4,128)S(1)}, u32[]{:S(2)}) copy-start(f32[3,1,256]{2,0,1:T(4,128)S(1)} %copy.59) | copy-start | bytes 9220
  86.4 7.6 %collective-permute-start.1 = (bf16[127,256]{1,0:T(8,128)(2,1)S(1)}, bf16[127,256]{1,0:T(8,128)(2,1)S(1)}, u32[]{:S(2)}, u32[]{:S(2)}) collective-permute-start(bf16[127,256]{1,0:T(8,128)(2,1)S(1)} %slice.134), channel_id=1, source_target_pairs={{0,1},{1,2},{2,3},{3,4},{4,5},{5,6},{6,7},{8,9},{9,10},{10,11},{11... | collective-permute-start | bytes 195080 | tf_op jit(solution)/shard_map/ppermute | solution.py:78
  100.6 0.7 copy-start.8
  104.2 71.4 %copy-start.30 = (bf16[256,4]{0,1:T(4,128)(2,1)S(1)}, bf16[256,4]{0,1:T(4,128)(2,1)}, u32[]{:S(2)}) copy-start(bf16[256,4]{0,1:T(4,128)(2,1)} %param.19) | copy-start | bytes 6148
  104.2 138.5 %all-gather.5.cloned.1.call-start = ((), (), s32[]{:S(2)}) async-start(), calls=%async_computation.7 | async-start | bytes 2228224 | tf_op jit(solution)/shard_map/all_gather | solution.py:134
  174.9 0.7 copy-start.7
  204.9 1.9 copy-start.29
  206.8 134.9 %reduce-scatter.8.cloned.1.call-start = ((), (), s32[]{:S(2)}) async-start(), calls=%async_computation.8 | async-start | bytes 2228224 | tf_op jit(solution)/shard_map/reduce_scatter | solution.py:162
  245.0 7.7 %collective-permute-start.2 = (bf16[127,256]{1,0:T(8,128)(2,1)S(1)}, bf16[127,256]{1,0:T(8,128)(2,1)S(1)}, u32[]{:S(2)}, u32[]{:S(2)}) collective-permute-start(bf16[127,256]{1,0:T(8,128)(2,1)S(1)} %slice.249), channel_id=1, source_target_pairs={{1,0},{2,1},{3,2},{4,3},{5,4},{6,5},{7,6},{9,8},{10,9},{11,10},{12... | collective-permute-start | bytes 195080 | tf_op jit(solution)/shard_map/ppermute | solution.py:78
  260.1 8.6 %copy-start.14 = (f32[3,256]{1,0:T(4,128)S(1)}, f32[3,256]{1,0:T(4,128)}, u32[]{:S(2)}) copy-start(f32[3,256]{1,0:T(4,128)} %copy-done.13) | copy-start | bytes 9220
  260.1 8.6 %copy-start.16 = (f32[3,256]{1,0:T(4,128)S(1)}, f32[3,256]{1,0:T(4,128)}, u32[]{:S(2)}) copy-start(f32[3,256]{1,0:T(4,128)} %get-tuple-element.76) | copy-start | bytes 9220
  260.1 8.6 %copy-start.18 = (f32[3,256]{1,0:T(4,128)S(1)}, f32[3,256]{1,0:T(4,128)}, u32[]{:S(2)}) copy-start(f32[3,256]{1,0:T(4,128)} %get-tuple-element.77) | copy-start | bytes 9220
  260.2 8.6 %copy-start.20 = (f32[3,256]{1,0:T(4,128)S(1)}, f32[3,256]{1,0:T(4,128)}, u32[]{:S(2)}) copy-start(f32[3,256]{1,0:T(4,128)} %get-tuple-element.78) | copy-start | bytes 9220
  260.2 8.6 %copy-start.22 = (f32[3,256]{1,0:T(4,128)S(1)}, f32[3,256]{1,0:T(4,128)}, u32[]{:S(2)}) copy-start(f32[3,256]{1,0:T(4,128)} %get-tuple-element.73) | copy-start | bytes 9220
  260.2 8.6 %copy-start.24 = (f32[3,256]{1,0:T(4,128)S(1)}, f32[3,256]{1,0:T(4,128)}, u32[]{:S(2)}) copy-start(f32[3,256]{1,0:T(4,128)} %get-tuple-element.74) | copy-start | bytes 9220
  260.2 8.6 %copy-start.26 = (f32[3,1,256]{2,0,1:T(4,128)S(1)}, f32[3,1,256]{2,0,1:T(4,128)}, u32[]{:S(2)}) copy-start(f32[3,1,256]{2,0,1:T(4,128)} %copy-done.25) | copy-start | bytes 9220
  261.2 7.5 %copy-start.1 = (f32[256,1,256]{2,0,1:T(8,128)}, f32[256,1,256]{2,0,1:T(8,128)S(1)}, u32[]{:S(2)}) copy-start(f32[256,1,256]{2,0,1:T(8,128)S(1)} %get-tuple-element.56) | copy-start | bytes 786436
  261.2 7.5 %copy-start.3 = (f32[256,1,256]{2,0,1:T(8,128)}, f32[256,1,256]{2,0,1:T(8,128)S(1)}, u32[]{:S(2)}) copy-start(f32[256,1,256]{2,0,1:T(8,128)S(1)} %get-tuple-element.57) | copy-start | bytes 786436
  261.3 7.3 %collective-permute-start.3 = (f32[6,3,256]{2,0,1:T(8,128)S(1)}, f32[6,3,256]{2,0,1:T(8,128)S(1)}, u32[]{:S(2)}, u32[]{:S(2)}) collective-permute-start(f32[6,3,256]{2,0,1:T(8,128)S(1)} %slice.136), channel_id=1, source_target_pairs={{1,0},{2,1},{3,2},{4,3},{5,4},{6,5},{7,6},{9,8},{10,9},{11,10},{12... | collective-permute-start | bytes 55304 | tf_op jit(solution)/shard_map/ppermute | solution.py:78
  275.4 0.9 copy-start.11
  275.4 1.0 copy-start.12
  275.4 3.0 copy-start.9
  275.4 152.3 %all-reduce.3.cloned.1.call-start = ((), (), s32[]{:S(2)}) async-start(), calls=%async_computation.11 | async-start | bytes 131072 | tf_op jit(solution)/shard_map/psum | solution.py:175
  278.4 226.8 %reduce-scatter.14.cloned.1.call-start = ((), (), s32[]{:S(2)}) async-start(), calls=%async_computation.12 | async-start | bytes 2359296 | tf_op jit(solution)/shard_map/reduce_scatter | solution.py:137
  282.2 324.7 %reduce-scatter.12.cloned.1.call-start = ((), (), s32[]{:S(2)}) async-start(), calls=%async_computation.10 | async-start | bytes 7077888 | tf_op jit(solution)/shard_map/reduce_scatter | solution.py:158
  288.3 5.3 copy-start.2
  288.3 5.3 copy-start.4
  288.4 53.3 %copy-start.6 = (f32[256,256]{0,1:T(8,128)S(1)}, f32[256,256]{0,1:T(8,128)}, u32[]{:S(2)}) copy-start(f32[256,256]{0,1:T(8,128)} %copy-done.5) | copy-start | bytes 786436
  288.4 392.3 %reduce-scatter.10.cloned.1.call-start = ((), (), s32[]{:S(2)}) async-start(), calls=%async_computation.9 | async-start | bytes 589824 | tf_op jit(solution)/shard_map/reduce_scatter | solution.py:170
  293.6 213.3 %copy-start.31 = (bf16[256,4]{0,1:T(4,128)(2,1)S(1)}, bf16[256,4]{0,1:T(4,128)(2,1)}, u32[]{:S(2)}) copy-start(bf16[256,4]{0,1:T(4,128)(2,1)} %convolution_convert_fusion.2) | copy-start | bytes 6148
  295.0 78.4 %copy-start.37 = (f32[256]{0:T(256)S(1)}, f32[256]{0:T(256)}, u32[]{:S(2)}) copy-start(f32[256]{0:T(256)} %get-tuple-element.61) | copy-start | bytes 3076
  295.0 78.4 %copy-start.35 = (bf16[3,256]{1,0:T(4,128)(2,1)S(1)}, bf16[3,256]{1,0:T(4,128)(2,1)}, u32[]{:S(2)}) copy-start(bf16[3,256]{1,0:T(4,128)(2,1)} %get-tuple-element.38) | copy-start | bytes 4612
  295.0 78.5 %copy-start.34 = (bf16[3,256]{1,0:T(4,128)(2,1)S(1)}, bf16[3,256]{1,0:T(4,128)(2,1)}, u32[]{:S(2)}) copy-start(bf16[3,256]{1,0:T(4,128)(2,1)} %get-tuple-element.39) | copy-start | bytes 4612
  295.0 78.5 %copy-start.33 = (bf16[3,256]{1,0:T(4,128)(2,1)S(1)}, bf16[3,256]{1,0:T(4,128)(2,1)}, u32[]{:S(2)}) copy-start(bf16[3,256]{1,0:T(4,128)(2,1)} %get-tuple-element.37) | copy-start | bytes 4612
  295.0 78.5 %copy-start.32 = (bf16[3,256]{1,0:T(4,128)(2,1)S(1)}, bf16[3,256]{1,0:T(4,128)(2,1)}, u32[]{:S(2)}) copy-start(bf16[3,256]{1,0:T(4,128)(2,1)} %get-tuple-element.55) | copy-start | bytes 4612
Sparse Core Ops, SparseCore 0:
  40.8 33.2 all-gather.2
  104.3 69.5 reduce-scatter.5
  206.9 35.7 all-gather.4
  275.6 66.0 reduce-scatter.7
  344.5 83.2 all-reduce.2
  431.3 73.7 reduce-scatter.13
  509.0 97.7 reduce-scatter.11
  610.9 69.6 reduce-scatter.9

commit v2 on v1

--- a/solution.py
+++ b/solution.py
@@ -88,25 +88,65 @@
     return total
 
 
+def split3(x):
+    parts = []
+    rest = x
+    for _ in range(3):
+        part = lax.reduce_precision(rest, exponent_bits=8, mantissa_bits=7)
+        parts.append(part)
+        rest = rest - part
+    return [p.astype(jnp.bfloat16) for p in parts]
+
+
+def split2(x):
+    hi = lax.reduce_precision(x, exponent_bits=8, mantissa_bits=7)
+    return [hi.astype(jnp.bfloat16), (x - hi).astype(jnp.bfloat16)]
+
+
+def as_rows(flat, width):
+    pad = (-flat.shape[0]) % width
+    return jnp.pad(flat, (0, pad)).reshape(-1, width)
+
+
 def body(ids, tags, embed, gain, w_in, short_filt, mr_filt, rates, w_out, w_tag):
     f32 = jnp.float32
+    bf16 = jnp.bfloat16
     high = lax.Precision.HIGHEST
     rows = ids.shape[0]
+    vocab = embed.shape[0]
+    cw = embed.shape[1]
     width = w_in.shape[1]
     taps = short_filt.shape[1]
     span = mr_filt.shape[0]
+    n_tags = w_tag.shape[1]
     n_ctx = lax.axis_size("ctx")
-    id_hot = (ids[:, None] == jnp.arange(embed.shape[0])[None, :]).astype(jnp.bfloat16)
+    k_ctx = lax.axis_index("ctx")
+    seq = rows * n_ctx
+
+    packed = jnp.concatenate([embed, jnp.stack(split3(gain), axis=0), w_tag.T], axis=0)
+    packed_full = lax.all_gather(packed, "dp", axis=1, tiled=True)
+    w_out_cols = lax.all_to_all(w_out, "dp", 1, 0, tiled=True)
+    packed_full, w_out_cols = lax.optimization_barrier((packed_full, w_out_cols))
+    embed_full = packed_full[:vocab]
+    gain_full = (
+        packed_full[vocab].astype(f32) + packed_full[vocab + 1].astype(f32)
+    ) + packed_full[vocab + 2].astype(f32)
+    w_tag_full_t = packed_full[vocab + 3 : vocab + 3 + n_tags].astype(f32)
+
+    emb32 = embed_full.astype(f32)
+    r_vocab = lax.rsqrt(jnp.sum(emb32 * emb32, axis=1) / width + 1e-06)
+    vocab_ids = jnp.arange(vocab)
+    id_mask = ids[:, None] == vocab_ids[None, :]
+    id_hot = id_mask.astype(bf16)
+    r = jnp.sum(jnp.where(id_mask, r_vocab[None, :], 0.0), axis=1)[:, None]
+    x0_full = jnp.dot(id_hot, embed_full, preferred_element_type=f32)
     x0 = jnp.dot(id_hot, embed, preferred_element_type=f32)
-    row_sq = lax.psum(jnp.sum(x0 * x0, axis=1), "dp")
-    r = lax.rsqrt(row_sq / width + 1e-06)[:, None]
-    u_slab = (x0 * r * gain[None, :]).astype(jnp.bfloat16)
-    u = lax.all_gather(u_slab, "dp", axis=1, tiled=True)
-    proj = jnp.einsum("td,jdc->tjc", u, w_in, preferred_element_type=f32).astype(jnp.bfloat16)
+    u = (x0_full * r * gain_full[None, :]).astype(bf16)
+    proj = jnp.einsum("td,jdc->tjc", u, w_in, preferred_element_type=f32).astype(bf16)
     head = shifted(proj[rows - (taps - 1) :], "ctx", 1)
     p_ext = jnp.concatenate([head, proj], axis=0)
     z = short_filter(p_ext, short_filt, rows)
-    kv = (z[:, 1] * z[:, 2]).astype(jnp.bfloat16)
+    kv = (z[:, 1] * z[:, 2]).astype(bf16)
     kv_head = shifted(kv[rows - (span - 1) :], "ctx", 1)
     kv_ext = jnp.concatenate([kv_head, kv, jnp.zeros((1,) + kv.shape[1:], kv.dtype)], axis=0)
     q = z[:, 0]
@@ -116,30 +156,28 @@
     decay = jnp.exp(-rates[None, :] * lags)
     taps_eff = mr_filt * decay
     kv_wide = kv_ext.astype(f32)
-
     m = medium_forward(kv_wide, taps_eff, rows)
-    h = (q * m).astype(jnp.bfloat16)
-    y_part = jnp.dot(h, w_out, preferred_element_type=f32)
-    y = lax.psum_scatter(y_part, "dp", scatter_dimension=1, tiled=True)
-    block_out = (x0 + y).astype(jnp.bfloat16)
+    h = (q * m).astype(bf16)
+    h_full = lax.all_gather(h, "dp", axis=1, tiled=True)
+    y = jnp.dot(h_full, w_out_cols, preferred_element_type=f32)
+    block_out = (x0 + y).astype(bf16)
+    id_hi = (ids // 32).astype(bf16)
+    id_lo = (ids % 32).astype(bf16)
+    h_ids = jnp.concatenate([h, as_rows(jnp.concatenate([id_hi, id_lo]), cw)], axis=0)
+    h_ids_all = lax.all_gather(h_ids, "ctx", axis=0, tiled=True).reshape(n_ctx, -1, cw)
     logits = lax.psum(jnp.dot(block_out, w_tag, preferred_element_type=f32), "dp")
     top = jnp.max(logits, axis=1)
     lse = top + jnp.log(jnp.sum(jnp.exp(logits - top[:, None]), axis=1))
-    tag_hot = (tags[:, None] == jnp.arange(w_tag.shape[1])[None, :]).astype(f32)
+    tag_hot = (tags[:, None] == jnp.arange(n_tags)[None, :]).astype(f32)
     loss_part = jnp.sum(lse - jnp.sum(logits * tag_hot, axis=1))
     dlog = jnp.exp(logits - lse[:, None]) - tag_hot
     dout = jnp.dot(dlog, w_tag.astype(f32).T, precision=high)
     tag_part = jnp.dot(block_out.astype(f32).T, dlog, precision=high)
-    dy = dout.astype(jnp.bfloat16)
-    dy_full = lax.all_gather(dy, "dp", axis=1, tiled=True)
+    dy_full = jnp.dot(dlog, w_tag_full_t, precision=high).astype(bf16)
     dh = lax.dot_general(dy_full, w_out, (((1,), (1,)), ((), ())), preferred_element_type=f32)
-    out_part = lax.dot_general(h, dy_full, (((0,), (0,)), ((), ())), preferred_element_type=f32)
-    d_w_out = lax.psum_scatter(
-        out_part.astype(jnp.bfloat16), "ctx", scatter_dimension=1, tiled=True
-    ).astype(jnp.float32)
     dq = dh * m
     dm = dh * q
-    dm_tail = shifted(dm[: span - 1].astype(jnp.bfloat16), "ctx", -1).astype(jnp.float32)
+    dm_tail = shifted(dm[: span - 1].astype(bf16), "ctx", -1).astype(f32)
     dm_ext = jnp.concatenate([dm, dm_tail, jnp.zeros((1,) + dm.shape[1:], f32)], axis=0)
     dkv, corr = medium_backward(dm_ext, kv_wide, taps_eff, rows)
     mr_part = corr * decay
@@ -153,41 +191,92 @@
         dp = dp + short_filt[None, :, s, :] * dz_ext[s : s + rows]
         shorts.append(jnp.sum(dz * p_ext[taps - 1 - s : taps - 1 - s + rows].astype(f32), axis=0))
     short_part = jnp.stack(shorts, axis=1)
-    dpb = dp.astype(jnp.bfloat16)
-    in_part = jnp.einsum("td,tjc->jdc", u, dpb, preferred_element_type=f32)
-    d_w_in = lax.psum_scatter(
-        in_part.astype(jnp.bfloat16), "ctx", scatter_dimension=1, tiled=True
-    ).astype(jnp.float32)
+    dpb = dp.astype(bf16)
     du_part = jnp.einsum("tjc,jdc->td", dpb, w_in, preferred_element_type=f32)
-    du = lax.psum_scatter(
-        du_part.astype(jnp.bfloat16), "dp", scatter_dimension=1, tiled=True
-    ).astype(jnp.float32)
+    du_part, h_ids_all = lax.optimization_barrier((du_part, h_ids_all))
+    dot_part = jnp.sum(du_part * gain_full[None, :] * x0_full, axis=1)
+    row_dot = lax.psum(dot_part, "dp")[:, None] / width
+    du = lax.psum_scatter(du_part.astype(bf16), "dp", scatter_dimension=1, tiled=True).astype(f32)
     gain_part = jnp.sum(du * x0 * r, axis=0)
     dn = du * gain[None, :]
-    row_dot = lax.psum(jnp.sum(dn * x0, axis=1), "dp")[:, None] / width
     dx0 = dout + r * (dn - x0 * r * r * row_dot)
-    embed_part = jnp.dot(id_hot.astype(f32).T, dx0, precision=high)
-    d_embed = lax.psum_scatter(embed_part, "ctx", scatter_dimension=0, tiled=True)
-    totals = (
-        lax.psum(loss_part.astype(jnp.bfloat16), "ctx").astype(jnp.float32),
-        lax.psum(gain_part.astype(jnp.bfloat16), "ctx").astype(jnp.float32),
-        lax.psum(short_part.astype(jnp.bfloat16), "ctx").astype(jnp.float32),
-        lax.psum(mr_part.astype(jnp.bfloat16), "ctx").astype(jnp.float32),
-        lax.psum(rate_part.astype(jnp.bfloat16), "ctx").astype(jnp.float32),
-        lax.psum(tag_part.astype(jnp.bfloat16), "ctx").astype(jnp.float32),
-    )
-    loss = totals[0] / (rows * n_ctx)
+
+    small = jnp.concatenate(
+        [
+            gain_part,
+            short_part.reshape(-1),
+            mr_part.reshape(-1),
+            rate_part,
+            tag_part.reshape(-1),
+            loss_part[None],
+        ]
+    )
+    n_small = small.shape[0]
+    dlog_parts = split2(dlog.reshape(-1))
+    tail = jnp.concatenate([small.astype(bf16)] + dlog_parts)
+    final = jnp.concatenate(
+        [jnp.transpose(dpb, (1, 0, 2)).reshape(-1, cw), dx0.astype(bf16), as_rows(tail, cw)],
+        axis=0,
+    )
+    final_all = lax.all_gather(final, "ctx", axis=0, tiled=True).reshape(n_ctx, -1, cw)
+    n_proj = 3 * rows
+    dp_all = final_all[:, :n_proj].reshape(n_ctx, 3, rows, cw)
+    dp_all = jnp.transpose(dp_all, (0, 2, 1, 3)).reshape(seq, 3, cw)
+    dx0_all = final_all[:, n_proj : n_proj + rows].reshape(seq, cw).astype(f32)
+    tail_all = final_all[:, n_proj + rows :].reshape(n_ctx, -1).astype(f32)
+    small_tot = jnp.sum(tail_all[:, :n_small], axis=0)
+    n_dlog = rows * n_tags
+    dlog_all = (
+        tail_all[:, n_small : n_small + n_dlog] + tail_all[:, n_small + n_dlog : n_small + 2 * n_dlog]
+    ).reshape(seq, n_tags)
+
+    h_all = h_ids_all[:, :rows].reshape(seq, cw)
+    id_rows = h_ids_all[:, rows:].reshape(n_ctx, -1).astype(jnp.int32)
+    ids_all = (id_rows[:, :rows] * 32 + id_rows[:, rows : 2 * rows]).reshape(seq)
+
+    f_cols = width // n_ctx
+    w_tag_cols = lax.dynamic_slice_in_dim(w_tag_full_t, k_ctx * f_cols, f_cols, 1)
+    dy_all = jnp.dot(dlog_all, w_tag_cols, precision=high).astype(bf16)
+    d_w_out = lax.dot_general(h_all, dy_all, (((0,), (0,)), ((), ())), preferred_element_type=f32)
+
+    all_mask = ids_all[:, None] == vocab_ids[None, :]
+    all_hot = all_mask.astype(bf16)
+    r_all = jnp.sum(jnp.where(all_mask, r_vocab[None, :], 0.0), axis=1)[:, None]
+    embed_k = lax.dynamic_slice_in_dim(embed_full, k_ctx * f_cols, f_cols, 1)
+    gain_k = lax.dynamic_slice_in_dim(gain_full, k_ctx * f_cols, f_cols, 0)
+    x0_k = jnp.dot(all_hot, embed_k, preferred_element_type=f32)
+    u_k = (x0_k * r_all * gain_k[None, :]).astype(bf16)
+    d_w_in = jnp.einsum("td,tjc->jdc", u_k, dp_all, preferred_element_type=f32)
+
+    v_rows = vocab // n_ctx
+    own_hot = (ids_all[:, None] == (k_ctx * v_rows + jnp.arange(v_rows))[None, :]).astype(f32)
+    d_embed = jnp.dot(own_hot.T, dx0_all, precision=high)
+
+    pos = 0
+    outs = []
+    for size, shape in (
+        (cw, (cw,)),
+        (3 * taps * cw, (3, taps, cw)),
+        (span * cw, (span, cw)),
+        (cw, (cw,)),
+        (cw * n_tags, (cw, n_tags)),
+        (1, ()),
+    ):
+        outs.append(small_tot[pos : pos + size].reshape(shape))
+        pos += size
+    gain_tot, short_tot, mr_tot, rate_tot, tag_tot, loss_tot = outs
+    loss = loss_tot / seq
     return (
         loss,
         block_out,
         d_embed,
-        totals[1],
+        gain_tot,
         d_w_in,
-        totals[2],
-        totals[3],
-        totals[4],
+        short_tot,
+        mr_tot,
+        rate_tot,
         d_w_out,
-        totals[5],
+        tag_tot,
     )
 
 

time: 690 us -> 412 us (0.60)
  waiting for transfers between devices: 454 us -> 209 us
  blocking collectives: 128 us -> 56.5 us
  local copies, waits for them, and re-layouts: 12.1 us -> 41.8 us
  other arithmetic: 19.2 us -> 27.3 us
    reduce_scatter x5 -> x1, waiting for transfers between devices: 319 us -> 35.3 us  [body(): lax.psum_scatter(du_part.astype(bf16), 'dp', scatter_dimension=1, tiled=T...]
    psum x3 -> x1, blocking collectives: 99.8 us -> 27.4 us  [body(): row_dot = lax.psum(dot_part, 'dp')[:, None] / width]
    all_gather x2 -> x4, waiting for transfers between devices: 66.4 us -> 127 us  [the longest x1 68 us: body(): lax.all_gather(final, 'ctx', axis=0, tiled=True).reshape(n_ctx, -1, cw)]
    psum x1 -> x0, waiting for transfers between devices: 54.3 us -> none  [body(): lax.psum(mr_part.astype(jnp.bfloat16), 'ctx').astype(jnp.float32)]
    all_to_all x0 -> x1, waiting for transfers between devices: none -> 32.6 us  [body(): w_out_cols = lax.all_to_all(w_out, 'dp', 1, 0, tiled=True)]
    slice x2 -> x14, local copies, waits for them, and re-layouts: 1.03 us -> 12.8 us  [the longest x1 4.84 us: body(): embed_full = packed_full[:vocab]]
    reduce_sum x0 -> x6, other arithmetic: none -> 11.5 us  [the longest x1 6.72 us: body(): dot_part = jnp.sum(du_part * gain_full[None, :] * x0_full, axis=1)]
    reshape x0 -> x11, local copies, waits for them, and re-layouts: none -> 11.1 us  [the longest x1 3.84 us: body(): dp_all = final_all[:, :n_proj].reshape(n_ctx, 3, rows, cw)]
  transfers between devices with their start and end apart: 12 -> 10, of which waited for: 12 -> 9; matrix products, arithmetic and copies ran while one was open for 5% -> 10% of each run, Pallas kernels for 0% -> 2%
where the time goes in v2:
time: 412 us; the launch traced here: 411 us
  waiting for transfers between devices  209 us (51%)
  blocking collectives  56.5 us (14%)
  local copies, waits for them, and re-layouts  41.8 us (10%)
  matrix products  29 us (7%)
  other arithmetic  27.3 us (7%)
  starting transfers between devices  19.3 us (5%)
  between operations  16.6 us (4%)
  Pallas kernels  11.3 us (3%)
    all_gather x1, waiting for transfers between devices, body(): lax.all_gather(final, 'ctx', axis=0, tiled=True).reshape(n_ctx, -1, cw)  68 us
    all_gather x1, waiting for transfers between devices, body(): h_full = lax.all_gather(h, 'dp', axis=1, tiled=True)  40.7 us
    reduce_scatter x1, waiting for transfers between devices, body(): lax.psum_scatter(du_part.astype(bf16), 'dp', scatter_dimension=1, tiled=T...  35.3 us
    all_to_all x1, waiting for transfers between devices, body(): w_out_cols = lax.all_to_all(w_out, 'dp', 1, 0, tiled=True)  32.6 us
    psum x1, blocking collectives, body(): lax.psum(jnp.dot(block_out, w_tag, preferred_element_type=f32), 'dp')  29.1 us
    psum x1, blocking collectives, body(): row_dot = lax.psum(dot_part, 'dp')[:, None] / width  27.4 us
    all_gather x1, waiting for transfers between devices, body(): packed_full = lax.all_gather(packed, 'dp', axis=1, tiled=True)  17.9 us
    ppermute x4, waiting for transfers between devices, shifted(): return lax.ppermute(block, axis, route)  14.6 us
  transfers between devices with their start and end apart: 10, of which 9 were waited for; matrix products, arithmetic and copies ran while one was open for 10% of the time, Pallas kernels for 2%

profile of v2, /device:TPU:0, one launch (start us, length us, event | category | flops | bytes accessed | tf_op | source)
XLA Modules:
  0.0 411.0 jit_solution(4854805812206038495)
XLA Ops:
  7.2 0.7 fusion.61
  7.9 2.9 concatenate.30
  10.9 4.1 copy.44
  15.0 5.5 %all-to-all-start = ((bf16[256,16,256]{0,2,1:T(8,128)(2,1)}), bf16[256,16,256]{0,2,1:T(8,128)(2,1)S(1)}, u32[]{:S(2)}, u32[]{:S(2)}) async-start(bf16[256,16,256]{0,2,1:T(8,128)(2,1)} %bitcast.130), calls=%async_computation | async-start | bytes 4194304 | tf_op jit(solution)/shard_map/all_to_all | solution.py:128
  20.7 32.6 %all-to-all-done = bf16[256,16,256]{0,2,1:T(8,128)(2,1)S(1)} async-done(((bf16[256,16,256]{0,2,1:T(8,128)(2,1)}), bf16[256,16,256]{0,2,1:T(8,128)(2,1)S(1)}, u32[]{:S(2)}, u32[]{:S(2)}) %all-to-all-start) | async-done | bytes 2097184 | tf_op jit(solution)/shard_map/all_to_all | solution.py:128
  53.3 1.3 copy-done.3
  54.6 4.1 copy.45
  58.7 17.9 %all-gather.7.cloned.1.call-done = bf16[519,4096]{1,0:T(8,128)(2,1)} async-done(((bf16[519,256]{1,0:T(8,128)(2,1)}), bf16[519,4096]{1,0:T(8,128)(2,1)}) %all-gather.7.cloned.1.call-update) | async-done | bytes 4251664 | tf_op jit(solution)/shard_map/all_gather | solution.py:127
  76.6 3.2 multiply_reduce_fusion
  79.8 1.1 convert_add_fusion
  81.0 1.3 fusion.38
  82.5 0.7 copy-done.35
  83.3 1.8 fusion.8
  85.2 4.9 %collective-permute-start = (bf16[6,3,256]{2,0,1:T(8,128)(2,1)S(1)}, bf16[6,3,256]{2,0,1:T(8,128)(2,1)S(1)}, u32[]{:S(2)}, u32[]{:S(2)}) collective-permute-start(bf16[6,3,256]{2,0,1:T(8,128)(2,1)S(1)} %slice.204), channel_id=1, source_target_pairs={{0,1},{1,2},{2,3},{3,4},{4,5},{5,6},{6,7},{8,9},{9,10},{10,11},{11... | collective-permute-start | bytes 27656 | tf_op jit(solution)/shard_map/ppermute | solution.py:78
  90.1 1.3 collective-permute-done
  92.2 5.7 %collective-permute-start.1 = (bf16[127,256]{1,0:T(8,128)(2,1)S(1)}, bf16[127,256]{1,0:T(8,128)(2,1)S(1)}, u32[]{:S(2)}, u32[]{:S(2)}) collective-permute-start(bf16[127,256]{1,0:T(8,128)(2,1)S(1)} %slice.218), channel_id=1, source_target_pairs={{0,1},{1,2},{2,3},{3,4},{4,5},{5,6},{6,7},{8,9},{9,10},{10,11},{11... | collective-permute-start | bytes 195080 | tf_op jit(solution)/shard_map/ppermute | solution.py:78
  98.0 0.8 fusion.54.g_ref
  98.8 1.0 collective-permute-done.1
  99.8 0.9 maximum_convert_fusion.kv_ref
  100.7 4.7 %shard_map.177 = f32[256,256]{1,0:T(8,128)} custom-call(f32[384,256]{1,0:T(8,128)} %maximum_convert_fusion.kv_ref, f32[128,256]{1,0:T(8,128)} %fusion.54.g_ref), custom_call_target="tpu_custom_call" | custom-call | tf_op jit(solution)/shard_map/pallas_call | solution.py:24
  105.4 1.7 multiply_convert_fusion.2
  107.2 1.2 fusion.39
  108.5 1.7 maximum_bitcast_fusion.1
  110.2 40.7 %all-gather.9.cloned.1.call-done = bf16[256,4096]{1,0:T(8,128)(2,1)} async-done(((bf16[256,256]{1,0:T(8,128)(2,1)}), bf16[256,4096]{1,0:T(8,128)(2,1)}) %all-gather.9.cloned.1.call-update) | async-done | bytes 2097168 | tf_op jit(solution)/shard_map/all_gather | solution.py:161
  150.9 2.3 fusion.11
  153.2 0.9 fusion.71
  154.1 29.1 %psum.14 = f32[256,4]{0,1:T(4,128)S(1)} all-reduce(f32[256,4]{0,1:T(4,128)S(1)} %fusion.71), channel_id=1, replica_groups=mesh['dp'=16,'ctx'=8] {'dp'}, use_global_device_ids=true, to_apply=%region_2.3 | all-reduce | flops 1024 | bytes 8192 | tf_op jit(solution)/shard_map/psum | solution.py:168
  183.2 0.7 select_reduce_fusion.2
  184.5 0.7 convert_subtract_fusion
  185.8 2.7 convolution_convert_fusion
  188.5 2.5 multiply_bitcast_fusion.2
  191.0 1.5 collective-permute-start.2
  192.6 6.1 %collective-permute-done.2 = bf16[127,256]{1,0:T(8,128)(2,1)S(1)} collective-permute-done((bf16[127,256]{1,0:T(8,128)(2,1)S(1)}, bf16[127,256]{1,0:T(8,128)(2,1)S(1)}, u32[]{:S(2)}, u32[]{:S(2)}) %collective-permute-start.2) | collective-permute-done | bytes 65056 | tf_op jit(solution)/shard_map/ppermute | solution.py:78
  198.7 0.9 maximum_maximum_fusion.dm_ref
  199.5 6.6 %shard_map.178 = (f32[256,256]{1,0:T(8,128)}, f32[128,256]{1,0:T(8,128)}) custom-call(f32[384,256]{1,0:T(8,128)} %maximum_maximum_fusion.dm_ref, f32[384,256]{1,0:T(8,128)} %maximum_convert_fusion.kv_ref, f32[128,256]{1,0:T(8,128)} %fusion.54.g_ref), custom_call_target="tpu_custom_call" | custom-call | tf_op jit(solution)/shard_map/pallas_call | solution.py:56
  206.1 1.0 multiply_bitcast_fusion.1
  207.2 1.6 collective-permute-start.3
  208.8 6.2 %collective-permute-done.3 = f32[6,3,256]{2,0,1:T(8,128)S(1)} collective-permute-done((f32[6,3,256]{2,0,1:T(8,128)S(1)}, f32[6,3,256]{2,0,1:T(8,128)S(1)}, u32[]{:S(2)}, u32[]{:S(2)}) %collective-permute-start.3) | collective-permute-done | bytes 18464 | tf_op jit(solution)/shard_map/ppermute | solution.py:78
  215.0 1.4 fusion.29
  216.4 3.9 convolution_bitcast_fusion
  220.4 6.7 %multiply_reduce_fusion.1 = (f32[256]{0:T(256)S(1)}, bf16[256,4096]{1,0:T(8,128)(2,1)}) fusion(f32[256,4096]{1,0:T(8,128)} %copy-done.1, f32[256,4096]{1,0:T(8,128)} %convolution_bitcast_fusion, f32[4096]{0:T(1024)S(1)} %bitcast.137), kind=kLoop, calls=%fused_computation.7 | loop fusion | flops 4194048 | bytes 10503168 | tf_op jit(solution)/shard_map/reduce_sum | solution.py:197
  228.0 0.8 fusion.26
  229.1 27.4 %psum.15 = f32[256]{0:T(256)S(1)} all-reduce(f32[256]{0:T(256)S(1)} %get-tuple-element.83), channel_id=1, replica_groups=mesh['dp'=16,'ctx'=8] {'dp'}, use_global_device_ids=true, to_apply=%region_7.8 | all-reduce | flops 256 | bytes 2048 | tf_op jit(solution)/shard_map/psum | solution.py:198
  256.6 35.3 %reduce-scatter.2.cloned.1.call-done = bf16[256,256]{1,0:T(8,128)(2,1)} async-done(((bf16[256,4096]{1,0:T(8,128)(2,1)}), bf16[256,256]{1,0:T(8,128)(2,1)}) %reduce-scatter.2.cloned.1.call-update) | async-done | bytes 131088 | tf_op jit(solution)/shard_map/reduce_scatter | solution.py:199
  291.9 1.0 fusion.49
  292.9 0.8 concatenate.37
  293.7 1.2 fusion.12
  295.0 0.9 maximum_bitcast_fusion
  295.9 0.9 slice.179
  296.8 4.8 %slice.158 = bf16[512,4096]{1,0:T(8,128)(2,1)} slice(bf16[519,4096]{1,0:T(8,128)(2,1)} %all-gather.7.cloned.1.call-done), slice={[0:512], [0:4096]} | slice | bytes 8388608 | tf_op jit(solution)/shard_map/slice | solution.py:130
  301.6 1.1 slice.200
  302.8 0.9 select_reduce_fusion
  303.8 68.0 %all-gather.13.cloned.1.call-done = bf16[8,1188,256]{2,1,0:T(8,128)(2,1)} async-done(((bf16[1,1188,256]{2,1,0:T(8,128)(2,1)}), bf16[8,1188,256]{2,1,0:T(8,128)(2,1)}) %all-gather.13.cloned.1.call-update) | async-done | bytes 4866064 | tf_op jit(solution)/shard_map/all_gather | solution.py:221
  371.8 1.1 slice.227
  374.7 0.7 reshape.143
  376.8 2.1 reshape.145
  378.9 3.7 slice.234
  382.6 3.8 copy.50
  386.5 3.5 reshape.141
  389.9 5.2 %convolution_bitcast_fusion.1 = f32[3,512,256]{1,2,0:T(8,128)S(1)} fusion(bf16[2048,3,256]{0,2,1:T(8,128)(2,1)} %reshape.141, f32[512]{0:T(512)S(1)} %bitcast.145, f32[2048]{0:T(1024)S(1)} %select_reduce_fusion, s32[2048]{0:T(1024)S(1)} %bitcast.139, bf16[512,4096]{1,0:T(8,128)(2,1)} %slice.158, s32[]{:T(128)S(6)} %select_n.28), kind=kOutput, calls=%fused_computation.16 | convolution fusion | flops 2688548864 | bytes 5261316 | tf_op jit(solution)/shard_map/td,tjc->jdc/dot_general | solution.py:249
  395.1 1.6 copy.51
  397.4 1.8 convolution_convert_fusion.1
  399.2 2.7 fusion.72
  401.9 1.4 fusion.13
  (170 shorter events, 7.2 us)
Async XLA Ops:
  7.2 69.4 %all-gather.7.cloned.1.call-start = ((), (), s32[]{:S(2)}) async-start(), calls=%async_computation.2 | async-start | bytes 4526080 | tf_op jit(solution)/shard_map/all_gather | solution.py:127
  10.9 9.7 %copy-start.28 = (f32[3,7,256]{2,1,0:T(8,128)S(1)}, f32[3,7,256]{2,1,0:T(8,128)}, u32[]{:S(2)}) copy-start(f32[3,7,256]{2,1,0:T(8,128)} %param.15) | copy-start | bytes 64516
  15.0 38.3 %all-to-all-start = ((bf16[256,16,256]{0,2,1:T(8,128)(2,1)}), bf16[256,16,256]{0,2,1:T(8,128)(2,1)S(1)}, u32[]{:S(2)}, u32[]{:S(2)}) async-start(bf16[256,16,256]{0,2,1:T(8,128)(2,1)} %bitcast.130), calls=%async_computation | async-start | bytes 4194304 | tf_op jit(solution)/shard_map/all_to_all | solution.py:128
  20.5 130.4 %all-gather.9.cloned.1.call-start = ((), (), s32[]{:S(2)}) async-start(), calls=%async_computation.3 | async-start | bytes 2228224 | tf_op jit(solution)/shard_map/all_gather | solution.py:161
  20.6 70.8 %copy-start.21 = (f32[3,256]{1,0:T(4,128)}, f32[3,256]{1,0:T(4,128)S(1)}, u32[]{:S(2)}) copy-start(f32[3,256]{1,0:T(4,128)S(1)} %get-tuple-element.113) | copy-start | bytes 9220
  20.6 70.8 %copy-start.22 = (f32[3,256]{1,0:T(4,128)}, f32[3,256]{1,0:T(4,128)S(1)}, u32[]{:S(2)}) copy-start(f32[3,256]{1,0:T(4,128)S(1)} %get-tuple-element.114) | copy-start | bytes 9220
  20.6 70.8 %copy-start.23 = (f32[3,256]{1,0:T(4,128)}, f32[3,256]{1,0:T(4,128)S(1)}, u32[]{:S(2)}) copy-start(f32[3,256]{1,0:T(4,128)S(1)} %get-tuple-element.115) | copy-start | bytes 9220
  20.7 70.8 %copy-start.24 = (f32[3,256]{1,0:T(4,128)}, f32[3,256]{1,0:T(4,128)S(1)}, u32[]{:S(2)}) copy-start(f32[3,256]{1,0:T(4,128)S(1)} %get-tuple-element.116) | copy-start | bytes 9220
  20.7 70.8 %copy-start.25 = (f32[3,256]{1,0:T(4,128)}, f32[3,256]{1,0:T(4,128)S(1)}, u32[]{:S(2)}) copy-start(f32[3,256]{1,0:T(4,128)S(1)} %get-tuple-element.111) | copy-start | bytes 9220
  20.7 70.8 %copy-start.26 = (f32[3,256]{1,0:T(4,128)}, f32[3,256]{1,0:T(4,128)S(1)}, u32[]{:S(2)}) copy-start(f32[3,256]{1,0:T(4,128)S(1)} %get-tuple-element.112) | copy-start | bytes 9220
  53.3 1.3 copy-start.3
  54.6 26.3 %copy-start.31 = (s32[256]{0:T(256)S(1)}, s32[256]{0:T(256)}, u32[]{:S(2)}) copy-start(s32[256]{0:T(256)} %param.10) | copy-start | bytes 3076
  54.6 28.6 %slice-start = ((s8[6291456]{0:T(1024)(128)(4,1)}), s8[2097152]{0:T(1024)(128)(4,1)S(1)}, s32[]{:S(2)}) async-start(s8[6291456]{0:T(1024)(128)(4,1)} %bitcast.124), calls=%async_computation.7 | async-start | bytes 4194304
  76.6 4.4 %copy-start = (bf16[519,4096]{1,0:T(8,128)(2,1)S(1)}, bf16[519,4096]{1,0:T(8,128)(2,1)}, u32[]{:S(2)}) copy-start(bf16[519,4096]{1,0:T(8,128)(2,1)} %all-gather.7.cloned.1.call-done) | copy-start | bytes 12754948
  79.8 3.4 slice-start.1
  81.0 1.3 copy-start.29
  82.3 2.8 copy-start.1
  82.5 0.7 copy-start.35
  83.2 6.8 %copy-start.39 = (f32[256]{0:T(256)S(1)}, f32[256]{0:T(256)}, u32[]{:S(2)}) copy-start(f32[256]{0:T(256)} %param.17) | copy-start | bytes 3076
  83.2 14.7 %copy-start.14 = (f32[128,256]{1,0:T(8,128)S(1)}, f32[128,256]{1,0:T(8,128)}, u32[]{:S(2)}) copy-start(f32[128,256]{1,0:T(8,128)} %param.16) | copy-start | bytes 393220
  85.1 6.3 %copy-start.10 = (bf16[256,3,256]{2,0,1:T(8,128)(2,1)}, bf16[256,3,256]{2,0,1:T(8,128)(2,1)S(1)}, u32[]{:S(2)}) copy-start(bf16[256,3,256]{2,0,1:T(8,128)(2,1)S(1)} %fusion.8) | copy-start | bytes 1179652
  85.1 65.8 %copy-start.2 = (bf16[16,256,256]{2,1,0:T(8,128)(2,1)S(1)}, bf16[16,256,256]{2,1,0:T(8,128)(2,1)}, u32[]{:S(2)}) copy-start(bf16[16,256,256]{2,1,0:T(8,128)(2,1)} %copy.45) | copy-start | bytes 6291460
  85.2 6.3 %collective-permute-start = (bf16[6,3,256]{2,0,1:T(8,128)(2,1)S(1)}, bf16[6,3,256]{2,0,1:T(8,128)(2,1)S(1)}, u32[]{:S(2)}, u32[]{:S(2)}) collective-permute-start(bf16[6,3,256]{2,0,1:T(8,128)(2,1)S(1)} %slice.204), channel_id=1, source_target_pairs={{0,1},{1,2},{2,3},{3,4},{4,5},{5,6},{6,7},{8,9},{9,10},{10,11},{11... | collective-permute-start | bytes 27656 | tf_op jit(solution)/shard_map/ppermute | solution.py:78
  90.0 20.2 %copy-start.37 = (f32[128]{0:T(128)}, f32[128]{0:T(128)S(1)}, u32[]{:S(2)}) copy-start(f32[128]{0:T(128)S(1)} %iota_convert_fusion) | copy-start | bytes 1540
  90.1 20.2 %copy-start.32 = (f32[256]{0:T(256)}, f32[256]{0:T(256)S(1)}, u32[]{:S(2)}) copy-start(f32[256]{0:T(256)S(1)} %neg.7) | copy-start | bytes 3076
  90.1 2.1 copy-start.27
  91.4 0.8 copy-start.19
  92.2 7.6 %collective-permute-start.1 = (bf16[127,256]{1,0:T(8,128)(2,1)S(1)}, bf16[127,256]{1,0:T(8,128)(2,1)S(1)}, u32[]{:S(2)}, u32[]{:S(2)}) collective-permute-start(bf16[127,256]{1,0:T(8,128)(2,1)S(1)} %slice.218), channel_id=1, source_target_pairs={{0,1},{1,2},{2,3},{3,4},{4,5},{5,6},{6,7},{8,9},{9,10},{10,11},{11... | collective-permute-start | bytes 195080 | tf_op jit(solution)/shard_map/ppermute | solution.py:78
  105.4 83.1 %copy-start.7 = (f32[256,256]{1,0:T(8,128)S(1)}, f32[256,256]{1,0:T(8,128)}, u32[]{:S(2)}) copy-start(f32[256,256]{1,0:T(8,128)} %shard_map.177) | copy-start | bytes 786436
  107.1 113.3 %all-gather.11.cloned.1.call-start = ((), (), s32[]{:S(2)}) async-start(), calls=%async_computation.5 | async-start | bytes 1216512 | tf_op jit(solution)/shard_map/all_gather | solution.py:167
  108.5 76.7 %copy-start.8 = (f32[256,256]{1,0:T(8,128)}, f32[256,256]{1,0:T(8,128)S(1)}, u32[]{:S(2)}) copy-start(f32[256,256]{1,0:T(8,128)S(1)} %fusion.39) | copy-start | bytes 786436
  110.2 181.7 %reduce-scatter.2.cloned.1.call-start = ((), (), s32[]{:S(2)}) async-start(), calls=%async_computation.4 | async-start | bytes 2228224 | tf_op jit(solution)/shard_map/reduce_scatter | solution.py:199
  153.2 74.1 %copy-start.12 = (bf16[256,256]{1,0:T(8,128)(2,1)}, bf16[256,256]{1,0:T(8,128)(2,1)S(1)}, u32[]{:S(2)}) copy-start(bf16[256,256]{1,0:T(8,128)(2,1)S(1)} %fusion.11) | copy-start | bytes 393220
  185.2 0.6 copy-start.17
  188.5 27.9 %slice-start.2 = ((s8[6291456]{0:T(1024)(128)(4,1)}), s8[2097152]{0:T(1024)(128)(4,1)S(1)}, s32[]{:S(2)}) async-start(s8[6291456]{0:T(1024)(128)(4,1)} %bitcast.126), calls=%async_computation.9 | async-start | bytes 4194304
  191.0 7.7 %collective-permute-start.2 = (bf16[127,256]{1,0:T(8,128)(2,1)S(1)}, bf16[127,256]{1,0:T(8,128)(2,1)S(1)}, u32[]{:S(2)}, u32[]{:S(2)}) collective-permute-start(bf16[127,256]{1,0:T(8,128)(2,1)S(1)} %slice.365), channel_id=1, source_target_pairs={{1,0},{2,1},{3,2},{4,3},{5,4},{6,5},{7,6},{9,8},{10,9},{11,10},{12... | collective-permute-start | bytes 195080 | tf_op jit(solution)/shard_map/ppermute | solution.py:78
  207.1 7.9 %copy-start.4 = (f32[256,1,256]{2,0,1:T(8,128)}, f32[256,1,256]{2,0,1:T(8,128)S(1)}, u32[]{:S(2)}) copy-start(f32[256,1,256]{2,0,1:T(8,128)S(1)} %get-tuple-element.90) | copy-start | bytes 786436
  207.1 9.3 %slice-start.3 = ((s8[6291456]{0:T(1024)(128)(4,1)}), s8[4194304]{0:T(1024)(128)(4,1)S(1)}, s32[]{:S(2)}) async-start(s8[6291456]{0:T(1024)(128)(4,1)} %bitcast.126), calls=%async_computation.10 | async-start | bytes 8388608
  207.2 7.7 %collective-permute-start.3 = (f32[6,3,256]{2,0,1:T(8,128)S(1)}, f32[6,3,256]{2,0,1:T(8,128)S(1)}, u32[]{:S(2)}, u32[]{:S(2)}) collective-permute-start(f32[6,3,256]{2,0,1:T(8,128)S(1)} %slice.220), channel_id=1, source_target_pairs={{1,0},{2,1},{3,2},{4,3},{5,4},{6,5},{7,6},{9,8},{10,9},{11,10},{12... | collective-permute-start | bytes 55304 | tf_op jit(solution)/shard_map/ppermute | solution.py:78
  220.3 6.9 %copy-start.18 = (f32[256,4]{0,1:T(4,128)S(1)}, f32[256,4]{0,1:T(4,128)}, u32[]{:S(2)}) copy-start(f32[256,4]{0,1:T(4,128)} %copy-done.17) | copy-start | bytes 12292
  220.3 7.7 %copy-start.5 = (f32[256,1,256]{2,0,1:T(8,128)S(1)}, f32[256,1,256]{2,0,1:T(8,128)}, u32[]{:S(2)}) copy-start(f32[256,1,256]{2,0,1:T(8,128)} %copy-done.4) | copy-start | bytes 786436
  220.3 7.7 %copy-start.11 = (bf16[256,3,256]{2,0,1:T(8,128)(2,1)S(1)}, bf16[256,3,256]{2,0,1:T(8,128)(2,1)}, u32[]{:S(2)}) copy-start(bf16[256,3,256]{2,0,1:T(8,128)(2,1)} %copy-done.10) | copy-start | bytes 1179652
  220.3 7.7 %copy-start.20 = (bf16[6,3,256]{2,0,1:T(8,128)(2,1)S(1)}, bf16[6,3,256]{2,0,1:T(8,128)(2,1)}, u32[]{:S(2)}) copy-start(bf16[6,3,256]{2,0,1:T(8,128)(2,1)} %copy-done.19) | copy-start | bytes 27652
  220.3 8.6 %copy-start.15 = (f32[128,256]{1,0:T(8,128)S(1)}, f32[128,256]{1,0:T(8,128)}, u32[]{:S(2)}) copy-start(f32[128,256]{1,0:T(8,128)} %param.16) | copy-start | bytes 393220
  220.3 8.6 %copy-start.16 = (f32[128,256]{1,0:T(8,128)S(1)}, f32[128,256]{1,0:T(8,128)}, u32[]{:S(2)}) copy-start(f32[128,256]{1,0:T(8,128)} %get-tuple-element.20) | copy-start | bytes 393220
  220.4 8.6 %copy-start.33 = (f32[256]{0:T(256)S(1)}, f32[256]{0:T(256)}, u32[]{:S(2)}) copy-start(f32[256]{0:T(256)} %copy-done.32) | copy-start | bytes 3076
  220.4 8.6 %copy-start.38 = (f32[128]{0:T(128)S(1)}, f32[128]{0:T(128)}, u32[]{:S(2)}) copy-start(f32[128]{0:T(128)} %copy-done.37) | copy-start | bytes 1540
  227.1 64.8 %copy-start.9 = (f32[256,256]{1,0:T(8,128)S(1)}, f32[256,256]{1,0:T(8,128)}, u32[]{:S(2)}) copy-start(f32[256,256]{1,0:T(8,128)} %copy-done.8) | copy-start | bytes 786436
  227.1 64.8 %copy-start.36 = (f32[256]{0:T(256)S(1)}, f32[256]{0:T(256)}, u32[]{:S(2)}) copy-start(f32[256]{0:T(256)} %copy-done.35) | copy-start | bytes 3076
  227.1 66.6 %copy-start.34 = (bf16[256,4]{0,1:T(4,128)(2,1)S(1)}, bf16[256,4]{0,1:T(4,128)(2,1)}, u32[]{:S(2)}) copy-start(bf16[256,4]{0,1:T(4,128)(2,1)} %param.19) | copy-start | bytes 6148
  227.1 66.6 %copy-start.40 = (f32[256]{0:T(256)S(1)}, f32[256]{0:T(256)}, u32[]{:S(2)}) copy-start(f32[256]{0:T(256)} %param.13) | copy-start | bytes 3076
  227.2 144.6 %all-gather.13.cloned.1.call-start = ((), (), s32[]{:S(2)}) async-start(), calls=%async_computation.6 | async-start | bytes 5492736 | tf_op jit(solution)/shard_map/all_gather | solution.py:221
  296.8 4.9 %copy-start.13 = (bf16[8,258,256]{2,1,0:T(8,128)(2,1)S(1)}, bf16[8,258,256]{2,1,0:T(8,128)(2,1)}, u32[]{:S(2)}) copy-start(bf16[8,258,256]{2,1,0:T(8,128)(2,1)} %all-gather.11.cloned.1.call-done) | copy-start | bytes 3170308
  296.8 6.0 %copy-start.30 = (f32[512]{0:T(512)S(1)}, f32[512]{0:T(512)}, u32[]{:S(2)}) copy-start(f32[512]{0:T(512)} %copy-done.29) | copy-start | bytes 6148
  389.9 7.4 %copy-start.6 = (f32[2048,4]{1,0:T(8,128)S(1)}, f32[2048,4]{1,0:T(8,128)}, u32[]{:S(2)}) copy-start(f32[2048,4]{1,0:T(8,128)} %reshape.145) | copy-start | bytes 98308
  397.4 4.5 %slice-start.4 = ((bf16[8,1188,256]{2,1,0:T(8,128)(2,1)}), bf16[8,256,256]{2,1,0:T(8,128)(2,1)S(1)}, s32[]{:S(2)}) async-start(bf16[8,1188,256]{2,1,0:T(8,128)(2,1)} %all-gather.13.cloned.1.call-done), calls=%async_computation.11 | async-start | bytes 2097152 | tf_op jit(solution)/shard_map/slice | solution.py:225
Sparse Core Ops, SparseCore 0:
  11.0 65.5 all-gather.6
  107.3 43.6 all-gather.8
  153.2 46.8 all-gather.10
  227.3 64.5 reduce-scatter.1
  296.0 75.7 all-gather.12

commit v3 on v2

--- a/solution.py
+++ b/solution.py
@@ -3,7 +3,6 @@
 from jax import lax
 from jax.sharding import PartitionSpec as P
 from jax.experimental import pallas as pl
-from jax.experimental.pallas import tpu as pltpu
 
 LANES = 128
 ROW_BLOCK = 64
@@ -108,7 +107,7 @@
     return jnp.pad(flat, (0, pad)).reshape(-1, width)
 
 
-def body(ids, tags, embed, gain, w_in, short_filt, mr_filt, rates, w_out, w_tag):
+def block(ids, tags, embed, gain, w_in, short_filt, mr_filt, rates, w_out, w_tag):
     f32 = jnp.float32
     bf16 = jnp.bfloat16
     high = lax.Precision.HIGHEST
@@ -192,11 +191,14 @@
         shorts.append(jnp.sum(dz * p_ext[taps - 1 - s : taps - 1 - s + rows].astype(f32), axis=0))
     short_part = jnp.stack(shorts, axis=1)
     dpb = dp.astype(bf16)
+    dp_all = lax.all_gather(jnp.transpose(dpb, (1, 0, 2)), "ctx", axis=1, tiled=True)
     du_part = jnp.einsum("tjc,jdc->td", dpb, w_in, preferred_element_type=f32)
     du_part, h_ids_all = lax.optimization_barrier((du_part, h_ids_all))
     dot_part = jnp.sum(du_part * gain_full[None, :] * x0_full, axis=1)
     row_dot = lax.psum(dot_part, "dp")[:, None] / width
-    du = lax.psum_scatter(du_part.astype(bf16), "dp", scatter_dimension=1, tiled=True).astype(f32)
+    n_dp = lax.axis_size("dp")
+    du_chunks = lax.all_to_all(du_part.astype(bf16), "dp", 1, 0, tiled=True)
+    du = jnp.sum(du_chunks.reshape(n_dp, rows, cw).astype(f32), axis=0)
     gain_part = jnp.sum(du * x0 * r, axis=0)
     dn = du * gain[None, :]
     dx0 = dout + r * (dn - x0 * r * r * row_dot)
@@ -215,15 +217,12 @@
     dlog_parts = split2(dlog.reshape(-1))
     tail = jnp.concatenate([small.astype(bf16)] + dlog_parts)
     final = jnp.concatenate(
-        [jnp.transpose(dpb, (1, 0, 2)).reshape(-1, cw), dx0.astype(bf16), as_rows(tail, cw)],
+        [dx0.astype(bf16), as_rows(tail, cw)],
         axis=0,
     )
     final_all = lax.all_gather(final, "ctx", axis=0, tiled=True).reshape(n_ctx, -1, cw)
-    n_proj = 3 * rows
-    dp_all = final_all[:, :n_proj].reshape(n_ctx, 3, rows, cw)
-    dp_all = jnp.transpose(dp_all, (0, 2, 1, 3)).reshape(seq, 3, cw)
-    dx0_all = final_all[:, n_proj : n_proj + rows].reshape(seq, cw).astype(f32)
-    tail_all = final_all[:, n_proj + rows :].reshape(n_ctx, -1).astype(f32)
+    dx0_all = final_all[:, :rows].reshape(seq, cw).astype(f32)
+    tail_all = final_all[:, rows:].reshape(n_ctx, -1).astype(f32)
     small_tot = jnp.sum(tail_all[:, :n_small], axis=0)
     n_dlog = rows * n_tags
     dlog_all = (
@@ -246,7 +245,7 @@
     gain_k = lax.dynamic_slice_in_dim(gain_full, k_ctx * f_cols, f_cols, 0)
     x0_k = jnp.dot(all_hot, embed_k, preferred_element_type=f32)
     u_k = (x0_k * r_all * gain_k[None, :]).astype(bf16)
-    d_w_in = jnp.einsum("td,tjc->jdc", u_k, dp_all, preferred_element_type=f32)
+    d_w_in = jnp.einsum("td,jtc->jdc", u_k, dp_all, preferred_element_type=f32)
 
     v_rows = vocab // n_ctx
     own_hot = (ids_all[:, None] == (k_ctx * v_rows + jnp.arange(v_rows))[None, :]).astype(f32)
@@ -294,7 +293,7 @@
         P("dp", None),
     )
     return jax.shard_map(
-        body,
+        block,
         mesh=mesh,
         in_specs=placed,
         out_specs=(

time: 412 us -> 425 us (1.032)
  blocking collectives: 56.5 us -> 76.5 us
  waiting for transfers between devices: 209 us -> 196 us
  local copies, waits for them, and re-layouts: 41.8 us -> 31.9 us
  matrix products: 29 us -> 37.2 us
    reduce_scatter x1 -> x0, waiting for transfers between devices: 35.3 us -> none  [body(): lax.psum_scatter(du_part.astype(bf16), 'dp', scatter_dimension=1, tiled=T...]
    all_gather x4 -> x5, waiting for transfers between devices: 127 us -> 152 us  [the longest x1 52.2 us: block(): lax.all_gather(jnp.transpose(dpb, (1, 0, 2)), 'ctx', axis=1, tiled=True)]
    psum x2, blocking collectives: 56.5 us -> 76.5 us  [the longest x1 47.5 us: block(): row_dot = lax.psum(dot_part, 'dp')[:, None] / width]
    dot_general x14, matrix products: 29 us -> 37.2 us  [the longest x1 7.04 us: block(): du_part = jnp.einsum('tjc,jdc->td', dpb, w_in, preferred_element_type=f32)]
    reshape x9 -> x7, local copies, waits for them, and re-layouts: 11.1 us -> 4.28 us  [the longest x3 1.45 us: block(): outs.append(small_tot[pos:pos + size].reshape(shape))]
    slice x17, local copies, waits for them, and re-layouts: 12.9 us -> 7.92 us  [the longest x1 4.75 us: block(): embed_full = packed_full[:vocab]]
    all_to_all x1 -> x2, starting transfers between devices: 5.53 us -> 9.25 us  [the longest x1 5.53 us: block(): w_out_cols = lax.all_to_all(w_out, 'dp', 1, 0, tiled=True)]
    unnamed x107 -> x75, local copies, waits for them, and re-layouts: 9.47 us -> 8.12 us
  transfers between devices with their start and end apart: 10 -> 11, of which waited for: 9 -> 9; matrix products, arithmetic and copies ran while one was open for 10% -> 14% of each run, Pallas kernels for 2% -> 2%
where the time goes in v3:
time: 425 us; the launch traced here: 423 us
  waiting for transfers between devices  196 us (46%)
  blocking collectives  76.5 us (18%)
  matrix products  37.2 us (9%)
  local copies, waits for them, and re-layouts  31.9 us (8%)
  other arithmetic  31.5 us (7%)
  starting transfers between devices  22.8 us (5%)
  between operations  16.4 us (4%)
  Pallas kernels  11.3 us (3%)
    all_gather x1, waiting for transfers between devices, block(): lax.all_gather(jnp.transpose(dpb, (1, 0, 2)), 'ctx', axis=1, tiled=True)  52.2 us
    psum x1, blocking collectives, block(): row_dot = lax.psum(dot_part, 'dp')[:, None] / width  47.5 us
    all_gather x1, waiting for transfers between devices, block(): lax.all_gather(final, 'ctx', axis=0, tiled=True).reshape(n_ctx, -1, cw)  41.2 us
    all_gather x1, waiting for transfers between devices, block(): h_full = lax.all_gather(h, 'dp', axis=1, tiled=True)  37.6 us
    all_to_all x1, waiting for transfers between devices, block(): w_out_cols = lax.all_to_all(w_out, 'dp', 1, 0, tiled=True)  32.6 us
    psum x1, blocking collectives, block(): lax.psum(jnp.dot(block_out, w_tag, preferred_element_type=f32), 'dp')  29 us
    all_gather x1, waiting for transfers between devices, block(): packed_full = lax.all_gather(packed, 'dp', axis=1, tiled=True)  20.9 us
    ppermute x4, starting transfers between devices, shifted(): return lax.ppermute(block, axis, route)  13.2 us
  transfers between devices with their start and end apart: 11, of which 9 were waited for; matrix products, arithmetic and copies ran while one was open for 14% of the time, Pallas kernels for 2%

profile of v3, /device:TPU:0, one launch (start us, length us, event | category | flops | bytes accessed | tf_op | source)
XLA Modules:
  0.0 423.4 jit_solution(3039654574239861055)
XLA Ops:
  7.2 0.7 fusion.57
  7.9 2.9 concatenate.30
  10.9 4.1 copy.45
  15.0 5.5 %all-to-all-start = ((bf16[256,16,256]{0,2,1:T(8,128)(2,1)}), bf16[256,16,256]{0,2,1:T(8,128)(2,1)S(1)}, u32[]{:S(2)}, u32[]{:S(2)}) async-start(bf16[256,16,256]{0,2,1:T(8,128)(2,1)} %bitcast.122), calls=%async_computation | async-start | bytes 4194304 | tf_op jit(solution)/shard_map/all_to_all | solution.py:127
  20.6 32.6 %all-to-all-done = bf16[256,16,256]{0,2,1:T(8,128)(2,1)S(1)} async-done(((bf16[256,16,256]{0,2,1:T(8,128)(2,1)}), bf16[256,16,256]{0,2,1:T(8,128)(2,1)S(1)}, u32[]{:S(2)}, u32[]{:S(2)}) %all-to-all-start) | async-done | bytes 2097184 | tf_op jit(solution)/shard_map/all_to_all | solution.py:127
  53.3 2.5 copy.46
  55.7 20.9 %all-gather.8.cloned.1.call-done = bf16[519,4096]{1,0:T(8,128)(2,1)} async-done(((bf16[519,256]{1,0:T(8,128)(2,1)}), bf16[519,4096]{1,0:T(8,128)(2,1)}) %all-gather.8.cloned.1.call-update) | async-done | bytes 4251664 | tf_op jit(solution)/shard_map/all_gather | solution.py:126
  76.6 3.2 multiply_reduce_fusion
  79.8 1.0 convert_add_fusion
  80.9 1.3 fusion.38
  82.4 5.9 %fusion.8 = bf16[256,3,256]{2,0,1:T(8,128)(2,1)S(1)} fusion(bf16[3,4096,256]{2,1,0:T(8,128)(2,1)} %param.14, f32[256,4096]{1,0:T(8,128)S(1)} %fusion.38, f32[4096]{0:T(1024)S(1)} %bitcast.128, f32[256]{0:T(256)S(1)} %select_reduce_fusion.1), kind=kOutput, calls=%fused_computation.20 | convolution fusion | flops 1613955072 | bytes 10896384 | tf_op jit(solution)/shard_map/td,jdc->tjc/dot_general | solution.py:144
  88.4 4.7 %collective-permute-start = (bf16[6,3,256]{2,0,1:T(8,128)(2,1)S(1)}, bf16[6,3,256]{2,0,1:T(8,128)(2,1)S(1)}, u32[]{:S(2)}, u32[]{:S(2)}) collective-permute-start(bf16[6,3,256]{2,0,1:T(8,128)(2,1)S(1)} %slice.200), channel_id=1, source_target_pairs={{0,1},{1,2},{2,3},{3,4},{4,5},{5,6},{6,7},{8,9},{9,10},{10,11},{11... | collective-permute-start | bytes 27656 | tf_op jit(solution)/shard_map/ppermute | solution.py:77
  93.2 1.3 collective-permute-done
  95.3 5.7 %collective-permute-start.1 = (bf16[127,256]{1,0:T(8,128)(2,1)S(1)}, bf16[127,256]{1,0:T(8,128)(2,1)S(1)}, u32[]{:S(2)}, u32[]{:S(2)}) collective-permute-start(bf16[127,256]{1,0:T(8,128)(2,1)S(1)} %slice.214), channel_id=1, source_target_pairs={{0,1},{1,2},{2,3},{3,4},{4,5},{5,6},{6,7},{8,9},{9,10},{10,11},{11... | collective-permute-start | bytes 195080 | tf_op jit(solution)/shard_map/ppermute | solution.py:77
  101.0 0.8 fusion.50.g_ref
  101.9 1.0 collective-permute-done.1
  102.9 0.9 maximum_convert_fusion.kv_ref
  103.8 4.7 %shard_map.177 = f32[256,256]{1,0:T(8,128)} custom-call(f32[384,256]{1,0:T(8,128)} %maximum_convert_fusion.kv_ref, f32[128,256]{1,0:T(8,128)} %fusion.50.g_ref), custom_call_target="tpu_custom_call" | custom-call | tf_op jit(solution)/shard_map/pallas_call | solution.py:23
  108.5 1.6 multiply_convert_fusion.2
  110.3 1.4 fusion.39
  111.7 1.7 maximum_bitcast_fusion.1
  113.4 37.6 %all-gather.10.cloned.1.call-done = bf16[256,4096]{1,0:T(8,128)(2,1)} async-done(((bf16[256,256]{1,0:T(8,128)(2,1)}), bf16[256,4096]{1,0:T(8,128)(2,1)}) %all-gather.10.cloned.1.call-update) | async-done | bytes 2097168 | tf_op jit(solution)/shard_map/all_gather | solution.py:160
  150.9 2.9 fusion.11
  154.7 29.0 %psum.14 = f32[256,4]{0,1:T(4,128)S(1)} all-reduce(f32[256,4]{0,1:T(4,128)S(1)} %fusion.67), channel_id=1, replica_groups=mesh['dp'=16,'ctx'=8] {'dp'}, use_global_device_ids=true, to_apply=%region_2.3 | all-reduce | flops 1024 | bytes 8192 | tf_op jit(solution)/shard_map/psum | solution.py:167
  184.4 4.1 convolution_convert_fusion
  188.5 1.0 convolution_convert_fusion.2
  189.5 0.8 copy.50
  190.4 2.3 multiply_bitcast_fusion.2
  192.7 0.7 copy-done.8
  193.4 1.5 collective-permute-start.2
  194.9 1.0 reshape.131
  196.7 0.7 reshape.130
  197.4 3.7 collective-permute-done.2
  201.1 1.8 maximum_maximum_fusion.dm_ref
  202.9 6.6 %shard_map.178 = (f32[256,256]{1,0:T(8,128)}, f32[128,256]{1,0:T(8,128)}) custom-call(f32[384,256]{1,0:T(8,128)} %maximum_maximum_fusion.dm_ref, f32[384,256]{1,0:T(8,128)} %maximum_convert_fusion.kv_ref, f32[128,256]{1,0:T(8,128)} %fusion.50.g_ref), custom_call_target="tpu_custom_call" | custom-call | tf_op jit(solution)/shard_map/pallas_call | solution.py:55
  209.5 1.0 multiply_bitcast_fusion.1
  210.6 1.3 collective-permute-start.3
  211.9 1.3 fusion.26
  213.2 5.1 %collective-permute-done.3 = f32[6,3,256]{2,0,1:T(8,128)S(1)} collective-permute-done((f32[6,3,256]{2,0,1:T(8,128)S(1)}, f32[6,3,256]{2,0,1:T(8,128)S(1)}, u32[]{:S(2)}, u32[]{:S(2)}) %collective-permute-start.3) | collective-permute-done | bytes 18464 | tf_op jit(solution)/shard_map/ppermute | solution.py:77
  218.4 7.0 %convolution_bitcast_fusion = f32[256,4096]{1,0:T(8,128)} fusion(bf16[3,4096,256]{2,1,0:T(8,128)(2,1)} %param.14, f32[262,3,256]{2,0,1:T(8,128)S(1)} %pad_maximum_fusion, f32[3,256]{1,0:T(4,128)S(1)} %get-tuple-element.111, f32[3,256]{1,0:T(4,128)S(1)} %get-tuple-element.112, f32[3,256]{1,0:T(4,128)S(1)} %get-tuple-element.113, ...), kind=kOutput, calls=%fused_computation.1 | convolution fusion | flops 1613758464 | bytes 16019456 | tf_op jit(solution)/shard_map/tjc,jdc->td/dot_general | solution.py:195
  225.5 6.0 %multiply_reduce_fusion.1 = (f32[256]{0:T(256)}, bf16[256,4096]{1,0:T(8,128)(2,1)S(1)}) fusion(f32[256,4096]{1,0:T(8,128)} %copy-done.1, f32[256,4096]{1,0:T(8,128)} %convolution_bitcast_fusion, f32[4096]{0:T(1024)S(1)} %bitcast.129), kind=kLoop, calls=%fused_computation.7 | loop fusion | flops 4194048 | bytes 10503168 | tf_op jit(solution)/shard_map/reduce_sum | solution.py:197
  231.5 1.5 copy.76
  233.0 3.7 all-to-all-start.1
  237.0 1.1 multiply_reduce_fusion.3
  238.6 47.5 %psum.15 = f32[256]{0:T(256)} all-reduce(f32[256]{0:T(256)} %get-tuple-element.83), channel_id=1, replica_groups=mesh['dp'=16,'ctx'=8] {'dp'}, use_global_device_ids=true, to_apply=%region_7.8 | all-reduce | flops 256 | bytes 2048 | tf_op jit(solution)/shard_map/psum | solution.py:198
  286.1 1.2 broadcast_multiply_fusion
  287.7 1.1 multiply_reduce_fusion.2
  288.7 1.3 fusion.12
  290.0 3.5 concatenate.37
  293.5 0.7 maximum_bitcast_fusion
  294.5 2.4 fusion.89
  297.4 0.9 slice.176
  298.3 4.7 %slice.155 = bf16[512,4096]{1,0:T(8,128)(2,1)} slice(bf16[519,4096]{1,0:T(8,128)(2,1)} %all-gather.8.cloned.1.call-done), slice={[0:512], [0:4096]} | slice | bytes 8388608 | tf_op jit(solution)/shard_map/slice | solution.py:129
  303.1 0.9 select_reduce_fusion
  304.1 41.2 %all-gather.16.cloned.1.call-done = bf16[8,420,256]{2,1,0:T(8,128)(2,1)} async-done(((bf16[1,420,256]{2,1,0:T(8,128)(2,1)}), bf16[8,420,256]{2,1,0:T(8,128)(2,1)}) %all-gather.16.cloned.1.call-update) | async-done | bytes 1720336 | tf_op jit(solution)/shard_map/all_gather | solution.py:223
  345.3 1.1 slice.223
  347.7 1.1 reshape.138
  348.8 0.7 reshape.136
  352.1 1.4 fusion.13
  353.5 1.8 convolution_convert_fusion.1
  355.3 1.5 fusion.68
  356.8 52.2 %all-gather.12.cloned.1.call-done = bf16[3,2048,256]{2,1,0:T(8,128)(2,1)} async-done(((bf16[3,256,256]{2,1,0:T(8,128)(2,1)}), bf16[3,2048,256]{2,1,0:T(8,128)(2,1)}) %all-gather.12.cloned.1.call-update) | async-done | bytes 3145744 | tf_op jit(solution)/shard_map/all_gather | solution.py:194
  409.0 5.1 %convolution_bitcast_fusion.1 = f32[3,512,256]{1,2,0:T(8,128)S(1)} fusion(bf16[3,2048,256]{2,1,0:T(8,128)(2,1)} %all-gather.12.cloned.1.call-done, f32[512]{0:T(512)S(1)} %bitcast.138, f32[2048]{0:T(1024)S(1)} %select_reduce_fusion, s32[2048]{0:T(1024)S(1)} %bitcast.132, bf16[512,4096]{1,0:T(8,128)(2,1)} %slice.155, s32[]{:T(128)S(6)} %select_n.28), kind=kOutput, calls=%fused_computation.18 | convolution fusion | flops 2688548864 | bytes 5261316 | tf_op jit(solution)/shard_map/td,jtc->jdc/dot_general | solution.py:248
  414.1 1.6 copy.53
  (138 shorter events, 8.8 us)
Async XLA Ops:
  7.2 69.4 %all-gather.8.cloned.1.call-start = ((), (), s32[]{:S(2)}) async-start(), calls=%async_computation.2 | async-start | bytes 4526080 | tf_op jit(solution)/shard_map/all_gather | solution.py:126
  10.9 9.7 %copy-start.13 = (f32[3,7,256]{2,1,0:T(8,128)S(1)}, f32[3,7,256]{2,1,0:T(8,128)}, u32[]{:S(2)}) copy-start(f32[3,7,256]{2,1,0:T(8,128)} %param.15) | copy-start | bytes 64516
  15.0 38.3 %all-to-all-start = ((bf16[256,16,256]{0,2,1:T(8,128)(2,1)}), bf16[256,16,256]{0,2,1:T(8,128)(2,1)S(1)}, u32[]{:S(2)}, u32[]{:S(2)}) async-start(bf16[256,16,256]{0,2,1:T(8,128)(2,1)} %bitcast.122), calls=%async_computation | async-start | bytes 4194304 | tf_op jit(solution)/shard_map/all_to_all | solution.py:127
  20.5 130.4 %all-gather.10.cloned.1.call-start = ((), (), s32[]{:S(2)}) async-start(), calls=%async_computation.3 | async-start | bytes 2228224 | tf_op jit(solution)/shard_map/all_gather | solution.py:160
  53.3 27.6 %copy-start.17 = (s32[256]{0:T(256)S(1)}, s32[256]{0:T(256)}, u32[]{:S(2)}) copy-start(s32[256]{0:T(256)} %param.10) | copy-start | bytes 3076
  76.6 4.3 %copy-start = (bf16[519,4096]{1,0:T(8,128)(2,1)S(1)}, bf16[519,4096]{1,0:T(8,128)(2,1)}, u32[]{:S(2)}) copy-start(bf16[519,4096]{1,0:T(8,128)(2,1)} %all-gather.8.cloned.1.call-done) | copy-start | bytes 12754948
  80.9 1.3 copy-start.15
  82.2 6.2 %copy-start.1 = (f32[256,4096]{1,0:T(8,128)}, f32[256,4096]{1,0:T(8,128)S(1)}, u32[]{:S(2)}) copy-start(f32[256,4096]{1,0:T(8,128)S(1)} %fusion.38) | copy-start | bytes 12582916
  82.4 6.0 %copy-start.18 = (f32[256]{0:T(256)}, f32[256]{0:T(256)S(1)}, u32[]{:S(2)}) copy-start(f32[256]{0:T(256)S(1)} %select_reduce_fusion.1) | copy-start | bytes 3076
  82.4 10.8 %copy-start.27 = (f32[256]{0:T(256)S(1)}, f32[256]{0:T(256)}, u32[]{:S(2)}) copy-start(f32[256]{0:T(256)} %param.17) | copy-start | bytes 3076
  82.4 18.6 %copy-start.11 = (f32[128,256]{1,0:T(8,128)S(1)}, f32[128,256]{1,0:T(8,128)}, u32[]{:S(2)}) copy-start(f32[128,256]{1,0:T(8,128)} %param.16) | copy-start | bytes 393220
  88.4 6.1 %copy-start.6 = (bf16[256,3,256]{2,0,1:T(8,128)(2,1)}, bf16[256,3,256]{2,0,1:T(8,128)(2,1)S(1)}, u32[]{:S(2)}) copy-start(bf16[256,3,256]{2,0,1:T(8,128)(2,1)S(1)} %fusion.8) | copy-start | bytes 1179652
  88.4 6.1 %collective-permute-start = (bf16[6,3,256]{2,0,1:T(8,128)(2,1)S(1)}, bf16[6,3,256]{2,0,1:T(8,128)(2,1)S(1)}, u32[]{:S(2)}, u32[]{:S(2)}) collective-permute-start(bf16[6,3,256]{2,0,1:T(8,128)(2,1)S(1)} %slice.200), channel_id=1, source_target_pairs={{0,1},{1,2},{2,3},{3,4},{4,5},{5,6},{6,7},{8,9},{9,10},{10,11},{11... | collective-permute-start | bytes 27656 | tf_op jit(solution)/shard_map/ppermute | solution.py:77
  93.2 8.6 %copy-start.25 = (f32[128]{0:T(128)}, f32[128]{0:T(128)S(1)}, u32[]{:S(2)}) copy-start(f32[128]{0:T(128)S(1)} %iota_convert_fusion) | copy-start | bytes 1540
  93.2 125.2 %copy-start.12 = (f32[3,1,256]{2,0,1:T(4,128)}, f32[3,1,256]{2,0,1:T(4,128)S(1)}, u32[]{:S(2)}) copy-start(f32[3,1,256]{2,0,1:T(4,128)S(1)} %copy.77) | copy-start | bytes 9220
  95.3 59.3 %copy-start.14 = (bf16[256,4]{0,1:T(4,128)(2,1)S(1)}, bf16[256,4]{0,1:T(4,128)(2,1)}, u32[]{:S(2)}) copy-start(bf16[256,4]{0,1:T(4,128)(2,1)} %param.19) | copy-start | bytes 6148
  95.3 88.5 %copy-start.24 = (s32[256]{0:T(256)S(1)}, s32[256]{0:T(256)}, u32[]{:S(2)}) copy-start(s32[256]{0:T(256)} %param.11) | copy-start | bytes 3076
  95.3 7.6 %collective-permute-start.1 = (bf16[127,256]{1,0:T(8,128)(2,1)S(1)}, bf16[127,256]{1,0:T(8,128)(2,1)S(1)}, u32[]{:S(2)}, u32[]{:S(2)}) collective-permute-start(bf16[127,256]{1,0:T(8,128)(2,1)S(1)} %slice.214), channel_id=1, source_target_pairs={{0,1},{1,2},{2,3},{3,4},{4,5},{5,6},{6,7},{8,9},{9,10},{10,11},{11... | collective-permute-start | bytes 195080 | tf_op jit(solution)/shard_map/ppermute | solution.py:77
  110.1 80.2 %copy-start.2 = (bf16[256,4096]{1,0:T(8,128)(2,1)S(1)}, bf16[256,4096]{1,0:T(8,128)(2,1)}, u32[]{:S(2)}) copy-start(bf16[256,4096]{1,0:T(8,128)(2,1)} %param.18) | copy-start | bytes 6291460
  110.1 80.2 %copy-start.5 = (f32[256,256]{1,0:T(8,128)S(1)}, f32[256,256]{1,0:T(8,128)}, u32[]{:S(2)}) copy-start(f32[256,256]{1,0:T(8,128)} %shard_map.177) | copy-start | bytes 786436
  110.1 115.3 %all-gather.14.cloned.1.call-start = ((), (), s32[]{:S(2)}) async-start(), calls=%async_computation.5 | async-start | bytes 1216512 | tf_op jit(solution)/shard_map/all_gather | solution.py:166
  111.7 77.8 %copy-start.4 = (f32[256,256]{1,0:T(8,128)}, f32[256,256]{1,0:T(8,128)S(1)}, u32[]{:S(2)}) copy-start(f32[256,256]{1,0:T(8,128)S(1)} %fusion.39) | copy-start | bytes 786436
  153.9 0.7 copy-start.9
  192.7 0.7 copy-start.8
  192.7 19.2 %copy-start.7 = (bf16[256,3,256]{2,0,1:T(8,128)(2,1)S(1)}, bf16[256,3,256]{2,0,1:T(8,128)(2,1)}, u32[]{:S(2)}) copy-start(bf16[256,3,256]{2,0,1:T(8,128)(2,1)} %copy-done.6) | copy-start | bytes 1179652
  193.4 7.7 %collective-permute-start.2 = (bf16[127,256]{1,0:T(8,128)(2,1)S(1)}, bf16[127,256]{1,0:T(8,128)(2,1)S(1)}, u32[]{:S(2)}, u32[]{:S(2)}) collective-permute-start(bf16[127,256]{1,0:T(8,128)(2,1)S(1)} %slice.360), channel_id=1, source_target_pairs={{1,0},{2,1},{3,2},{4,3},{5,4},{6,5},{7,6},{9,8},{10,9},{11,10},{12... | collective-permute-start | bytes 195080 | tf_op jit(solution)/shard_map/ppermute | solution.py:77
  210.5 15.0 %copy-start.3 = (f32[256,1,256]{2,0,1:T(8,128)}, f32[256,1,256]{2,0,1:T(8,128)S(1)}, u32[]{:S(2)}) copy-start(f32[256,1,256]{2,0,1:T(8,128)S(1)} %get-tuple-element.90) | copy-start | bytes 786436
  210.6 7.8 %collective-permute-start.3 = (f32[6,3,256]{2,0,1:T(8,128)S(1)}, f32[6,3,256]{2,0,1:T(8,128)S(1)}, u32[]{:S(2)}, u32[]{:S(2)}) collective-permute-start(f32[6,3,256]{2,0,1:T(8,128)S(1)} %slice.216), channel_id=1, source_target_pairs={{1,0},{2,1},{3,2},{4,3},{5,4},{6,5},{7,6},{9,8},{10,9},{11,10},{12... | collective-permute-start | bytes 55304 | tf_op jit(solution)/shard_map/ppermute | solution.py:77
  231.4 5.3 %copy-start.23 = (bf16[3,256]{1,0:T(4,128)(2,1)S(1)}, bf16[3,256]{1,0:T(4,128)(2,1)}, u32[]{:S(2)}) copy-start(bf16[3,256]{1,0:T(4,128)(2,1)} %get-tuple-element.85) | copy-start | bytes 4612
  231.4 5.4 %copy-start.22 = (bf16[3,256]{1,0:T(4,128)(2,1)S(1)}, bf16[3,256]{1,0:T(4,128)(2,1)}, u32[]{:S(2)}) copy-start(bf16[3,256]{1,0:T(4,128)(2,1)} %get-tuple-element.87) | copy-start | bytes 4612
  231.4 5.4 %copy-start.21 = (bf16[3,256]{1,0:T(4,128)(2,1)S(1)}, bf16[3,256]{1,0:T(4,128)(2,1)}, u32[]{:S(2)}) copy-start(bf16[3,256]{1,0:T(4,128)(2,1)} %get-tuple-element.86) | copy-start | bytes 4612
  231.5 5.4 %copy-start.20 = (bf16[3,256]{1,0:T(4,128)(2,1)S(1)}, bf16[3,256]{1,0:T(4,128)(2,1)}, u32[]{:S(2)}) copy-start(bf16[3,256]{1,0:T(4,128)(2,1)} %get-tuple-element.76) | copy-start | bytes 4612
  231.5 5.4 %copy-start.19 = (bf16[3,256]{1,0:T(4,128)(2,1)S(1)}, bf16[3,256]{1,0:T(4,128)(2,1)}, u32[]{:S(2)}) copy-start(bf16[3,256]{1,0:T(4,128)(2,1)} %get-tuple-element.77) | copy-start | bytes 4612
  231.5 5.5 %copy-start.26 = (f32[128]{0:T(128)S(1)}, f32[128]{0:T(128)}, u32[]{:S(2)}) copy-start(f32[128]{0:T(128)} %copy-done.25) | copy-start | bytes 1540
  233.0 54.3 %all-to-all-start.1 = ((bf16[256,16,256]{2,0,1:T(8,128)(2,1)}), bf16[256,16,256]{2,0,1:T(8,128)(2,1)S(1)}, u32[]{:S(2)}, u32[]{:S(2)}) async-start(bf16[256,16,256]{2,0,1:T(8,128)(2,1)} %bitcast.120), calls=%async_computation.1 | async-start | bytes 4194304 | tf_op jit(solution)/shard_map/all_to_all | solution.py:200
  236.7 108.6 %all-gather.16.cloned.1.call-start = ((), (), s32[]{:S(2)}) async-start(), calls=%async_computation.6 | async-start | bytes 1953792 | tf_op jit(solution)/shard_map/all_gather | solution.py:223
  294.3 114.8 %all-gather.12.cloned.1.call-start = ((), (), s32[]{:S(2)}) async-start(), calls=%async_computation.4 | async-start | bytes 3538944 | tf_op jit(solution)/shard_map/all_gather | solution.py:194
  298.3 4.8 %copy-start.10 = (bf16[8,258,256]{2,1,0:T(8,128)(2,1)S(1)}, bf16[8,258,256]{2,1,0:T(8,128)(2,1)}, u32[]{:S(2)}) copy-start(bf16[8,258,256]{2,1,0:T(8,128)(2,1)} %all-gather.14.cloned.1.call-done) | copy-start | bytes 3170308
  298.3 4.8 %copy-start.16 = (f32[512]{0:T(512)S(1)}, f32[512]{0:T(512)}, u32[]{:S(2)}) copy-start(f32[512]{0:T(512)} %copy-done.15) | copy-start | bytes 6148
  346.5 5.7 %slice-start = ((bf16[8,420,256]{2,1,0:T(8,128)(2,1)}), bf16[8,256,256]{2,1,0:T(8,128)(2,1)S(1)}, s32[]{:S(2)}) async-start(bf16[8,420,256]{2,1,0:T(8,128)(2,1)} %all-gather.16.cloned.1.call-done), calls=%async_computation.7 | async-start | bytes 2097152 | tf_op jit(solution)/shard_map/slice | solution.py:224
  346.5 5.6 %copy-start.28 = (s32[64]{0:T(128)S(1)}, s32[64]{0:T(128)}, u32[]{:S(2)}) copy-start(s32[64]{0:T(128)} %iota_add_fusion) | copy-start | bytes 772
  347.0 8.2 %slice-start.1 = ((bf16[8,258,256]{2,1,0:T(8,128)(2,1)}), bf16[8,256,256]{2,1,0:T(8,128)(2,1)S(1)}, s32[]{:S(2)}) async-start(bf16[8,258,256]{2,1,0:T(8,128)(2,1)} %all-gather.14.cloned.1.call-done), calls=%async_computation.8 | async-start | bytes 2097152 | tf_op jit(solution)/shard_map/slice | solution.py:232
Sparse Core Ops, SparseCore 0:
  11.0 65.5 all-gather.7
  110.3 40.6 all-gather.9
  153.3 46.8 all-gather.13
  294.4 50.8 all-gather.15
  348.1 60.9 all-gather.11

commit v4 on v3

--- a/solution.py
+++ b/solution.py
@@ -164,7 +164,12 @@
     id_lo = (ids % 32).astype(bf16)
     h_ids = jnp.concatenate([h, as_rows(jnp.concatenate([id_hi, id_lo]), cw)], axis=0)
     h_ids_all = lax.all_gather(h_ids, "ctx", axis=0, tiled=True).reshape(n_ctx, -1, cw)
-    logits = lax.psum(jnp.dot(block_out, w_tag, preferred_element_type=f32), "dp")
+    logit_part = jnp.dot(block_out, w_tag, preferred_element_type=f32)
+    n_dp = lax.axis_size("dp")
+    logit_parts = lax.all_to_all(
+        jnp.broadcast_to(logit_part[None], (n_dp,) + logit_part.shape), "dp", 0, 0, tiled=True
+    )
+    logits = jnp.sum(logit_parts, axis=0)
     top = jnp.max(logits, axis=1)
     lse = top + jnp.log(jnp.sum(jnp.exp(logits - top[:, None]), axis=1))
     tag_hot = (tags[:, None] == jnp.arange(n_tags)[None, :]).astype(f32)
@@ -195,10 +200,20 @@
     du_part = jnp.einsum("tjc,jdc->td", dpb, w_in, preferred_element_type=f32)
     du_part, h_ids_all = lax.optimization_barrier((du_part, h_ids_all))
     dot_part = jnp.sum(du_part * gain_full[None, :] * x0_full, axis=1)
-    row_dot = lax.psum(dot_part, "dp")[:, None] / width
     n_dp = lax.axis_size("dp")
-    du_chunks = lax.all_to_all(du_part.astype(bf16), "dp", 1, 0, tiled=True)
-    du = jnp.sum(du_chunks.reshape(n_dp, rows, cw).astype(f32), axis=0)
+    dot_rows = as_rows(jnp.concatenate(split2(dot_part)), cw)
+    n_dot = dot_rows.shape[0]
+    du_send = jnp.concatenate(
+        [
+            du_part.astype(bf16).reshape(rows, n_dp, cw),
+            jnp.broadcast_to(dot_rows[:, None, :], (n_dot, n_dp, cw)),
+        ],
+        axis=0,
+    )
+    du_recv = lax.all_to_all(du_send, "dp", 1, 1, tiled=True).astype(f32)
+    du = jnp.sum(du_recv[:rows], axis=1)
+    dot_recv = jnp.sum(du_recv[rows:], axis=1).reshape(-1)
+    row_dot = (dot_recv[:rows] + dot_recv[rows : 2 * rows])[:, None] / width
     gain_part = jnp.sum(du * x0 * r, axis=0)
     dn = du * gain[None, :]
     dx0 = dout + r * (dn - x0 * r * r * row_dot)
@@ -220,7 +235,9 @@
         [dx0.astype(bf16), as_rows(tail, cw)],
         axis=0,
     )
-    final_all = lax.all_gather(final, "ctx", axis=0, tiled=True).reshape(n_ctx, -1, cw)
+    final_all = lax.all_to_all(
+        jnp.broadcast_to(final[None], (n_ctx,) + final.shape), "ctx", 0, 0, tiled=True
+    )
     dx0_all = final_all[:, :rows].reshape(seq, cw).astype(f32)
     tail_all = final_all[:, rows:].reshape(n_ctx, -1).astype(f32)
     small_tot = jnp.sum(tail_all[:, :n_small], axis=0)

time: 425 us -> 332 us (0.78)
  blocking collectives: 76.5 us -> 0 us
  waiting for transfers between devices: 196 us -> 161 us
  starting transfers between devices: 22.8 us -> 32.6 us
  local copies, waits for them, and re-layouts: 31.9 us -> 39.6 us
    psum x2 -> x0, blocking collectives: 76.5 us -> none  [the longest x1 47.5 us: block(): row_dot = lax.psum(dot_part, 'dp')[:, None] / width]
    all_to_all x1 -> x3, waiting for transfers between devices: 0.01 us -> 52.8 us  [the longest x1 31.2 us: block(): lax.all_to_all(jnp.broadcast_to(final[None], (n_ctx,) + final.shape), 'ct...]
    all_gather x1, waiting for transfers between devices: 52.2 us -> 0.01 us  [block(): lax.all_gather(jnp.transpose(dpb, (1, 0, 2)), 'ctx', axis=1, tiled=True)]
    all_gather x1 -> x0, waiting for transfers between devices: 41.2 us -> none  [block(): lax.all_gather(final, 'ctx', axis=0, tiled=True).reshape(n_ctx, -1, cw)]
    all_to_all x1 -> x3, starting transfers between devices: 3.72 us -> 13.7 us  [the longest x1 5.47 us: block(): lax.all_to_all(jnp.broadcast_to(final[None], (n_ctx,) + final.shape), 'ct...]
    unnamed x75 -> x89, local copies, waits for them, and re-layouts: 8.12 us -> 16.9 us
    convert_element_type x0 -> x2, other arithmetic: none -> 5.75 us  [the longest x1 5.41 us: block(): du_part.astype(bf16).reshape(rows, n_dp, cw)]
    reduce_sum x2 -> x3, other arithmetic: 6.27 us -> 1.22 us  [the longest x1 0.93 us: block(): dot_recv = jnp.sum(du_recv[rows:], axis=1).reshape(-1)]
  transfers between devices with their start and end apart: 11 -> 12, of which waited for: 9 -> 11; matrix products, arithmetic and copies ran while one was open for 14% -> 20% of each run, Pallas kernels for 2% -> 2%
where the time goes in v4:
time: 332 us; the launch traced here: 328 us
  waiting for transfers between devices  161 us (48%)
  local copies, waits for them, and re-layouts  39.6 us (12%)
  matrix products  37 us (11%)
  starting transfers between devices  32.6 us (10%)
  other arithmetic  29.8 us (9%)
  between operations  16.6 us (5%)
  Pallas kernels  11.3 us (3%)
    all_gather x1, waiting for transfers between devices, block(): h_full = lax.all_gather(h, 'dp', axis=1, tiled=True)  41.4 us
    all_to_all x1, waiting for transfers between devices, block(): w_out_cols = lax.all_to_all(w_out, 'dp', 1, 0, tiled=True)  32.6 us
    all_to_all x1, waiting for transfers between devices, block(): lax.all_to_all(jnp.broadcast_to(final[None], (n_ctx,) + final.shape), 'ct...  31.2 us
    all_gather x1, waiting for transfers between devices, block(): packed_full = lax.all_gather(packed, 'dp', axis=1, tiled=True)  20.9 us
    all_to_all x1, waiting for transfers between devices, block(): du_recv = lax.all_to_all(du_send, 'dp', 1, 1, tiled=True).astype(f32)  17.1 us
    unnamed x89, local copies, waits for them, and re-layouts  16.9 us
    ppermute x4, starting transfers between devices, shifted(): return lax.ppermute(block, axis, route)  13.2 us
    ppermute x4, waiting for transfers between devices, shifted(): return lax.ppermute(block, axis, route)  10.8 us
  transfers between devices with their start and end apart: 12, of which 11 were waited for; matrix products, arithmetic and copies ran while one was open for 20% of the time, Pallas kernels for 2%

profile of v4, /device:TPU:0, one launch (start us, length us, event | category | flops | bytes accessed | tf_op | source)
XLA Modules:
  0.0 328.3 jit_solution(18161882104547653991)
XLA Ops:
  7.9 2.9 concatenate.37
  10.9 4.1 %copy.56 = bf16[256,4096]{0,1:T(8,128)(2,1)} copy(bf16[256,4096]{1,0:T(8,128)(2,1)} %param.18) | data formatting | bytes 4194304 | tf_op args[8]
  15.0 5.5 %all-to-all-start = ((bf16[256,16,256]{0,2,1:T(8,128)(2,1)}), bf16[256,16,256]{0,2,1:T(8,128)(2,1)S(1)}, u32[]{:S(2)}, u32[]{:S(2)}) async-start(bf16[256,16,256]{0,2,1:T(8,128)(2,1)} %bitcast.123), calls=%async_computation | async-start | bytes 4194304 | tf_op jit(solution)/shard_map/all_to_all | solution.py:127
  20.7 32.6 %all-to-all-done = bf16[256,16,256]{0,2,1:T(8,128)(2,1)S(1)} async-done(((bf16[256,16,256]{0,2,1:T(8,128)(2,1)}), bf16[256,16,256]{0,2,1:T(8,128)(2,1)S(1)}, u32[]{:S(2)}, u32[]{:S(2)}) %all-to-all-start) | async-done | bytes 2097184 | tf_op jit(solution)/shard_map/all_to_all | solution.py:127
  53.3 2.5 copy.57
  55.8 20.9 %all-gather.6.cloned.1.call-done = bf16[519,4096]{1,0:T(8,128)(2,1)} async-done(((bf16[519,256]{1,0:T(8,128)(2,1)}), bf16[519,4096]{1,0:T(8,128)(2,1)}) %all-gather.6.cloned.1.call-update) | async-done | bytes 4251664 | tf_op jit(solution)/shard_map/all_gather | solution.py:126
  76.6 3.2 multiply_reduce_fusion
  79.8 1.0 convert_add_fusion
  80.9 1.3 fusion.38
  82.5 5.9 %fusion.8 = bf16[256,3,256]{2,0,1:T(8,128)(2,1)S(1)} fusion(bf16[3,4096,256]{2,1,0:T(8,128)(2,1)} %param.14, f32[256,4096]{1,0:T(8,128)S(1)} %fusion.38, f32[4096]{0:T(1024)S(1)} %bitcast.130, f32[256]{0:T(256)S(1)} %select_reduce_fusion.1), kind=kOutput, calls=%fused_computation.21 | convolution fusion | flops 1613955072 | bytes 10896384 | tf_op jit(solution)/shard_map/td,jdc->tjc/dot_general | solution.py:144
  88.4 4.7 %collective-permute-start = (bf16[6,3,256]{2,0,1:T(8,128)(2,1)S(1)}, bf16[6,3,256]{2,0,1:T(8,128)(2,1)S(1)}, u32[]{:S(2)}, u32[]{:S(2)}) collective-permute-start(bf16[6,3,256]{2,0,1:T(8,128)(2,1)S(1)} %slice.218), channel_id=1, source_target_pairs={{0,1},{1,2},{2,3},{3,4},{4,5},{5,6},{6,7},{8,9},{9,10},{10,11},{11... | collective-permute-start | bytes 27656 | tf_op jit(solution)/shard_map/ppermute | solution.py:77
  93.3 1.3 collective-permute-done
  95.4 5.7 %collective-permute-start.1 = (bf16[127,256]{1,0:T(8,128)(2,1)S(1)}, bf16[127,256]{1,0:T(8,128)(2,1)S(1)}, u32[]{:S(2)}, u32[]{:S(2)}) collective-permute-start(bf16[127,256]{1,0:T(8,128)(2,1)S(1)} %slice.232), channel_id=1, source_target_pairs={{0,1},{1,2},{2,3},{3,4},{4,5},{5,6},{6,7},{8,9},{9,10},{10,11},{11... | collective-permute-start | bytes 195080 | tf_op jit(solution)/shard_map/ppermute | solution.py:77
  101.9 1.0 collective-permute-done.1
  103.0 0.9 maximum_convert_fusion.kv_ref
  103.8 4.7 %shard_map.177 = f32[256,256]{1,0:T(8,128)} custom-call(f32[384,256]{1,0:T(8,128)} %maximum_convert_fusion.kv_ref, f32[128,256]{1,0:T(8,128)} %fusion.50.g_ref), custom_call_target="tpu_custom_call" | custom-call | tf_op jit(solution)/shard_map/pallas_call | solution.py:23
  108.5 1.6 multiply_convert_fusion.2
  110.9 1.4 fusion.39
  112.3 41.4 %all-gather.8.cloned.1.call-done = bf16[256,4096]{1,0:T(8,128)(2,1)} async-done(((bf16[256,256]{1,0:T(8,128)(2,1)}), bf16[256,4096]{1,0:T(8,128)(2,1)}) %all-gather.8.cloned.1.call-update) | async-done | bytes 2097168 | tf_op jit(solution)/shard_map/all_gather | solution.py:160
  153.7 2.9 fusion.11
  158.1 4.1 %all-to-all-start.1 = ((f32[16,256,4]{1,2,0:T(4,128)}), f32[16,256,4]{1,2,0:T(4,128)S(1)}, u32[]{:S(2)}, u32[]{:S(2)}) async-start(f32[16,256,4]{1,2,0:T(4,128)} %broadcast_in_dim.38), calls=%async_computation.1 | async-start | bytes 131072 | tf_op jit(solution)/shard_map/all_to_all | solution.py:169
  162.3 1.6 maximum_bitcast_fusion
  163.9 4.5 %all-to-all-done.1 = f32[16,256,4]{1,2,0:T(4,128)S(1)} async-done(((f32[16,256,4]{1,2,0:T(4,128)}), f32[16,256,4]{1,2,0:T(4,128)S(1)}, u32[]{:S(2)}, u32[]{:S(2)}) %all-to-all-start.1) | async-done | bytes 65568 | tf_op jit(solution)/shard_map/all_to_all | solution.py:169
  169.1 4.1 %convolution_convert_fusion = bf16[256,4096]{1,0:T(8,128)(2,1)} fusion(f32[256,4]{0,1:T(4,128)S(1)} %convert_subtract_fusion, bf16[519,4096]{1,0:T(8,128)(2,1)} %all-gather.6.cloned.1.call-done), kind=kOutput, calls=%fused_computation.2 | convolution fusion | flops 51380224 | bytes 2134016 | tf_op jit(solution)/shard_map/dot_general | solution.py:180
  173.2 1.7 convolution_convert_fusion.2
  174.9 0.8 copy.61
  175.7 2.4 multiply_bitcast_fusion.2
  178.9 1.5 collective-permute-start.2
  180.3 1.0 sub.67
  182.8 3.7 %collective-permute-done.2 = bf16[127,256]{1,0:T(8,128)(2,1)S(1)} collective-permute-done((bf16[127,256]{1,0:T(8,128)(2,1)S(1)}, bf16[127,256]{1,0:T(8,128)(2,1)S(1)}, u32[]{:S(2)}, u32[]{:S(2)}) %collective-permute-start.2) | collective-permute-done | bytes 65056 | tf_op jit(solution)/shard_map/ppermute | solution.py:77
  186.5 1.8 maximum_maximum_fusion.dm_ref
  188.3 6.6 %shard_map.178 = (f32[256,256]{1,0:T(8,128)}, f32[128,256]{1,0:T(8,128)}) custom-call(f32[384,256]{1,0:T(8,128)} %maximum_maximum_fusion.dm_ref, f32[384,256]{1,0:T(8,128)} %maximum_convert_fusion.kv_ref, f32[128,256]{1,0:T(8,128)} %fusion.50.g_ref), custom_call_target="tpu_custom_call" | custom-call | tf_op jit(solution)/shard_map/pallas_call | solution.py:55
  194.9 1.0 multiply_bitcast_fusion.1
  196.0 1.3 collective-permute-start.3
  197.3 1.3 fusion.26
  199.2 4.7 %collective-permute-done.3 = f32[6,3,256]{2,0,1:T(8,128)S(1)} collective-permute-done((f32[6,3,256]{2,0,1:T(8,128)S(1)}, f32[6,3,256]{2,0,1:T(8,128)S(1)}, u32[]{:S(2)}, u32[]{:S(2)}) %collective-permute-start.3) | collective-permute-done | bytes 18464 | tf_op jit(solution)/shard_map/ppermute | solution.py:77
  204.0 7.1 %convolution_bitcast_fusion = f32[256,4096]{1,0:T(8,128)} fusion(bf16[3,4096,256]{2,1,0:T(8,128)(2,1)} %param.14, f32[262,3,256]{2,0,1:T(8,128)S(1)} %pad_maximum_fusion.1, f32[3,256]{1,0:T(4,128)S(1)} %get-tuple-element.123, f32[3,256]{1,0:T(4,128)S(1)} %get-tuple-element.124, f32[3,256]{1,0:T(4,128)S(1)} %get-tuple-element.125, ...), kind=kOutput, calls=%fused_computation.1 | convolution fusion | flops 1613758464 | bytes 16019456 | tf_op jit(solution)/shard_map/tjc,jdc->td/dot_general | solution.py:200
  211.1 2.9 all-gather.12.cloned.1.call-done
  214.1 5.4 %fusion.67 = (bf16[256,4096]{1,0:T(8,128)(2,1)S(1)}, f32[256]{0:T(256)S(1)}) fusion(f32[256,4096]{1,0:T(8,128)} %convolution_bitcast_fusion, f32[256,4096]{1,0:T(8,128)} %copy-done.2, f32[4096]{0:T(1024)S(1)} %bitcast.131), kind=kLoop, calls=%fused_computation.174 | loop fusion | flops 4194048 | bytes 10503168 | tf_op jit(solution)/shard_map/convert_element_type | solution.py:208
  219.7 1.5 pad_maximum_fusion
  221.3 4.1 %all-to-all-start.2 = ((bf16[258,16,256]{2,0,1:T(8,128)(2,1)}), bf16[258,16,256]{2,0,1:T(8,128)(2,1)S(1)}, u32[]{:S(2)}, u32[]{:S(2)}) async-start(bf16[258,16,256]{2,0,1:T(8,128)(2,1)} %pad_maximum_fusion), calls=%async_computation.2 | async-start | bytes 4325376 | tf_op jit(solution)/shard_map/all_to_all | solution.py:213
  225.4 1.3 constant_dynamic-update-slice_fusion.5
  226.7 2.4 fusion.92
  229.1 1.2 constant_dynamic-update-slice_fusion.4
  230.3 1.3 constant_dynamic-update-slice_fusion.3
  231.6 1.3 constant_dynamic-update-slice_fusion.2
  232.8 1.3 constant_dynamic-update-slice_fusion.1
  235.4 1.1 multiply_reduce_fusion.3
  236.6 17.1 %all-to-all-done.2 = bf16[258,16,256]{2,0,1:T(8,128)(2,1)S(1)} async-done(((bf16[258,16,256]{2,0,1:T(8,128)(2,1)}), bf16[258,16,256]{2,0,1:T(8,128)(2,1)S(1)}, u32[]{:S(2)}, u32[]{:S(2)}) %all-to-all-start.2) | async-done | bytes 2113568 | tf_op jit(solution)/shard_map/all_to_all | solution.py:213
  254.1 2.0 copy-done.1
  256.5 0.8 concatenate.46
  257.4 0.9 slice_reduce_fusion.2
  258.7 1.4 broadcast_in_dim.47
  260.1 5.5 %all-to-all-start.3 = ((bf16[8,420,256]{2,1,0:T(8,128)(2,1)}), bf16[8,420,256]{2,1,0:T(8,128)(2,1)S(1)}, u32[]{:S(2)}, u32[]{:S(2)}) async-start(bf16[8,420,256]{2,1,0:T(8,128)(2,1)} %broadcast_in_dim.47), calls=%async_computation.3 | async-start | bytes 3473408 | tf_op jit(solution)/shard_map/all_to_all | solution.py:238
  265.6 0.9 slice.190
  266.4 4.7 %slice.169 = bf16[512,4096]{1,0:T(8,128)(2,1)} slice(bf16[519,4096]{1,0:T(8,128)(2,1)} %all-gather.6.cloned.1.call-done), slice={[0:512], [0:4096]} | slice | bytes 8388608 | tf_op jit(solution)/shard_map/slice | solution.py:129
  271.2 0.9 select_reduce_fusion
  272.2 31.2 %all-to-all-done.3 = bf16[8,420,256]{2,1,0:T(8,128)(2,1)S(1)} async-done(((bf16[8,420,256]{2,1,0:T(8,128)(2,1)}), bf16[8,420,256]{2,1,0:T(8,128)(2,1)S(1)}, u32[]{:S(2)}, u32[]{:S(2)}) %all-to-all-start.3) | async-done | bytes 1720352 | tf_op jit(solution)/shard_map/all_to_all | solution.py:238
  304.6 1.1 reshape.178
  309.2 1.4 fusion.13
  310.6 1.8 convolution_convert_fusion.1
  312.4 1.5 fusion.71
  313.9 5.1 %convolution_bitcast_fusion.1 = f32[3,512,256]{1,2,0:T(8,128)S(1)} fusion(bf16[3,2048,256]{2,1,0:T(8,128)(2,1)} %all-gather.10.cloned.1.call-done, f32[512]{0:T(512)S(1)} %bitcast.142, f32[2048]{0:T(1024)S(1)} %select_reduce_fusion, s32[2048]{0:T(1024)S(1)} %bitcast.134, bf16[512,4096]{1,0:T(8,128)(2,1)} %slice.169, s32[]{:T(128)S(6)} %select_n.28), kind=kOutput, calls=%fused_computation.19 | convolution fusion | flops 2688548864 | bytes 5261316 | tf_op jit(solution)/shard_map/td,jtc->jdc/dot_general | solution.py:265
  319.0 1.6 copy.64
  (159 shorter events, 15.4 us)
Async XLA Ops:
  7.2 69.4 %all-gather.6.cloned.1.call-start = ((), (), s32[]{:S(2)}) async-start(), calls=%async_computation.4 | async-start | bytes 4526080 | tf_op jit(solution)/shard_map/all_gather | solution.py:126
  10.9 9.7 %copy-start.17 = (f32[3,7,256]{2,1,0:T(8,128)S(1)}, f32[3,7,256]{2,1,0:T(8,128)}, u32[]{:S(2)}) copy-start(f32[3,7,256]{2,1,0:T(8,128)} %param.15) | copy-start | bytes 64516
  15.0 38.3 %all-to-all-start = ((bf16[256,16,256]{0,2,1:T(8,128)(2,1)}), bf16[256,16,256]{0,2,1:T(8,128)(2,1)S(1)}, u32[]{:S(2)}, u32[]{:S(2)}) async-start(bf16[256,16,256]{0,2,1:T(8,128)(2,1)} %bitcast.123), calls=%async_computation | async-start | bytes 4194304 | tf_op jit(solution)/shard_map/all_to_all | solution.py:127
  20.5 133.2 %all-gather.8.cloned.1.call-start = ((), (), s32[]{:S(2)}) async-start(), calls=%async_computation.5 | async-start | bytes 2228224 | tf_op jit(solution)/shard_map/all_gather | solution.py:160
  53.3 27.6 %copy-start.22 = (s32[256]{0:T(256)S(1)}, s32[256]{0:T(256)}, u32[]{:S(2)}) copy-start(s32[256]{0:T(256)} %param.10) | copy-start | bytes 3076
  76.6 4.3 %copy-start = (bf16[519,4096]{1,0:T(8,128)(2,1)S(1)}, bf16[519,4096]{1,0:T(8,128)(2,1)}, u32[]{:S(2)}) copy-start(bf16[519,4096]{1,0:T(8,128)(2,1)} %all-gather.6.cloned.1.call-done) | copy-start | bytes 12754948
  80.9 1.3 copy-start.20
  82.2 6.2 %copy-start.2 = (f32[256,4096]{1,0:T(8,128)}, f32[256,4096]{1,0:T(8,128)S(1)}, u32[]{:S(2)}) copy-start(f32[256,4096]{1,0:T(8,128)S(1)} %fusion.38) | copy-start | bytes 12582916
  82.4 6.0 %copy-start.25 = (f32[256]{0:T(256)}, f32[256]{0:T(256)S(1)}, u32[]{:S(2)}) copy-start(f32[256]{0:T(256)S(1)} %select_reduce_fusion.1) | copy-start | bytes 3076
  82.4 10.8 %copy-start.35 = (f32[256]{0:T(256)S(1)}, f32[256]{0:T(256)}, u32[]{:S(2)}) copy-start(f32[256]{0:T(256)} %param.17) | copy-start | bytes 3076
  82.4 18.6 %copy-start.13 = (f32[128,256]{1,0:T(8,128)S(1)}, f32[128,256]{1,0:T(8,128)}, u32[]{:S(2)}) copy-start(f32[128,256]{1,0:T(8,128)} %param.16) | copy-start | bytes 393220
  88.4 6.2 %copy-start.8 = (bf16[256,3,256]{2,0,1:T(8,128)(2,1)}, bf16[256,3,256]{2,0,1:T(8,128)(2,1)S(1)}, u32[]{:S(2)}) copy-start(bf16[256,3,256]{2,0,1:T(8,128)(2,1)S(1)} %fusion.8) | copy-start | bytes 1179652
  88.4 6.1 %collective-permute-start = (bf16[6,3,256]{2,0,1:T(8,128)(2,1)S(1)}, bf16[6,3,256]{2,0,1:T(8,128)(2,1)S(1)}, u32[]{:S(2)}, u32[]{:S(2)}) collective-permute-start(bf16[6,3,256]{2,0,1:T(8,128)(2,1)S(1)} %slice.218), channel_id=1, source_target_pairs={{0,1},{1,2},{2,3},{3,4},{4,5},{5,6},{6,7},{8,9},{9,10},{10,11},{11... | collective-permute-start | bytes 27656 | tf_op jit(solution)/shard_map/ppermute | solution.py:77
  93.2 17.0 %copy-start.34 = (f32[128]{0:T(128)}, f32[128]{0:T(128)S(1)}, u32[]{:S(2)}) copy-start(f32[128]{0:T(128)S(1)} %iota_convert_fusion) | copy-start | bytes 1540
  93.2 2.1 copy-start.14
  93.3 17.0 %copy-start.23 = (f32[256]{0:T(256)}, f32[256]{0:T(256)S(1)}, u32[]{:S(2)}) copy-start(f32[256]{0:T(256)S(1)} %neg.7) | copy-start | bytes 3076
  95.3 62.0 %copy-start.18 = (bf16[256,4]{0,1:T(4,128)(2,1)S(1)}, bf16[256,4]{0,1:T(4,128)(2,1)}, u32[]{:S(2)}) copy-start(bf16[256,4]{0,1:T(4,128)(2,1)} %param.19) | copy-start | bytes 6148
  95.3 73.1 %copy-start.33 = (s32[256]{0:T(256)S(1)}, s32[256]{0:T(256)}, u32[]{:S(2)}) copy-start(s32[256]{0:T(256)} %param.11) | copy-start | bytes 3076
  95.4 7.6 %collective-permute-start.1 = (bf16[127,256]{1,0:T(8,128)(2,1)S(1)}, bf16[127,256]{1,0:T(8,128)(2,1)S(1)}, u32[]{:S(2)}, u32[]{:S(2)}) collective-permute-start(bf16[127,256]{1,0:T(8,128)(2,1)S(1)} %slice.232), channel_id=1, source_target_pairs={{0,1},{1,2},{2,3},{3,4},{4,5},{5,6},{6,7},{8,9},{9,10},{10,11},{11... | collective-permute-start | bytes 195080 | tf_op jit(solution)/shard_map/ppermute | solution.py:77
  110.9 64.8 %copy-start.3 = (bf16[256,4096]{1,0:T(8,128)(2,1)S(1)}, bf16[256,4096]{1,0:T(8,128)(2,1)}, u32[]{:S(2)}) copy-start(bf16[256,4096]{1,0:T(8,128)(2,1)} %param.18) | copy-start | bytes 6291460
  110.9 64.8 %copy-start.7 = (f32[256,256]{1,0:T(8,128)S(1)}, f32[256,256]{1,0:T(8,128)}, u32[]{:S(2)}) copy-start(f32[256,256]{1,0:T(8,128)} %shard_map.177) | copy-start | bytes 786436
  112.3 62.6 %copy-start.5 = (f32[256,256]{1,0:T(8,128)}, f32[256,256]{1,0:T(8,128)S(1)}, u32[]{:S(2)}) copy-start(f32[256,256]{1,0:T(8,128)S(1)} %fusion.39) | copy-start | bytes 786436
  156.6 0.7 copy-start.11
  158.1 10.3 %all-to-all-start.1 = ((f32[16,256,4]{1,2,0:T(4,128)}), f32[16,256,4]{1,2,0:T(4,128)S(1)}, u32[]{:S(2)}, u32[]{:S(2)}) async-start(f32[16,256,4]{1,2,0:T(4,128)} %broadcast_in_dim.38), calls=%async_computation.1 | async-start | bytes 131072 | tf_op jit(solution)/shard_map/all_to_all | solution.py:169
  162.3 51.8 %all-gather.12.cloned.1.call-start = ((), (), s32[]{:S(2)}) async-start(), calls=%async_computation.7 | async-start | bytes 1216512 | tf_op jit(solution)/shard_map/all_gather | solution.py:166
  175.7 6.3 %copy-start.28 = (bf16[256,4]{0,1:T(4,128)(2,1)S(1)}, bf16[256,4]{0,1:T(4,128)(2,1)}, u32[]{:S(2)}) copy-start(bf16[256,4]{0,1:T(4,128)(2,1)} %convolution_convert_fusion.2) | copy-start | bytes 6148
  178.1 0.7 copy-start.10
  178.1 19.2 %copy-start.9 = (bf16[256,3,256]{2,0,1:T(8,128)(2,1)S(1)}, bf16[256,3,256]{2,0,1:T(8,128)(2,1)}, u32[]{:S(2)}) copy-start(bf16[256,3,256]{2,0,1:T(8,128)(2,1)} %copy-done.8) | copy-start | bytes 1179652
  178.1 25.9 %copy-start.15 = (f32[3,1,256]{2,0,1:T(4,128)S(1)}, f32[3,1,256]{2,0,1:T(4,128)}, u32[]{:S(2)}) copy-start(f32[3,1,256]{2,0,1:T(4,128)} %copy-done.14) | copy-start | bytes 9220
  178.9 7.7 %collective-permute-start.2 = (bf16[127,256]{1,0:T(8,128)(2,1)S(1)}, bf16[127,256]{1,0:T(8,128)(2,1)S(1)}, u32[]{:S(2)}, u32[]{:S(2)}) collective-permute-start(bf16[127,256]{1,0:T(8,128)(2,1)S(1)} %slice.388), channel_id=1, source_target_pairs={{1,0},{2,1},{3,2},{4,3},{5,4},{6,5},{7,6},{9,8},{10,9},{11,10},{12... | collective-permute-start | bytes 195080 | tf_op jit(solution)/shard_map/ppermute | solution.py:77
  195.9 8.1 %copy-start.4 = (f32[256,1,256]{2,0,1:T(8,128)}, f32[256,1,256]{2,0,1:T(8,128)S(1)}, u32[]{:S(2)}) copy-start(f32[256,1,256]{2,0,1:T(8,128)S(1)} %get-tuple-element.100) | copy-start | bytes 786436
  196.0 7.9 %collective-permute-start.3 = (f32[6,3,256]{2,0,1:T(8,128)S(1)}, f32[6,3,256]{2,0,1:T(8,128)S(1)}, u32[]{:S(2)}, u32[]{:S(2)}) collective-permute-start(f32[6,3,256]{2,0,1:T(8,128)S(1)} %slice.234), channel_id=1, source_target_pairs={{1,0},{2,1},{3,2},{4,3},{5,4},{6,5},{7,6},{9,8},{10,9},{11,10},{12... | collective-permute-start | bytes 55304 | tf_op jit(solution)/shard_map/ppermute | solution.py:77
  219.7 7.0 %copy-start.16 = (f32[3,1,256]{2,0,1:T(4,128)S(1)}, f32[3,1,256]{2,0,1:T(4,128)}, u32[]{:S(2)}) copy-start(f32[3,1,256]{2,0,1:T(4,128)} %copy-done.14) | copy-start | bytes 9220
  221.3 32.5 %all-to-all-start.2 = ((bf16[258,16,256]{2,0,1:T(8,128)(2,1)}), bf16[258,16,256]{2,0,1:T(8,128)(2,1)S(1)}, u32[]{:S(2)}, u32[]{:S(2)}) async-start(bf16[258,16,256]{2,0,1:T(8,128)(2,1)} %pad_maximum_fusion), calls=%async_computation.2 | async-start | bytes 4325376 | tf_op jit(solution)/shard_map/all_to_all | solution.py:213
  225.4 8.7 %copy-start.29 = (bf16[3,256]{1,0:T(4,128)(2,1)S(1)}, bf16[3,256]{1,0:T(4,128)(2,1)}, u32[]{:S(2)}) copy-start(bf16[3,256]{1,0:T(4,128)(2,1)} %get-tuple-element.98) | copy-start | bytes 4612
  225.4 10.0 %copy-start.24 = (f32[256]{0:T(256)S(1)}, f32[256]{0:T(256)}, u32[]{:S(2)}) copy-start(f32[256]{0:T(256)} %copy-done.23) | copy-start | bytes 3076
  225.4 88.5 %all-gather.10.cloned.1.call-start = ((), (), s32[]{:S(2)}) async-start(), calls=%async_computation.6 | async-start | bytes 3538944 | tf_op jit(solution)/shard_map/all_gather | solution.py:199
  236.6 19.8 %copy-start.6 = (f32[256,256]{1,0:T(8,128)S(1)}, f32[256,256]{1,0:T(8,128)}, u32[]{:S(2)}) copy-start(f32[256,256]{1,0:T(8,128)} %copy-done.5) | copy-start | bytes 786436
  236.6 19.8 %copy-start.26 = (f32[256]{0:T(256)S(1)}, f32[256]{0:T(256)}, u32[]{:S(2)}) copy-start(f32[256]{0:T(256)} %copy-done.25) | copy-start | bytes 3076
  236.6 19.9 %copy-start.27 = (bf16[1024]{0:T(1024)(128)(2,1)S(1)}, bf16[1024]{0:T(1024)(128)(2,1)}, u32[]{:S(2)}) copy-start(bf16[1024]{0:T(1024)(128)(2,1)} %reshape.172) | copy-start | bytes 6148
  236.6 19.9 %copy-start.30 = (bf16[1024]{0:T(1024)(128)(2,1)S(1)}, bf16[1024]{0:T(1024)(128)(2,1)}, u32[]{:S(2)}) copy-start(bf16[1024]{0:T(1024)(128)(2,1)} %get-tuple-element.114) | copy-start | bytes 6148
  236.6 19.9 %copy-start.31 = (bf16[1024]{0:T(1024)(128)(2,1)S(1)}, bf16[1024]{0:T(1024)(128)(2,1)}, u32[]{:S(2)}) copy-start(bf16[1024]{0:T(1024)(128)(2,1)} %get-tuple-element.115) | copy-start | bytes 6148
  254.1 2.0 copy-start.1
  256.1 2.2 copy-start.19
  256.1 2.2 copy-start.32
  260.1 43.3 %all-to-all-start.3 = ((bf16[8,420,256]{2,1,0:T(8,128)(2,1)}), bf16[8,420,256]{2,1,0:T(8,128)(2,1)S(1)}, u32[]{:S(2)}, u32[]{:S(2)}) async-start(bf16[8,420,256]{2,1,0:T(8,128)(2,1)} %broadcast_in_dim.47), calls=%async_computation.3 | async-start | bytes 3473408 | tf_op jit(solution)/shard_map/all_to_all | solution.py:238
  266.4 4.8 %copy-start.12 = (bf16[8,258,256]{2,1,0:T(8,128)(2,1)S(1)}, bf16[8,258,256]{2,1,0:T(8,128)(2,1)}, u32[]{:S(2)}) copy-start(bf16[8,258,256]{2,1,0:T(8,128)(2,1)} %all-gather.12.cloned.1.call-done) | copy-start | bytes 3170308
  266.4 4.8 %copy-start.21 = (f32[512]{0:T(512)S(1)}, f32[512]{0:T(512)}, u32[]{:S(2)}) copy-start(f32[512]{0:T(512)} %copy-done.20) | copy-start | bytes 6148
  307.8 4.6 %slice-start = ((bf16[8,258,256]{2,1,0:T(8,128)(2,1)}), bf16[8,256,256]{2,1,0:T(8,128)(2,1)S(1)}, s32[]{:S(2)}) async-start(bf16[8,258,256]{2,1,0:T(8,128)(2,1)} %all-gather.12.cloned.1.call-done), calls=%async_computation.8 | async-start | bytes 2097152 | tf_op jit(solution)/shard_map/slice | solution.py:249
Sparse Core Ops, SparseCore 0:
  11.0 65.5 all-gather.5
  110.3 43.3 all-gather.7
  165.4 48.6 all-gather.11
  229.2 83.8 all-gather.9

commit v5 on v4

--- a/solution.py
+++ b/solution.py
@@ -122,15 +122,21 @@
     k_ctx = lax.axis_index("ctx")
     seq = rows * n_ctx
 
-    packed = jnp.concatenate([embed, jnp.stack(split3(gain), axis=0), w_tag.T], axis=0)
+    n_dp = lax.axis_size("dp")
+    half = vocab // 2
+    packed = jnp.concatenate([embed[:half], jnp.stack(split3(gain), axis=0), w_tag.T], axis=0)
     packed_full = lax.all_gather(packed, "dp", axis=1, tiled=True)
-    w_out_cols = lax.all_to_all(w_out, "dp", 1, 0, tiled=True)
-    packed_full, w_out_cols = lax.optimization_barrier((packed_full, w_out_cols))
-    embed_full = packed_full[:vocab]
+    upper = lax.all_to_all(
+        jnp.broadcast_to(embed[None, half:], (n_dp, vocab - half, cw)), "dp", 0, 0, tiled=True
+    )
+    upper_full = jnp.transpose(upper, (1, 0, 2)).reshape(vocab - half, width)
+    w_out_later, upper_full = lax.optimization_barrier((w_out, upper_full))
+    w_out_cols = lax.all_to_all(w_out_later, "dp", 1, 0, tiled=True)
+    embed_full = jnp.concatenate([packed_full[:half], upper_full], axis=0)
     gain_full = (
-        packed_full[vocab].astype(f32) + packed_full[vocab + 1].astype(f32)
-    ) + packed_full[vocab + 2].astype(f32)
-    w_tag_full_t = packed_full[vocab + 3 : vocab + 3 + n_tags].astype(f32)
+        packed_full[half].astype(f32) + packed_full[half + 1].astype(f32)
+    ) + packed_full[half + 2].astype(f32)
+    w_tag_full_t = packed_full[half + 3 : half + 3 + n_tags].astype(f32)
 
     emb32 = embed_full.astype(f32)
     r_vocab = lax.rsqrt(jnp.sum(emb32 * emb32, axis=1) / width + 1e-06)
@@ -165,7 +171,6 @@
     h_ids = jnp.concatenate([h, as_rows(jnp.concatenate([id_hi, id_lo]), cw)], axis=0)
     h_ids_all = lax.all_gather(h_ids, "ctx", axis=0, tiled=True).reshape(n_ctx, -1, cw)
     logit_part = jnp.dot(block_out, w_tag, preferred_element_type=f32)
-    n_dp = lax.axis_size("dp")
     logit_parts = lax.all_to_all(
         jnp.broadcast_to(logit_part[None], (n_dp,) + logit_part.shape), "dp", 0, 0, tiled=True
     )
@@ -200,7 +205,6 @@
     du_part = jnp.einsum("tjc,jdc->td", dpb, w_in, preferred_element_type=f32)
     du_part, h_ids_all = lax.optimization_barrier((du_part, h_ids_all))
     dot_part = jnp.sum(du_part * gain_full[None, :] * x0_full, axis=1)
-    n_dp = lax.axis_size("dp")
     dot_rows = as_rows(jnp.concatenate(split2(dot_part)), cw)
     n_dot = dot_rows.shape[0]
     du_send = jnp.concatenate(

time: 332 us -> 341 us (1.027)
  waiting for transfers between devices: 161 us -> 167 us
  starting transfers between devices: 32.6 us -> 37.1 us
    all_gather x1, waiting for transfers between devices: 41.4 us -> 15.1 us  [block(): h_full = lax.all_gather(h, 'dp', axis=1, tiled=True)]
    all_to_all x1 -> x2, waiting for transfers between devices: 32.6 us -> 57.2 us  [the longest x1 31.3 us: block(): lax.all_to_all(jnp.broadcast_to(embed[None, half:], (n_dp, vocab - half,...]
    all_gather x1, waiting for transfers between devices: 20.9 us -> 14.9 us  [block(): packed_full = lax.all_gather(packed, 'dp', axis=1, tiled=True)]
    unnamed x89 -> x108, local copies, waits for them, and re-layouts: 16.9 us -> 11.5 us
    all_to_all x1 -> x2, starting transfers between devices: 5.53 us -> 10.2 us  [the longest x1 5.71 us: block(): lax.all_to_all(jnp.broadcast_to(embed[None, half:], (n_dp, vocab - half,...]
    all_to_all x1, waiting for transfers between devices: 17.1 us -> 21.7 us  [block(): du_recv = lax.all_to_all(du_send, 'dp', 1, 1, tiled=True).astype(f32)]
    all_to_all x1 -> x2, local copies, waits for them, and re-layouts: 2.48 us -> 6.76 us  [the longest x1 3.91 us: block(): w_out_cols = lax.all_to_all(w_out_later, 'dp', 1, 0, tiled=True)]
    all_gather x1, waiting for transfers between devices: 2.94 us -> 7.13 us  [block(): lax.all_gather(h_ids, 'ctx', axis=0, tiled=True).reshape(n_ctx, -1, cw)]
  transfers between devices with their start and end apart: 12 -> 13, of which waited for: 11 -> 12; matrix products, arithmetic and copies ran while one was open for 20% -> 19% of each run, Pallas kernels for 2% -> 2%
where the time goes in v5:
time: 341 us; the launch traced here: 338 us
  waiting for transfers between devices  167 us (49%)
  local copies, waits for them, and re-layouts  41.3 us (12%)
  starting transfers between devices  37.1 us (11%)
  matrix products  35.3 us (10%)
  other arithmetic  29.5 us (9%)
  between operations  16.6 us (5%)
  Pallas kernels  11.3 us (3%)
    all_to_all x1, waiting for transfers between devices, block(): lax.all_to_all(jnp.broadcast_to(final[None], (n_ctx,) + final.shape), 'ct...  32.4 us
    all_to_all x1, waiting for transfers between devices, block(): lax.all_to_all(jnp.broadcast_to(embed[None, half:], (n_dp, vocab - half,...  31.3 us
    all_to_all x1, waiting for transfers between devices, block(): w_out_cols = lax.all_to_all(w_out_later, 'dp', 1, 0, tiled=True)  26 us
    all_to_all x1, waiting for transfers between devices, block(): du_recv = lax.all_to_all(du_send, 'dp', 1, 1, tiled=True).astype(f32)  21.7 us
    all_gather x1, waiting for transfers between devices, block(): h_full = lax.all_gather(h, 'dp', axis=1, tiled=True)  15.1 us
    all_gather x1, waiting for transfers between devices, block(): packed_full = lax.all_gather(packed, 'dp', axis=1, tiled=True)  14.9 us
    ppermute x4, waiting for transfers between devices, shifted(): return lax.ppermute(block, axis, route)  13.7 us
    ppermute x4, starting transfers between devices, shifted(): return lax.ppermute(block, axis, route)  13.2 us
  transfers between devices with their start and end apart: 13, of which 12 were waited for; matrix products, arithmetic and copies ran while one was open for 19% of the time, Pallas kernels for 2%

profile of v5, /device:TPU:0, one launch (start us, length us, event | category | flops | bytes accessed | tf_op | source)
XLA Modules:
  0.0 337.7 jit_solution(6248302152743846776)
XLA Ops:
  8.2 0.8 copy.90
  9.0 1.0 fusion.72
  10.1 0.8 concatenate.40
  11.0 1.5 broadcast_in_dim.37
  12.5 5.7 %all-to-all-start = ((bf16[16,256,256]{2,1,0:T(8,128)(2,1)}), bf16[16,256,256]{2,1,0:T(8,128)(2,1)}, u32[]{:S(2)}, u32[]{:S(2)}) async-start(bf16[16,256,256]{2,1,0:T(8,128)(2,1)} %broadcast_in_dim.37), calls=%async_computation | async-start | bytes 4194304 | tf_op jit(solution)/shard_map/all_to_all | solution.py:129
  18.3 31.3 %all-to-all-done = bf16[16,256,256]{2,1,0:T(8,128)(2,1)} async-done(((bf16[16,256,256]{2,1,0:T(8,128)(2,1)}), bf16[16,256,256]{2,1,0:T(8,128)(2,1)}, u32[]{:S(2)}, u32[]{:S(2)}) %all-to-all-start) | async-done | bytes 2097184 | tf_op jit(solution)/shard_map/all_to_all | solution.py:129
  49.6 2.8 copy.94
  52.5 14.9 %all-gather.6.cloned.1.call-done = bf16[263,4096]{0,1:T(8,128)(2,1)} async-done(((bf16[263,256]{0,1:T(8,128)(2,1)}), bf16[263,4096]{0,1:T(8,128)(2,1)}) %all-gather.6.cloned.1.call-update) | async-done | bytes 2154512 | tf_op jit(solution)/shard_map/all_gather | solution.py:128
  67.3 1.7 slice.226
  69.1 1.0 multiply_reduce_fusion
  70.2 4.3 %fusion.2 = f32[256,4096]{1,0:T(8,128)S(1)} fusion(bf16[256,4096]{0,1:T(8,128)(2,1)} %bitcast.123, bf16[256,4096]{0,1:T(8,128)(2,1)S(1)} %slice.226, s32[256]{0:T(256)S(1)} %copy-done.32), kind=kOutput, calls=%fused_computation.15 | convolution fusion | flops 1082261504 | bytes 8389632 | tf_op jit(solution)/shard_map/dot_general | solution.py:147
  74.7 2.5 fusion.70
  77.3 1.9 fusion.9
  79.1 4.8 %collective-permute-start = (bf16[6,3,256]{2,0,1:T(8,128)(2,1)S(1)}, bf16[6,3,256]{2,0,1:T(8,128)(2,1)S(1)}, u32[]{:S(2)}, u32[]{:S(2)}) collective-permute-start(bf16[6,3,256]{2,0,1:T(8,128)(2,1)S(1)} %slice.230), channel_id=1, source_target_pairs={{0,1},{1,2},{2,3},{3,4},{4,5},{5,6},{6,7},{8,9},{9,10},{10,11},{11... | collective-permute-start | bytes 27656 | tf_op jit(solution)/shard_map/ppermute | solution.py:77
  84.0 1.3 collective-permute-done
  86.0 0.9 copy-done.6
  86.9 5.7 %collective-permute-start.1 = (bf16[127,256]{1,0:T(8,128)(2,1)S(1)}, bf16[127,256]{1,0:T(8,128)(2,1)S(1)}, u32[]{:S(2)}, u32[]{:S(2)}) collective-permute-start(bf16[127,256]{1,0:T(8,128)(2,1)S(1)} %slice.244), channel_id=1, source_target_pairs={{0,1},{1,2},{2,3},{3,4},{4,5},{5,6},{6,7},{8,9},{9,10},{10,11},{11... | collective-permute-start | bytes 195080 | tf_op jit(solution)/shard_map/ppermute | solution.py:77
  93.5 1.0 collective-permute-done.1
  94.5 0.9 maximum_convert_fusion.kv_ref
  95.4 4.7 %shard_map.177 = f32[256,256]{1,0:T(8,128)} custom-call(f32[384,256]{1,0:T(8,128)} %maximum_convert_fusion.kv_ref, f32[128,256]{1,0:T(8,128)} %fusion.52.g_ref), custom_call_target="tpu_custom_call" | custom-call | tf_op jit(solution)/shard_map/pallas_call | solution.py:23
  100.1 1.7 multiply_convert_fusion.2
  101.8 4.1 %copy.95 = bf16[256,4096]{0,1:T(8,128)(2,1)} copy(bf16[256,4096]{1,0:T(8,128)(2,1)} %param.18) | data formatting | bytes 4194304 | tf_op jit(solution)/shard_map/optimization_barrier | solution.py:133
  105.9 4.4 %all-to-all-start.1 = ((bf16[256,16,256]{0,2,1:T(8,128)(2,1)}), bf16[256,16,256]{0,2,1:T(8,128)(2,1)}, u32[]{:S(2)}, u32[]{:S(2)}) async-start(bf16[256,16,256]{0,2,1:T(8,128)(2,1)} %bitcast.125), calls=%async_computation.1 | async-start | bytes 4194304 | tf_op jit(solution)/shard_map/all_to_all | solution.py:134
  111.7 1.2 fusion.40
  112.9 26.0 %all-to-all-done.1 = bf16[256,16,256]{0,2,1:T(8,128)(2,1)} async-done(((bf16[256,16,256]{0,2,1:T(8,128)(2,1)}), bf16[256,16,256]{0,2,1:T(8,128)(2,1)}, u32[]{:S(2)}, u32[]{:S(2)}) %all-to-all-start.1) | async-done | bytes 2097184 | tf_op jit(solution)/shard_map/all_to_all | solution.py:134
  138.9 3.9 %copy.96 = bf16[16,256,256]{2,1,0:T(8,128)(2,1)} copy(bf16[16,256,256]{1,2,0:T(8,128)(2,1)} %bitcast.8) | data formatting | bytes 4194304 | tf_op jit(solution)/shard_map/all_to_all | solution.py:134
  142.8 15.1 %all-gather.8.cloned.1.call-done = bf16[256,4096]{1,0:T(8,128)(2,1)} async-done(((bf16[256,256]{1,0:T(8,128)(2,1)}), bf16[256,4096]{1,0:T(8,128)(2,1)}) %all-gather.8.cloned.1.call-update) | async-done | bytes 2097168 | tf_op jit(solution)/shard_map/all_gather | solution.py:166
  157.9 2.9 fusion.12
  162.2 3.5 %all-to-all-start.2 = ((f32[16,256,4]{1,2,0:T(4,128)}), f32[16,256,4]{1,2,0:T(4,128)S(1)}, u32[]{:S(2)}, u32[]{:S(2)}) async-start(f32[16,256,4]{1,2,0:T(4,128)} %broadcast_in_dim.41), calls=%async_computation.2 | async-start | bytes 131072 | tf_op jit(solution)/shard_map/all_to_all | solution.py:174
  165.9 1.6 maximum_bitcast_fusion
  167.5 4.3 %all-to-all-done.2 = f32[16,256,4]{1,2,0:T(4,128)S(1)} async-done(((f32[16,256,4]{1,2,0:T(4,128)}), f32[16,256,4]{1,2,0:T(4,128)S(1)}, u32[]{:S(2)}, u32[]{:S(2)}) %all-to-all-start.2) | async-done | bytes 65568 | tf_op jit(solution)/shard_map/all_to_all | solution.py:174
  173.8 1.7 convolution_convert_fusion.2
  176.3 2.2 convolution_convert_fusion
  178.5 1.8 multiply_bitcast_fusion.2
  180.3 1.4 collective-permute-start.2
  183.3 7.4 %collective-permute-done.2 = bf16[127,256]{1,0:T(8,128)(2,1)S(1)} collective-permute-done((bf16[127,256]{1,0:T(8,128)(2,1)S(1)}, bf16[127,256]{1,0:T(8,128)(2,1)S(1)}, u32[]{:S(2)}, u32[]{:S(2)}) %collective-permute-start.2) | collective-permute-done | bytes 65056 | tf_op jit(solution)/shard_map/ppermute | solution.py:77
  190.8 0.9 maximum_maximum_fusion.dm_ref
  191.6 6.5 %shard_map.178 = (f32[256,256]{1,0:T(8,128)}, f32[128,256]{1,0:T(8,128)}) custom-call(f32[384,256]{1,0:T(8,128)} %maximum_maximum_fusion.dm_ref, f32[384,256]{1,0:T(8,128)} %maximum_convert_fusion.kv_ref, f32[128,256]{1,0:T(8,128)} %fusion.52.g_ref), custom_call_target="tpu_custom_call" | custom-call | tf_op jit(solution)/shard_map/pallas_call | solution.py:55
  198.2 1.0 multiply_bitcast_fusion.1
  199.3 1.3 collective-permute-start.3
  200.6 1.3 fusion.27
  202.5 4.0 %collective-permute-done.3 = f32[6,3,256]{2,0,1:T(8,128)S(1)} collective-permute-done((f32[6,3,256]{2,0,1:T(8,128)S(1)}, f32[6,3,256]{2,0,1:T(8,128)S(1)}, u32[]{:S(2)}, u32[]{:S(2)}) %collective-permute-start.3) | collective-permute-done | bytes 18464 | tf_op jit(solution)/shard_map/ppermute | solution.py:77
  206.6 7.1 %convolution_bitcast_fusion = f32[256,4096]{1,0:T(8,128)} fusion(bf16[3,4096,256]{2,1,0:T(8,128)(2,1)} %param.14, f32[262,3,256]{2,0,1:T(8,128)S(1)} %pad_maximum_fusion.3, f32[3,256]{1,0:T(4,128)S(1)} %get-tuple-element.147, f32[3,256]{1,0:T(4,128)S(1)} %get-tuple-element.148, f32[3,256]{1,0:T(4,128)S(1)} %get-tuple-element.149, ...), kind=kOutput, calls=%fused_computation.1 | convolution fusion | flops 1613758464 | bytes 16019456 | tf_op jit(solution)/shard_map/tjc,jdc->td/dot_general | solution.py:205
  213.7 7.1 %all-gather.12.cloned.1.call-done = bf16[8,258,256]{2,1,0:T(8,128)(2,1)} async-done(((bf16[1,258,256]{2,1,0:T(8,128)(2,1)}), bf16[8,258,256]{2,1,0:T(8,128)(2,1)}) %all-gather.12.cloned.1.call-update) | async-done | bytes 1056784 | tf_op jit(solution)/shard_map/all_gather | solution.py:172
  220.8 5.4 %fusion.71 = (bf16[256,4096]{1,0:T(8,128)(2,1)S(1)}, f32[256]{0:T(256)S(1)}) fusion(f32[256,4096]{1,0:T(8,128)} %convolution_bitcast_fusion, f32[256,4096]{1,0:T(8,128)} %copy-done.11, f32[4096]{0:T(1024)S(1)} %get-tuple-element.113), kind=kLoop, calls=%fused_computation.179 | loop fusion | flops 4194048 | bytes 10503168 | tf_op jit(solution)/shard_map/convert_element_type | solution.py:212
  226.5 1.5 pad_maximum_fusion.2
  228.0 4.5 %all-to-all-start.3 = ((bf16[258,16,256]{2,0,1:T(8,128)(2,1)}), bf16[258,16,256]{2,0,1:T(8,128)(2,1)S(1)}, u32[]{:S(2)}, u32[]{:S(2)}) async-start(bf16[258,16,256]{2,0,1:T(8,128)(2,1)} %pad_maximum_fusion.2), calls=%async_computation.3 | async-start | bytes 4325376 | tf_op jit(solution)/shard_map/all_to_all | solution.py:217
  232.9 2.4 fusion.97
  238.1 1.1 multiply_reduce_fusion.3
  239.2 21.7 %all-to-all-done.3 = bf16[258,16,256]{2,0,1:T(8,128)(2,1)S(1)} async-done(((bf16[258,16,256]{2,0,1:T(8,128)(2,1)}), bf16[258,16,256]{2,0,1:T(8,128)(2,1)S(1)}, u32[]{:S(2)}, u32[]{:S(2)}) %all-to-all-start.3) | async-done | bytes 2113568 | tf_op jit(solution)/shard_map/all_to_all | solution.py:217
  261.6 1.6 copy-done.1
  264.2 0.9 slice_reduce_fusion.2
  265.6 1.3 broadcast_in_dim.50
  266.9 5.2 %all-to-all-start.4 = ((bf16[8,420,256]{2,1,0:T(8,128)(2,1)}), bf16[8,420,256]{2,1,0:T(8,128)(2,1)S(1)}, u32[]{:S(2)}, u32[]{:S(2)}) async-start(bf16[8,420,256]{2,1,0:T(8,128)(2,1)} %broadcast_in_dim.50), calls=%async_computation.4 | async-start | bytes 3473408 | tf_op jit(solution)/shard_map/all_to_all | solution.py:242
  272.1 2.6 slice.245
  274.8 1.1 dynamic-slice_reduce_fusion
  275.9 0.9 select_reduce_fusion
  276.9 32.4 %all-to-all-done.4 = bf16[8,420,256]{2,1,0:T(8,128)(2,1)S(1)} async-done(((bf16[8,420,256]{2,1,0:T(8,128)(2,1)}), bf16[8,420,256]{2,1,0:T(8,128)(2,1)S(1)}, u32[]{:S(2)}, u32[]{:S(2)}) %all-to-all-start.4) | async-done | bytes 1720352 | tf_op jit(solution)/shard_map/all_to_all | solution.py:242
  312.7 1.1 reshape.183
  315.1 1.4 fusion.14
  316.4 2.7 convolution_convert_fusion.1
  319.2 1.5 fusion.76
  320.7 6.2 %convolution_bitcast_fusion.1 = f32[3,512,256]{1,2,0:T(8,128)} fusion(bf16[3,2048,256]{2,1,0:T(8,128)(2,1)} %all-gather.10.cloned.1.call-done, f32[512]{0:T(512)S(1)} %dynamic-slice_reduce_fusion, f32[2048]{0:T(1024)S(1)} %select_reduce_fusion, s32[2048]{0:T(1024)S(1)} %bitcast.136, s32[]{:T(128)S(6)} %select_n.28, bf16[256,4096]{0,1:T(8,128)(2,1)} %copy-done.5, ...), kind=kOutput, calls=%fused_computation.24 | convolution fusion | flops 2689597440 | bytes 8931332 | tf_op jit(solution)/shard_map/td,jtc->jdc/dot_general | solution.py:269
  327.0 3.0 copy.103
  (185 shorter events, 20.4 us)
Async XLA Ops:
  7.2 60.2 %all-gather.6.cloned.1.call-start = ((), (), s32[]{:S(2)}) async-start(), calls=%async_computation.5 | async-start | bytes 3342336 | tf_op jit(solution)/shard_map/all_gather | solution.py:128
  12.5 5.8 %copy-start.22 = (f32[3,7,256]{2,1,0:T(8,128)S(1)}, f32[3,7,256]{2,1,0:T(8,128)}, u32[]{:S(2)}) copy-start(f32[3,7,256]{2,1,0:T(8,128)} %param.15) | copy-start | bytes 64516
  12.5 37.1 %all-to-all-start = ((bf16[16,256,256]{2,1,0:T(8,128)(2,1)}), bf16[16,256,256]{2,1,0:T(8,128)(2,1)}, u32[]{:S(2)}, u32[]{:S(2)}) async-start(bf16[16,256,256]{2,1,0:T(8,128)(2,1)} %broadcast_in_dim.37), calls=%async_computation | async-start | bytes 4194304 | tf_op jit(solution)/shard_map/all_to_all | solution.py:129
  18.2 139.7 %all-gather.8.cloned.1.call-start = ((), (), s32[]{:S(2)}) async-start(), calls=%async_computation.6 | async-start | bytes 2228224 | tf_op jit(solution)/shard_map/all_gather | solution.py:166
  52.5 17.7 %copy-start.3 = (bf16[16,256,256]{1,2,0:T(8,128)(2,1)}, bf16[16,256,256]{1,2,0:T(8,128)(2,1)S(1)}, u32[]{:S(2)}) copy-start(bf16[16,256,256]{1,2,0:T(8,128)(2,1)S(1)} %copy.94) | copy-start | bytes 6291460
  69.1 5.4 %copy-start.5 = (bf16[256,4096]{0,1:T(8,128)(2,1)}, bf16[256,4096]{0,1:T(8,128)(2,1)S(1)}, u32[]{:S(2)}) copy-start(bf16[256,4096]{0,1:T(8,128)(2,1)S(1)} %slice.226) | copy-start | bytes 6291460
  69.1 1.1 copy-start.32
  69.1 8.1 %slice-start.1 = ((s8[6291456]{0:T(1024)(128)(4,1)}), s8[4194304]{0:T(1024)(128)(4,1)S(1)}, s32[]{:S(2)}) async-start(s8[6291456]{0:T(1024)(128)(4,1)} %bitcast.143), calls=%async_computation.10 | async-start | bytes 8388608
  70.2 4.3 %copy-start.26 = (f32[512]{0:T(512)}, f32[512]{0:T(512)S(1)}, u32[]{:S(2)}) copy-start(f32[512]{0:T(512)S(1)} %add_rsqrt_fusion) | copy-start | bytes 6148
  70.2 4.5 %copy-start = (bf16[263,4096]{0,1:T(8,128)(2,1)S(1)}, bf16[263,4096]{0,1:T(8,128)(2,1)}, u32[]{:S(2)}) copy-start(bf16[263,4096]{0,1:T(8,128)(2,1)} %all-gather.6.cloned.1.call-done) | copy-start | bytes 6463492
  70.2 7.0 %slice-start.2 = ((s8[6291456]{0:T(1024)(128)(4,1)}), s8[2097152]{0:T(1024)(128)(4,1)S(1)}, s32[]{:S(2)}) async-start(s8[6291456]{0:T(1024)(128)(4,1)} %bitcast.143), calls=%async_computation.11 | async-start | bytes 4194304
  74.5 2.7 copy-start.11
  74.7 2.5 copy-start.30
  77.2 6.7 %copy-start.42 = (f32[256]{0:T(256)S(1)}, f32[256]{0:T(256)}, u32[]{:S(2)}) copy-start(f32[256]{0:T(256)} %param.17) | copy-start | bytes 3076
  77.2 15.4 %copy-start.17 = (f32[128,256]{1,0:T(8,128)S(1)}, f32[128,256]{1,0:T(8,128)}, u32[]{:S(2)}) copy-start(f32[128,256]{1,0:T(8,128)} %param.16) | copy-start | bytes 393220
  79.1 7.8 %copy-start.13 = (bf16[256,3,256]{2,0,1:T(8,128)(2,1)}, bf16[256,3,256]{2,0,1:T(8,128)(2,1)S(1)}, u32[]{:S(2)}) copy-start(bf16[256,3,256]{2,0,1:T(8,128)(2,1)S(1)} %fusion.9) | copy-start | bytes 1179652
  79.1 6.2 %collective-permute-start = (bf16[6,3,256]{2,0,1:T(8,128)(2,1)S(1)}, bf16[6,3,256]{2,0,1:T(8,128)(2,1)S(1)}, u32[]{:S(2)}, u32[]{:S(2)}) collective-permute-start(bf16[6,3,256]{2,0,1:T(8,128)(2,1)S(1)} %slice.230), channel_id=1, source_target_pairs={{0,1},{1,2},{2,3},{3,4},{4,5},{5,6},{6,7},{8,9},{9,10},{10,11},{11... | collective-permute-start | bytes 27656 | tf_op jit(solution)/shard_map/ppermute | solution.py:77
  83.9 9.5 %copy-start.41 = (f32[128]{0:T(128)}, f32[128]{0:T(128)S(1)}, u32[]{:S(2)}) copy-start(f32[128]{0:T(128)S(1)} %iota_convert_fusion) | copy-start | bytes 1540
  84.0 17.9 %copy-start.28 = (f32[256]{0:T(256)}, f32[256]{0:T(256)S(1)}, u32[]{:S(2)}) copy-start(f32[256]{0:T(256)S(1)} %neg.7) | copy-start | bytes 3076
  84.0 2.9 copy-start.19
  86.0 0.9 copy-start.6
  86.9 7.6 %collective-permute-start.1 = (bf16[127,256]{1,0:T(8,128)(2,1)S(1)}, bf16[127,256]{1,0:T(8,128)(2,1)S(1)}, u32[]{:S(2)}, u32[]{:S(2)}) collective-permute-start(bf16[127,256]{1,0:T(8,128)(2,1)S(1)} %slice.244), channel_id=1, source_target_pairs={{0,1},{1,2},{2,3},{3,4},{4,5},{5,6},{6,7},{8,9},{9,10},{10,11},{11... | collective-permute-start | bytes 195080 | tf_op jit(solution)/shard_map/ppermute | solution.py:77
  105.9 33.0 %all-to-all-start.1 = ((bf16[256,16,256]{0,2,1:T(8,128)(2,1)}), bf16[256,16,256]{0,2,1:T(8,128)(2,1)}, u32[]{:S(2)}, u32[]{:S(2)}) async-start(bf16[256,16,256]{0,2,1:T(8,128)(2,1)} %bitcast.125), calls=%async_computation.1 | async-start | bytes 4194304 | tf_op jit(solution)/shard_map/all_to_all | solution.py:134
  112.9 48.0 %copy-start.9 = (f32[256,256]{1,0:T(8,128)}, f32[256,256]{1,0:T(8,128)S(1)}, u32[]{:S(2)}) copy-start(f32[256,256]{1,0:T(8,128)S(1)} %fusion.40) | copy-start | bytes 786436
  157.9 3.0 copy-start.24
  160.9 0.7 copy-start.15
  161.5 17.0 %copy-start.12 = (f32[256,256]{1,0:T(8,128)S(1)}, f32[256,256]{1,0:T(8,128)}, u32[]{:S(2)}) copy-start(f32[256,256]{1,0:T(8,128)} %shard_map.177) | copy-start | bytes 786436
  162.2 9.6 %all-to-all-start.2 = ((f32[16,256,4]{1,2,0:T(4,128)}), f32[16,256,4]{1,2,0:T(4,128)S(1)}, u32[]{:S(2)}, u32[]{:S(2)}) async-start(f32[16,256,4]{1,2,0:T(4,128)} %broadcast_in_dim.41), calls=%async_computation.2 | async-start | bytes 131072 | tf_op jit(solution)/shard_map/all_to_all | solution.py:174
  165.7 55.1 %all-gather.12.cloned.1.call-start = ((), (), s32[]{:S(2)}) async-start(), calls=%async_computation.8 | async-start | bytes 1216512 | tf_op jit(solution)/shard_map/all_gather | solution.py:172
  176.3 2.2 copy-start.2
  178.5 3.3 copy-start.18
  178.5 4.0 %copy-start.34 = (bf16[256,4]{0,1:T(4,128)(2,1)S(1)}, bf16[256,4]{0,1:T(4,128)(2,1)}, u32[]{:S(2)}) copy-start(bf16[256,4]{0,1:T(4,128)(2,1)} %convolution_convert_fusion.2) | copy-start | bytes 6148
  178.5 12.2 %copy-start.35 = (f32[384]{0:T(512)S(1)}, f32[384]{0:T(512)}, u32[]{:S(2)}) copy-start(f32[384]{0:T(512)} %pad.24.clone) | copy-start | bytes 4612
  180.3 17.9 %copy-start.7 = (f32[256,3,256]{2,0,1:T(8,128)S(1)}, f32[256,3,256]{2,0,1:T(8,128)}, u32[]{:S(2)}) copy-start(f32[256,3,256]{2,0,1:T(8,128)} %copy-done.6) | copy-start | bytes 2359300
  180.3 10.4 %collective-permute-start.2 = (bf16[127,256]{1,0:T(8,128)(2,1)S(1)}, bf16[127,256]{1,0:T(8,128)(2,1)S(1)}, u32[]{:S(2)}, u32[]{:S(2)}) collective-permute-start(bf16[127,256]{1,0:T(8,128)(2,1)S(1)} %slice.398), channel_id=1, source_target_pairs={{1,0},{2,1},{3,2},{4,3},{5,4},{6,5},{7,6},{9,8},{10,9},{11,10},{12... | collective-permute-start | bytes 195080 | tf_op jit(solution)/shard_map/ppermute | solution.py:77
  190.7 9.8 %copy-start.14 = (bf16[256,3,256]{2,0,1:T(8,128)(2,1)S(1)}, bf16[256,3,256]{2,0,1:T(8,128)(2,1)}, u32[]{:S(2)}) copy-start(bf16[256,3,256]{2,0,1:T(8,128)(2,1)} %copy-done.13) | copy-start | bytes 1179652
  199.2 7.4 %copy-start.8 = (f32[256,1,256]{2,0,1:T(8,128)}, f32[256,1,256]{2,0,1:T(8,128)S(1)}, u32[]{:S(2)}) copy-start(f32[256,1,256]{2,0,1:T(8,128)S(1)} %get-tuple-element.122) | copy-start | bytes 786436
  199.2 7.4 %copy-start.20 = (f32[3,1,256]{2,0,1:T(4,128)S(1)}, f32[3,1,256]{2,0,1:T(4,128)}, u32[]{:S(2)}) copy-start(f32[3,1,256]{2,0,1:T(4,128)} %copy-done.19) | copy-start | bytes 9220
  199.3 7.2 %collective-permute-start.3 = (f32[6,3,256]{2,0,1:T(8,128)S(1)}, f32[6,3,256]{2,0,1:T(8,128)S(1)}, u32[]{:S(2)}, u32[]{:S(2)}) collective-permute-start(f32[6,3,256]{2,0,1:T(8,128)S(1)} %slice.247), channel_id=1, source_target_pairs={{1,0},{2,1},{3,2},{4,3},{5,4},{6,5},{7,6},{9,8},{10,9},{11,10},{12... | collective-permute-start | bytes 55304 | tf_op jit(solution)/shard_map/ppermute | solution.py:77
  228.0 4.8 %copy-start.23 = (bf16[3,7,256]{2,0,1:T(4,128)(2,1)S(1)}, bf16[3,7,256]{2,0,1:T(4,128)(2,1)}, u32[]{:S(2)}) copy-start(bf16[3,7,256]{2,0,1:T(4,128)(2,1)} %constant_dynamic-update-slice_fusion.6) | copy-start | bytes 32260
  228.0 4.8 %copy-start.37 = (bf16[3,256]{1,0:T(4,128)(2,1)S(1)}, bf16[3,256]{1,0:T(4,128)(2,1)}, u32[]{:S(2)}) copy-start(bf16[3,256]{1,0:T(4,128)(2,1)} %get-tuple-element.119) | copy-start | bytes 4612
  228.0 4.8 %copy-start.21 = (f32[3,1,256]{2,0,1:T(4,128)S(1)}, f32[3,1,256]{2,0,1:T(4,128)}, u32[]{:S(2)}) copy-start(f32[3,1,256]{2,0,1:T(4,128)} %copy-done.19) | copy-start | bytes 9220
  228.0 32.9 %all-to-all-start.3 = ((bf16[258,16,256]{2,0,1:T(8,128)(2,1)}), bf16[258,16,256]{2,0,1:T(8,128)(2,1)S(1)}, u32[]{:S(2)}, u32[]{:S(2)}) async-start(bf16[258,16,256]{2,0,1:T(8,128)(2,1)} %pad_maximum_fusion.2), calls=%async_computation.3 | async-start | bytes 4325376 | tf_op jit(solution)/shard_map/all_to_all | solution.py:217
  232.5 88.2 %all-gather.10.cloned.1.call-start = ((), (), s32[]{:S(2)}) async-start(), calls=%async_computation.7 | async-start | bytes 3538944 | tf_op jit(solution)/shard_map/all_gather | solution.py:204
  232.8 5.2 %copy-start.36 = (bf16[3,256]{1,0:T(4,128)(2,1)S(1)}, bf16[3,256]{1,0:T(4,128)(2,1)}, u32[]{:S(2)}) copy-start(bf16[3,256]{1,0:T(4,128)(2,1)} %get-tuple-element.120) | copy-start | bytes 4612
  232.9 5.2 %copy-start.29 = (f32[256]{0:T(256)S(1)}, f32[256]{0:T(256)}, u32[]{:S(2)}) copy-start(f32[256]{0:T(256)} %copy-done.28) | copy-start | bytes 3076
  261.3 2.0 copy-start.1
  261.3 2.0 copy-start.10
  261.3 2.0 copy-start.31
  261.3 2.1 copy-start.33
  261.3 2.1 copy-start.38
  261.3 2.1 copy-start.39
  261.3 3.8 %copy-start.25 = (bf16[256,4]{0,1:T(4,128)(2,1)S(1)}, bf16[256,4]{0,1:T(4,128)(2,1)}, u32[]{:S(2)}) copy-start(bf16[256,4]{0,1:T(4,128)(2,1)} %param.19) | copy-start | bytes 6148
  261.3 3.8 %copy-start.40 = (f32[256]{0:T(256)S(1)}, f32[256]{0:T(256)}, u32[]{:S(2)}) copy-start(f32[256]{0:T(256)} %param.13) | copy-start | bytes 3076
  266.9 42.4 %all-to-all-start.4 = ((bf16[8,420,256]{2,1,0:T(8,128)(2,1)}), bf16[8,420,256]{2,1,0:T(8,128)(2,1)S(1)}, u32[]{:S(2)}, u32[]{:S(2)}) async-start(bf16[8,420,256]{2,1,0:T(8,128)(2,1)} %broadcast_in_dim.50), calls=%async_computation.4 | async-start | bytes 3473408 | tf_op jit(solution)/shard_map/all_to_all | solution.py:242
  272.1 3.8 %copy-start.16 = (bf16[8,258,256]{2,1,0:T(8,128)(2,1)S(1)}, bf16[8,258,256]{2,1,0:T(8,128)(2,1)}, u32[]{:S(2)}) copy-start(bf16[8,258,256]{2,1,0:T(8,128)(2,1)} %all-gather.12.cloned.1.call-done) | copy-start | bytes 3170308
  272.1 3.8 %copy-start.27 = (f32[512]{0:T(512)S(1)}, f32[512]{0:T(512)}, u32[]{:S(2)}) copy-start(f32[512]{0:T(512)} %copy-done.26) | copy-start | bytes 6148
  315.1 4.1 %slice-start = ((bf16[8,258,256]{2,1,0:T(8,128)(2,1)}), bf16[8,256,256]{2,1,0:T(8,128)(2,1)S(1)}, s32[]{:S(2)}) async-start(bf16[8,258,256]{2,1,0:T(8,128)(2,1)} %all-gather.12.cloned.1.call-done), calls=%async_computation.9 | async-start | bytes 2097152 | tf_op jit(solution)/shard_map/slice | solution.py:253
  319.2 1.6 copy-start.4
Sparse Core Ops, SparseCore 0:
  11.1 56.1 all-gather.5
  102.0 55.8 all-gather.7
  168.8 51.9 all-gather.11
  235.4 84.2 all-gather.9

commit v6 on v5

--- a/solution.py
+++ b/solution.py
@@ -201,7 +201,9 @@
         shorts.append(jnp.sum(dz * p_ext[taps - 1 - s : taps - 1 - s + rows].astype(f32), axis=0))
     short_part = jnp.stack(shorts, axis=1)
     dpb = dp.astype(bf16)
-    dp_all = lax.all_gather(jnp.transpose(dpb, (1, 0, 2)), "ctx", axis=1, tiled=True)
+    dp01_all = lax.all_gather(
+        jnp.transpose(dpb[:, :2], (1, 0, 2)), "ctx", axis=1, tiled=True
+    )
     du_part = jnp.einsum("tjc,jdc->td", dpb, w_in, preferred_element_type=f32)
     du_part, h_ids_all = lax.optimization_barrier((du_part, h_ids_all))
     dot_part = jnp.sum(du_part * gain_full[None, :] * x0_full, axis=1)
@@ -235,15 +237,21 @@
     n_small = small.shape[0]
     dlog_parts = split2(dlog.reshape(-1))
     tail = jnp.concatenate([small.astype(bf16)] + dlog_parts)
+    v_rows = vocab // n_ctx
+    embed_part = jnp.dot(id_hot.astype(f32).T, dx0, precision=high)
+    common = jnp.concatenate([dpb[:, 2], as_rows(tail, cw)], axis=0)
     final = jnp.concatenate(
-        [dx0.astype(bf16), as_rows(tail, cw)],
-        axis=0,
-    )
-    final_all = lax.all_to_all(
-        jnp.broadcast_to(final[None], (n_ctx,) + final.shape), "ctx", 0, 0, tiled=True
-    )
-    dx0_all = final_all[:, :rows].reshape(seq, cw).astype(f32)
-    tail_all = final_all[:, rows:].reshape(n_ctx, -1).astype(f32)
+        [
+            embed_part.astype(bf16).reshape(n_ctx, v_rows, cw),
+            jnp.broadcast_to(common[None], (n_ctx,) + common.shape),
+        ],
+        axis=1,
+    )
+    final_all = lax.all_to_all(final, "ctx", 0, 0, tiled=True)
+    d_embed = jnp.sum(final_all[:, :v_rows].astype(f32), axis=0)
+    dp2_all = final_all[:, v_rows : v_rows + rows].reshape(seq, cw)
+    dp_all = jnp.concatenate([dp01_all, dp2_all[None]], axis=0)
+    tail_all = final_all[:, v_rows + rows :].reshape(n_ctx, -1).astype(f32)
     small_tot = jnp.sum(tail_all[:, :n_small], axis=0)
     n_dlog = rows * n_tags
     dlog_all = (
@@ -268,9 +276,6 @@
     u_k = (x0_k * r_all * gain_k[None, :]).astype(bf16)
     d_w_in = jnp.einsum("td,jtc->jdc", u_k, dp_all, preferred_element_type=f32)
 
-    v_rows = vocab // n_ctx
-    own_hot = (ids_all[:, None] == (k_ctx * v_rows + jnp.arange(v_rows))[None, :]).astype(f32)
-    d_embed = jnp.dot(own_hot.T, dx0_all, precision=high)
 
     pos = 0
     outs = []

time: 341 us -> 351 us (1.029)
  local copies, waits for them, and re-layouts: 41.3 us -> 58.9 us
  waiting for transfers between devices: 167 us -> 155 us
  other arithmetic: 29.5 us -> 35.4 us
    concatenate x1, local copies, waits for them, and re-layouts: 0.76 us -> 6.14 us  [block(): tail = jnp.concatenate([small.astype(bf16)] + dlog_parts)]
    all_to_all x1, waiting for transfers between devices: 21.7 us -> 17.6 us  [block(): du_recv = lax.all_to_all(du_send, 'dp', 1, 1, tiled=True).astype(f32)]
    unnamed x108 -> x122, local copies, waits for them, and re-layouts: 11.5 us -> 15.3 us
    all_to_all x1, waiting for transfers between devices: 32.4 us -> 28.7 us  [block(): final_all = lax.all_to_all(final, 'ctx', 0, 0, tiled=True)]
  transfers between devices with their start and end apart: 13 -> 13, of which waited for: 12 -> 12; matrix products, arithmetic and copies ran while one was open for 19% -> 22% of each run, Pallas kernels for 2% -> 2%
where the time goes in v6:
time: 351 us; the launch traced here: 349 us
  waiting for transfers between devices  155 us (44%)
  local copies, waits for them, and re-layouts  58.9 us (17%)
  starting transfers between devices  37.5 us (11%)
  other arithmetic  35.4 us (10%)
  matrix products  34.9 us (10%)
  between operations  16.7 us (5%)
  Pallas kernels  11.3 us (3%)
    all_to_all x1, waiting for transfers between devices, block(): lax.all_to_all(jnp.broadcast_to(embed[None, half:], (n_dp, vocab - half,...  31.2 us
    all_to_all x1, waiting for transfers between devices, block(): final_all = lax.all_to_all(final, 'ctx', 0, 0, tiled=True)  28.7 us
    all_to_all x1, waiting for transfers between devices, block(): w_out_cols = lax.all_to_all(w_out_later, 'dp', 1, 0, tiled=True)  26 us
    all_to_all x1, waiting for transfers between devices, block(): du_recv = lax.all_to_all(du_send, 'dp', 1, 1, tiled=True).astype(f32)  17.6 us
    unnamed x122, local copies, waits for them, and re-layouts  15.3 us
    all_gather x1, waiting for transfers between devices, block(): h_full = lax.all_gather(h, 'dp', axis=1, tiled=True)  15.1 us
    all_gather x1, waiting for transfers between devices, block(): packed_full = lax.all_gather(packed, 'dp', axis=1, tiled=True)  14.8 us
    ppermute x4, starting transfers between devices, shifted(): return lax.ppermute(block, axis, route)  13.1 us
  transfers between devices with their start and end apart: 13, of which 12 were waited for; matrix products, arithmetic and copies ran while one was open for 22% of the time, Pallas kernels for 2%

profile of v6, /device:TPU:0, one launch (start us, length us, event | category | flops | bytes accessed | tf_op | source)
XLA Modules:
  0.0 349.2 jit_solution(3343585827546151185)
XLA Ops:
  11.0 1.5 broadcast_in_dim.37
  12.5 5.7 %all-to-all-start = ((bf16[16,256,256]{2,1,0:T(8,128)(2,1)}), bf16[16,256,256]{2,1,0:T(8,128)(2,1)}, u32[]{:S(2)}, u32[]{:S(2)}) async-start(bf16[16,256,256]{2,1,0:T(8,128)(2,1)} %broadcast_in_dim.37), calls=%async_computation | async-start | bytes 4194304 | tf_op jit(solution)/shard_map/all_to_all | solution.py:129
  18.4 31.2 %all-to-all-done = bf16[16,256,256]{2,1,0:T(8,128)(2,1)} async-done(((bf16[16,256,256]{2,1,0:T(8,128)(2,1)}), bf16[16,256,256]{2,1,0:T(8,128)(2,1)}, u32[]{:S(2)}, u32[]{:S(2)}) %all-to-all-start) | async-done | bytes 2097184 | tf_op jit(solution)/shard_map/all_to_all | solution.py:129
  49.6 2.8 copy.97
  52.5 14.8 %all-gather.6.cloned.1.call-done = bf16[263,4096]{0,1:T(8,128)(2,1)} async-done(((bf16[263,256]{0,1:T(8,128)(2,1)}), bf16[263,4096]{0,1:T(8,128)(2,1)}) %all-gather.6.cloned.1.call-update) | async-done | bytes 2154512 | tf_op jit(solution)/shard_map/all_gather | solution.py:128
  67.3 1.7 slice.238
  70.2 4.3 %fusion.6 = f32[256,4096]{1,0:T(8,128)S(1)} fusion(bf16[256,4096]{0,1:T(8,128)(2,1)} %bitcast.127, bf16[256,4096]{0,1:T(8,128)(2,1)S(1)} %slice.238, s32[256]{0:T(256)S(1)} %copy-done.41), kind=kOutput, calls=%fused_computation.19 | convolution fusion | flops 1082261504 | bytes 8389632 | tf_op jit(solution)/shard_map/dot_general | solution.py:147
  74.7 2.4 fusion.73
  77.2 1.9 fusion.16
  79.1 4.8 %collective-permute-start = (bf16[6,3,256]{2,0,1:T(8,128)(2,1)S(1)}, bf16[6,3,256]{2,0,1:T(8,128)(2,1)S(1)}, u32[]{:S(2)}, u32[]{:S(2)}) collective-permute-start(bf16[6,3,256]{2,0,1:T(8,128)(2,1)S(1)} %slice.242), channel_id=1, source_target_pairs={{0,1},{1,2},{2,3},{3,4},{4,5},{5,6},{6,7},{8,9},{9,10},{10,11},{11... | collective-permute-start | bytes 27656 | tf_op jit(solution)/shard_map/ppermute | solution.py:77
  84.0 1.3 collective-permute-done
  87.0 5.7 %collective-permute-start.1 = (bf16[127,256]{1,0:T(8,128)(2,1)S(1)}, bf16[127,256]{1,0:T(8,128)(2,1)S(1)}, u32[]{:S(2)}, u32[]{:S(2)}) collective-permute-start(bf16[127,256]{1,0:T(8,128)(2,1)S(1)} %slice.256), channel_id=1, source_target_pairs={{0,1},{1,2},{2,3},{3,4},{4,5},{5,6},{6,7},{8,9},{9,10},{10,11},{11... | collective-permute-start | bytes 195080 | tf_op jit(solution)/shard_map/ppermute | solution.py:77
  95.4 4.7 %shard_map.177 = f32[256,256]{1,0:T(8,128)} custom-call(f32[384,256]{1,0:T(8,128)} %maximum_convert_fusion.kv_ref, f32[128,256]{1,0:T(8,128)} %fusion.55.g_ref), custom_call_target="tpu_custom_call" | custom-call | tf_op jit(solution)/shard_map/pallas_call | solution.py:23
  100.1 1.7 multiply_convert_fusion.2
  101.9 4.1 %copy.98 = bf16[256,4096]{0,1:T(8,128)(2,1)} copy(bf16[256,4096]{1,0:T(8,128)(2,1)} %param.18) | data formatting | bytes 4194304 | tf_op jit(solution)/shard_map/optimization_barrier | solution.py:133
  106.0 4.4 %all-to-all-start.1 = ((bf16[256,16,256]{0,2,1:T(8,128)(2,1)}), bf16[256,16,256]{0,2,1:T(8,128)(2,1)}, u32[]{:S(2)}, u32[]{:S(2)}) async-start(bf16[256,16,256]{0,2,1:T(8,128)(2,1)} %bitcast.129), calls=%async_computation.1 | async-start | bytes 4194304 | tf_op jit(solution)/shard_map/all_to_all | solution.py:134
  111.7 1.2 fusion.43
  113.0 26.0 %all-to-all-done.1 = bf16[256,16,256]{0,2,1:T(8,128)(2,1)} async-done(((bf16[256,16,256]{0,2,1:T(8,128)(2,1)}), bf16[256,16,256]{0,2,1:T(8,128)(2,1)}, u32[]{:S(2)}, u32[]{:S(2)}) %all-to-all-start.1) | async-done | bytes 2097184 | tf_op jit(solution)/shard_map/all_to_all | solution.py:134
  138.9 3.9 %copy.99 = bf16[16,256,256]{2,1,0:T(8,128)(2,1)} copy(bf16[16,256,256]{1,2,0:T(8,128)(2,1)} %bitcast.8) | data formatting | bytes 4194304 | tf_op jit(solution)/shard_map/all_to_all | solution.py:134
  142.8 15.1 %all-gather.8.cloned.1.call-done = bf16[256,4096]{1,0:T(8,128)(2,1)} async-done(((bf16[256,256]{1,0:T(8,128)(2,1)}), bf16[256,4096]{1,0:T(8,128)(2,1)}) %all-gather.8.cloned.1.call-update) | async-done | bytes 2097168 | tf_op jit(solution)/shard_map/all_gather | solution.py:166
  157.9 2.9 fusion.19
  161.7 3.5 %all-to-all-start.2 = ((f32[16,256,4]{1,2,0:T(4,128)}), f32[16,256,4]{1,2,0:T(4,128)S(1)}, u32[]{:S(2)}, u32[]{:S(2)}) async-start(f32[16,256,4]{1,2,0:T(4,128)} %broadcast_in_dim.41), calls=%async_computation.2 | async-start | bytes 131072 | tf_op jit(solution)/shard_map/all_to_all | solution.py:174
  165.5 1.6 maximum_bitcast_fusion
  167.1 4.3 %all-to-all-done.2 = f32[16,256,4]{1,2,0:T(4,128)S(1)} async-done(((f32[16,256,4]{1,2,0:T(4,128)}), f32[16,256,4]{1,2,0:T(4,128)S(1)}, u32[]{:S(2)}, u32[]{:S(2)}) %all-to-all-start.2) | async-done | bytes 65568 | tf_op jit(solution)/shard_map/all_to_all | solution.py:174
  175.0 2.2 convolution_convert_fusion
  177.2 1.8 multiply_bitcast_fusion.2
  180.3 1.3 collective-permute-start.2
  184.8 5.6 %collective-permute-done.2 = bf16[127,256]{1,0:T(8,128)(2,1)S(1)} collective-permute-done((bf16[127,256]{1,0:T(8,128)(2,1)}, bf16[127,256]{1,0:T(8,128)(2,1)S(1)}, u32[]{:S(2)}, u32[]{:S(2)}) %collective-permute-start.2) | collective-permute-done | bytes 65056 | tf_op jit(solution)/shard_map/ppermute | solution.py:77
  190.3 1.8 maximum_maximum_fusion.dm_ref
  192.1 6.6 %shard_map.178 = (f32[256,256]{1,0:T(8,128)}, f32[128,256]{1,0:T(8,128)}) custom-call(f32[384,256]{1,0:T(8,128)} %maximum_maximum_fusion.dm_ref, f32[384,256]{1,0:T(8,128)} %maximum_convert_fusion.kv_ref, f32[128,256]{1,0:T(8,128)} %fusion.55.g_ref), custom_call_target="tpu_custom_call" | custom-call | tf_op jit(solution)/shard_map/pallas_call | solution.py:55
  198.7 1.2 multiply_bitcast_fusion.1
  200.1 1.3 collective-permute-start.3
  201.4 1.3 fusion.31
  203.3 4.1 %collective-permute-done.3 = f32[6,3,256]{2,0,1:T(8,128)S(1)} collective-permute-done((f32[6,3,256]{2,0,1:T(8,128)S(1)}, f32[6,3,256]{2,0,1:T(8,128)S(1)}, u32[]{:S(2)}, u32[]{:S(2)}) %collective-permute-start.3) | collective-permute-done | bytes 18464 | tf_op jit(solution)/shard_map/ppermute | solution.py:77
  209.0 6.7 %convolution_bitcast_fusion = f32[256,4096]{1,0:T(8,128)} fusion(bf16[256,3,256]{2,0,1:T(8,128)(2,1)S(1)} %fusion.34, bf16[3,4096,256]{2,1,0:T(8,128)(2,1)} %param.14), kind=kOutput, calls=%fused_computation.1 | convolution fusion | flops 1610612736 | bytes 10878976 | tf_op jit(solution)/shard_map/tjc,jdc->td/dot_general | solution.py:207
  215.7 4.7 %all-gather.12.cloned.1.call-done = bf16[8,258,256]{2,1,0:T(8,128)(2,1)} async-done(((bf16[1,258,256]{2,1,0:T(8,128)(2,1)}), bf16[8,258,256]{2,1,0:T(8,128)(2,1)}) %all-gather.12.cloned.1.call-update) | async-done | bytes 1056784 | tf_op jit(solution)/shard_map/all_gather | solution.py:172
  220.4 5.3 %fusion.74 = (bf16[256,4096]{1,0:T(8,128)(2,1)S(1)}, f32[256]{0:T(256)S(1)}) fusion(f32[256,4096]{1,0:T(8,128)} %convolution_bitcast_fusion, f32[256,4096]{1,0:T(8,128)} %copy-done.11, f32[4096]{0:T(1024)S(1)} %copy-done.21), kind=kLoop, calls=%fused_computation.183 | loop fusion | flops 4194048 | bytes 10503168 | tf_op jit(solution)/shard_map/convert_element_type | solution.py:214
  226.0 1.5 pad_maximum_fusion.2
  227.5 4.6 %all-to-all-start.3 = ((bf16[258,16,256]{2,0,1:T(8,128)(2,1)}), bf16[258,16,256]{2,0,1:T(8,128)(2,1)}, u32[]{:S(2)}, u32[]{:S(2)}) async-start(bf16[258,16,256]{2,0,1:T(8,128)(2,1)} %pad_maximum_fusion.2), calls=%async_computation.3 | async-start | bytes 4325376 | tf_op jit(solution)/shard_map/all_to_all | solution.py:219
  232.4 1.3 constant_dynamic-update-slice_fusion.5
  233.6 1.2 constant_dynamic-update-slice_fusion.4
  234.9 1.3 constant_dynamic-update-slice_fusion.3
  239.2 1.1 multiply_reduce_fusion.3
  242.9 17.6 %all-to-all-done.3 = bf16[258,16,256]{2,0,1:T(8,128)(2,1)} async-done(((bf16[258,16,256]{2,0,1:T(8,128)(2,1)}), bf16[258,16,256]{2,0,1:T(8,128)(2,1)}, u32[]{:S(2)}, u32[]{:S(2)}) %all-to-all-start.3) | async-done | bytes 2113568 | tf_op jit(solution)/shard_map/all_to_all | solution.py:219
  260.6 1.9 convert_element_type.198
  262.8 1.7 copy-done.1
  265.2 6.1 %concatenate.56 = bf16[41729]{0:T(1024)(128)(2,1)} concatenate(bf16[256]{0:T(256)(128)(2,1)} %multiply_reduce_fusion.2, bf16[5376]{0:T(1024)(128)(2,1)S(1)} %copy-done.22, bf16[32768]{0:T(1024)(128)(2,1)} %bitcast.138, bf16[256]{0:T(256)(128)(2,1)} %negate_convert_fusion, bf16[1024]{0:T(1024)(128)(2,1)} %reshape.174, bf16[1]{0:T(256)(128)(2,1)} %bitcast.27, ...), dimensions={0} | concatenate | bytes 166916 | tf_op jit(solution)/shard_map/concatenate | solution.py:239
  271.4 1.5 pad.4
  272.9 1.6 reshape.175
  276.3 1.3 convolution_add_fusion
  277.6 1.4 convolution_convert_fusion.2
  279.1 1.4 pad_maximum_fusion.3
  280.6 5.7 %all-to-all-start.4 = ((bf16[8,484,256]{2,1,0:T(8,128)(2,1)}), bf16[8,484,256]{2,1,0:T(8,128)(2,1)}, u32[]{:S(2)}, u32[]{:S(2)}) async-start(bf16[8,484,256]{2,1,0:T(8,128)(2,1)} %pad_maximum_fusion.3), calls=%async_computation.4 | async-start | bytes 3997696 | tf_op jit(solution)/shard_map/all_to_all | solution.py:250
  286.2 1.4 slice.257
  287.6 1.1 dynamic-slice_reduce_fusion
  289.7 28.7 %all-to-all-done.4 = bf16[8,484,256]{2,1,0:T(8,128)(2,1)} async-done(((bf16[8,484,256]{2,1,0:T(8,128)(2,1)}), bf16[8,484,256]{2,1,0:T(8,128)(2,1)}, u32[]{:S(2)}, u32[]{:S(2)}) %all-to-all-start.4) | async-done | bytes 1982496 | tf_op jit(solution)/shard_map/all_to_all | solution.py:250
  318.4 1.1 slice.271
  320.6 1.3 slice.277
  322.6 6.1 %fusion.13 = f32[3,512,256]{1,2,0:T(8,128)} fusion(bf16[1,2048,256]{2,1,0:T(8,128)(2,1)S(1)} %bitcast.135, bf16[2,2048,256]{2,1,0:T(8,128)(2,1)} %all-gather.10.cloned.1.call-done, f32[512]{0:T(512)S(1)} %dynamic-slice_reduce_fusion, f32[2048]{0:T(1024)S(1)} %select_reduce_fusion, s32[2048]{0:T(1024)S(1)} %bitcast.143, s32[]{:T(128)S(6)} %select_n.28, ...), kind=kOutput, calls=%fused_computation.29 | convolution fusion | flops 2691170304 | bytes 8931332 | tf_op jit(solution)/shard_map/td,jtc->jdc/dot_general | solution.py:277
  328.7 3.0 copy.106
  333.9 1.1 reshape.179
  335.7 2.7 convolution_convert_fusion.1
  338.4 1.5 fusion.79
  339.9 1.6 convert_reduce_fusion
  (202 shorter events, 36.1 us)
Async XLA Ops:
  7.2 60.1 %all-gather.6.cloned.1.call-start = ((), (), s32[]{:S(2)}) async-start(), calls=%async_computation.5 | async-start | bytes 3342336 | tf_op jit(solution)/shard_map/all_gather | solution.py:128
  12.5 5.8 %copy-start.37 = (f32[3,7,256]{2,1,0:T(8,128)S(1)}, f32[3,7,256]{2,1,0:T(8,128)}, u32[]{:S(2)}) copy-start(f32[3,7,256]{2,1,0:T(8,128)} %param.15) | copy-start | bytes 64516
  12.5 37.1 %all-to-all-start = ((bf16[16,256,256]{2,1,0:T(8,128)(2,1)}), bf16[16,256,256]{2,1,0:T(8,128)(2,1)}, u32[]{:S(2)}, u32[]{:S(2)}) async-start(bf16[16,256,256]{2,1,0:T(8,128)(2,1)} %broadcast_in_dim.37), calls=%async_computation | async-start | bytes 4194304 | tf_op jit(solution)/shard_map/all_to_all | solution.py:129
  18.2 139.7 %all-gather.8.cloned.1.call-start = ((), (), s32[]{:S(2)}) async-start(), calls=%async_computation.6 | async-start | bytes 2228224 | tf_op jit(solution)/shard_map/all_gather | solution.py:166
  18.3 67.0 %copy-start.23 = (f32[3,256]{1,0:T(4,128)}, f32[3,256]{1,0:T(4,128)S(1)}, u32[]{:S(2)}) copy-start(f32[3,256]{1,0:T(4,128)S(1)} %get-tuple-element.149) | copy-start | bytes 9220
  18.3 67.0 %copy-start.25 = (f32[3,256]{1,0:T(4,128)}, f32[3,256]{1,0:T(4,128)S(1)}, u32[]{:S(2)}) copy-start(f32[3,256]{1,0:T(4,128)S(1)} %get-tuple-element.150) | copy-start | bytes 9220
  18.3 66.9 %copy-start.27 = (f32[3,256]{1,0:T(4,128)}, f32[3,256]{1,0:T(4,128)S(1)}, u32[]{:S(2)}) copy-start(f32[3,256]{1,0:T(4,128)S(1)} %get-tuple-element.151) | copy-start | bytes 9220
  18.4 66.9 %copy-start.29 = (f32[3,256]{1,0:T(4,128)}, f32[3,256]{1,0:T(4,128)S(1)}, u32[]{:S(2)}) copy-start(f32[3,256]{1,0:T(4,128)S(1)} %get-tuple-element.152) | copy-start | bytes 9220
  18.4 66.9 %copy-start.31 = (f32[3,256]{1,0:T(4,128)}, f32[3,256]{1,0:T(4,128)S(1)}, u32[]{:S(2)}) copy-start(f32[3,256]{1,0:T(4,128)S(1)} %get-tuple-element.147) | copy-start | bytes 9220
  18.4 66.9 %copy-start.33 = (f32[3,256]{1,0:T(4,128)}, f32[3,256]{1,0:T(4,128)S(1)}, u32[]{:S(2)}) copy-start(f32[3,256]{1,0:T(4,128)S(1)} %get-tuple-element.148) | copy-start | bytes 9220
  52.5 17.6 %copy-start.3 = (bf16[16,256,256]{1,2,0:T(8,128)(2,1)}, bf16[16,256,256]{1,2,0:T(8,128)(2,1)S(1)}, u32[]{:S(2)}) copy-start(bf16[16,256,256]{1,2,0:T(8,128)(2,1)S(1)} %copy.97) | copy-start | bytes 6291460
  69.0 5.4 %copy-start.5 = (bf16[256,4096]{0,1:T(8,128)(2,1)}, bf16[256,4096]{0,1:T(8,128)(2,1)S(1)}, u32[]{:S(2)}) copy-start(bf16[256,4096]{0,1:T(8,128)(2,1)S(1)} %slice.238) | copy-start | bytes 6291460
  69.1 1.1 copy-start.41
  69.1 8.1 %slice-start = ((s8[6291456]{0:T(1024)(128)(4,1)}), s8[4194304]{0:T(1024)(128)(4,1)S(1)}, s32[]{:S(2)}) async-start(s8[6291456]{0:T(1024)(128)(4,1)} %bitcast.124), calls=%async_computation.9 | async-start | bytes 8388608
  70.1 4.3 %copy-start.39 = (f32[512]{0:T(512)}, f32[512]{0:T(512)S(1)}, u32[]{:S(2)}) copy-start(f32[512]{0:T(512)S(1)} %add_rsqrt_fusion) | copy-start | bytes 6148
  70.1 4.5 %copy-start = (bf16[263,4096]{0,1:T(8,128)(2,1)S(1)}, bf16[263,4096]{0,1:T(8,128)(2,1)}, u32[]{:S(2)}) copy-start(bf16[263,4096]{0,1:T(8,128)(2,1)} %all-gather.6.cloned.1.call-done) | copy-start | bytes 6463492
  70.2 7.0 %slice-start.1 = ((s8[6291456]{0:T(1024)(128)(4,1)}), s8[2097152]{0:T(1024)(128)(4,1)S(1)}, s32[]{:S(2)}) async-start(s8[6291456]{0:T(1024)(128)(4,1)} %bitcast.124), calls=%async_computation.10 | async-start | bytes 4194304
  74.5 2.7 copy-start.11
  74.7 2.5 copy-start.43
  77.2 1.9 copy-start.20
  77.2 6.7 %copy-start.49 = (f32[256]{0:T(256)S(1)}, f32[256]{0:T(256)}, u32[]{:S(2)}) copy-start(f32[256]{0:T(256)} %param.17) | copy-start | bytes 3076
  77.2 15.5 %copy-start.18 = (f32[128,256]{1,0:T(8,128)S(1)}, f32[128,256]{1,0:T(8,128)}, u32[]{:S(2)}) copy-start(f32[128,256]{1,0:T(8,128)} %param.16) | copy-start | bytes 393220
  79.1 7.8 %copy-start.13 = (bf16[256,3,256]{2,0,1:T(8,128)(2,1)}, bf16[256,3,256]{2,0,1:T(8,128)(2,1)S(1)}, u32[]{:S(2)}) copy-start(bf16[256,3,256]{2,0,1:T(8,128)(2,1)S(1)} %fusion.16) | copy-start | bytes 1179652
  79.1 6.2 %collective-permute-start = (bf16[6,3,256]{2,0,1:T(8,128)(2,1)S(1)}, bf16[6,3,256]{2,0,1:T(8,128)(2,1)S(1)}, u32[]{:S(2)}, u32[]{:S(2)}) collective-permute-start(bf16[6,3,256]{2,0,1:T(8,128)(2,1)S(1)} %slice.242), channel_id=1, source_target_pairs={{0,1},{1,2},{2,3},{3,4},{4,5},{5,6},{6,7},{8,9},{9,10},{10,11},{11... | collective-permute-start | bytes 27656 | tf_op jit(solution)/shard_map/ppermute | solution.py:77
  83.9 17.9 %copy-start.48 = (f32[128]{0:T(128)}, f32[128]{0:T(128)S(1)}, u32[]{:S(2)}) copy-start(f32[128]{0:T(128)S(1)} %iota_convert_fusion) | copy-start | bytes 1540
  83.9 17.9 %copy-start.42 = (f32[256]{0:T(256)}, f32[256]{0:T(256)S(1)}, u32[]{:S(2)}) copy-start(f32[256]{0:T(256)S(1)} %neg.7) | copy-start | bytes 3076
  84.0 17.9 %copy-start.35 = (f32[3,1,256]{2,0,1:T(4,128)}, f32[3,1,256]{2,0,1:T(4,128)S(1)}, u32[]{:S(2)}) copy-start(f32[3,1,256]{2,0,1:T(4,128)S(1)} %copy.131) | copy-start | bytes 9220
  86.0 0.9 copy-start.6
  87.0 7.6 %collective-permute-start.1 = (bf16[127,256]{1,0:T(8,128)(2,1)S(1)}, bf16[127,256]{1,0:T(8,128)(2,1)S(1)}, u32[]{:S(2)}, u32[]{:S(2)}) collective-permute-start(bf16[127,256]{1,0:T(8,128)(2,1)S(1)} %slice.256), channel_id=1, source_target_pairs={{0,1},{1,2},{2,3},{3,4},{4,5},{5,6},{6,7},{8,9},{9,10},{10,11},{11... | collective-permute-start | bytes 195080 | tf_op jit(solution)/shard_map/ppermute | solution.py:77
  106.0 33.0 %all-to-all-start.1 = ((bf16[256,16,256]{0,2,1:T(8,128)(2,1)}), bf16[256,16,256]{0,2,1:T(8,128)(2,1)}, u32[]{:S(2)}, u32[]{:S(2)}) async-start(bf16[256,16,256]{0,2,1:T(8,128)(2,1)} %bitcast.129), calls=%async_computation.1 | async-start | bytes 4194304 | tf_op jit(solution)/shard_map/all_to_all | solution.py:134
  112.9 47.9 %copy-start.9 = (f32[256,256]{1,0:T(8,128)}, f32[256,256]{1,0:T(8,128)S(1)}, u32[]{:S(2)}) copy-start(f32[256,256]{1,0:T(8,128)S(1)} %fusion.43) | copy-start | bytes 786436
  157.9 3.0 copy-start.38
  160.9 18.0 %copy-start.16 = (bf16[256,256]{1,0:T(8,128)(2,1)}, bf16[256,256]{1,0:T(8,128)(2,1)S(1)}, u32[]{:S(2)}) copy-start(bf16[256,256]{1,0:T(8,128)(2,1)S(1)} %fusion.19) | copy-start | bytes 393220
  161.7 9.6 %all-to-all-start.2 = ((f32[16,256,4]{1,2,0:T(4,128)}), f32[16,256,4]{1,2,0:T(4,128)S(1)}, u32[]{:S(2)}, u32[]{:S(2)}) async-start(f32[16,256,4]{1,2,0:T(4,128)} %broadcast_in_dim.41), calls=%async_computation.2 | async-start | bytes 131072 | tf_op jit(solution)/shard_map/all_to_all | solution.py:174
  165.3 55.1 %all-gather.12.cloned.1.call-start = ((), (), s32[]{:S(2)}) async-start(), calls=%async_computation.8 | async-start | bytes 1216512 | tf_op jit(solution)/shard_map/all_gather | solution.py:172
  175.0 2.2 copy-start.2
  180.3 10.0 %collective-permute-start.2 = (bf16[127,256]{1,0:T(8,128)(2,1)}, bf16[127,256]{1,0:T(8,128)(2,1)S(1)}, u32[]{:S(2)}, u32[]{:S(2)}) collective-permute-start(bf16[127,256]{1,0:T(8,128)(2,1)} %slice.416), channel_id=1, source_target_pairs={{1,0},{2,1},{3,2},{4,3},{5,4},{6,5},{7,6},{9,8},{10,9},{11,10},{12... | collective-permute-start | bytes 195080 | tf_op jit(solution)/shard_map/ppermute | solution.py:77
  198.7 2.7 copy-start.14
  199.9 7.6 %copy-start.24 = (f32[3,256]{1,0:T(4,128)S(1)}, f32[3,256]{1,0:T(4,128)}, u32[]{:S(2)}) copy-start(f32[3,256]{1,0:T(4,128)} %copy-done.23) | copy-start | bytes 9220
  199.9 7.6 %copy-start.26 = (f32[3,256]{1,0:T(4,128)S(1)}, f32[3,256]{1,0:T(4,128)}, u32[]{:S(2)}) copy-start(f32[3,256]{1,0:T(4,128)} %copy-done.25) | copy-start | bytes 9220
  200.0 7.6 %copy-start.28 = (f32[3,256]{1,0:T(4,128)S(1)}, f32[3,256]{1,0:T(4,128)}, u32[]{:S(2)}) copy-start(f32[3,256]{1,0:T(4,128)} %copy-done.27) | copy-start | bytes 9220
  200.0 7.6 %copy-start.30 = (f32[3,256]{1,0:T(4,128)S(1)}, f32[3,256]{1,0:T(4,128)}, u32[]{:S(2)}) copy-start(f32[3,256]{1,0:T(4,128)} %copy-done.29) | copy-start | bytes 9220
  200.0 7.6 %copy-start.32 = (f32[3,256]{1,0:T(4,128)S(1)}, f32[3,256]{1,0:T(4,128)}, u32[]{:S(2)}) copy-start(f32[3,256]{1,0:T(4,128)} %copy-done.31) | copy-start | bytes 9220
  200.0 7.6 %copy-start.34 = (f32[3,256]{1,0:T(4,128)S(1)}, f32[3,256]{1,0:T(4,128)}, u32[]{:S(2)}) copy-start(f32[3,256]{1,0:T(4,128)} %copy-done.33) | copy-start | bytes 9220
  200.0 7.6 %copy-start.36 = (f32[3,1,256]{2,0,1:T(4,128)S(1)}, f32[3,1,256]{2,0,1:T(4,128)}, u32[]{:S(2)}) copy-start(f32[3,1,256]{2,0,1:T(4,128)} %copy-done.35) | copy-start | bytes 9220
  200.1 7.4 %collective-permute-start.3 = (f32[6,3,256]{2,0,1:T(8,128)S(1)}, f32[6,3,256]{2,0,1:T(8,128)S(1)}, u32[]{:S(2)}, u32[]{:S(2)}) collective-permute-start(f32[6,3,256]{2,0,1:T(8,128)S(1)} %slice.259), channel_id=1, source_target_pairs={{1,0},{2,1},{3,2},{4,3},{5,4},{6,5},{7,6},{9,8},{10,9},{11,10},{12... | collective-permute-start | bytes 55304 | tf_op jit(solution)/shard_map/ppermute | solution.py:77
  208.3 0.7 copy-start.7
  209.0 11.4 %copy-start.21 = (f32[4096]{0:T(1024)S(1)}, f32[4096]{0:T(1024)}, u32[]{:S(2)}) copy-start(f32[4096]{0:T(1024)} %copy-done.20) | copy-start | bytes 49156
  227.5 8.6 %copy-start.47 = (bf16[3,256]{1,0:T(4,128)(2,1)S(1)}, bf16[3,256]{1,0:T(4,128)(2,1)}, u32[]{:S(2)}) copy-start(bf16[3,256]{1,0:T(4,128)(2,1)} %get-tuple-element.107) | copy-start | bytes 4612
  227.5 9.2 %copy-start.46 = (bf16[3,256]{1,0:T(4,128)(2,1)S(1)}, bf16[3,256]{1,0:T(4,128)(2,1)}, u32[]{:S(2)}) copy-start(bf16[3,256]{1,0:T(4,128)(2,1)} %get-tuple-element.105) | copy-start | bytes 4612
  227.5 9.8 %copy-start.45 = (bf16[3,256]{1,0:T(4,128)(2,1)S(1)}, bf16[3,256]{1,0:T(4,128)(2,1)}, u32[]{:S(2)}) copy-start(bf16[3,256]{1,0:T(4,128)(2,1)} %get-tuple-element.120) | copy-start | bytes 4612
  227.5 14.0 %copy-start.8 = (bf16[256,3,256]{2,0,1:T(8,128)(2,1)S(1)}, bf16[256,3,256]{2,0,1:T(8,128)(2,1)}, u32[]{:S(2)}) copy-start(bf16[256,3,256]{2,0,1:T(8,128)(2,1)} %copy-done.7) | copy-start | bytes 1179652
  227.5 33.0 %all-to-all-start.3 = ((bf16[258,16,256]{2,0,1:T(8,128)(2,1)}), bf16[258,16,256]{2,0,1:T(8,128)(2,1)}, u32[]{:S(2)}, u32[]{:S(2)}) async-start(bf16[258,16,256]{2,0,1:T(8,128)(2,1)} %pad_maximum_fusion.2), calls=%async_computation.3 | async-start | bytes 4325376 | tf_op jit(solution)/shard_map/all_to_all | solution.py:219
  232.1 90.5 %all-gather.10.cloned.1.call-start = ((), (), s32[]{:S(2)}) async-start(), calls=%async_computation.7 | async-start | bytes 2359296 | tf_op jit(solution)/shard_map/all_gather | solution.py:204
  262.5 2.0 copy-start.1
  262.5 2.0 copy-start.10
  262.5 2.0 copy-start.44
  262.5 2.7 copy-start.22
  262.6 12.8 %copy-start.19 = (bf16[256,256]{1,0:T(8,128)(2,1)S(1)}, bf16[256,256]{1,0:T(8,128)(2,1)}, u32[]{:S(2)}) copy-start(bf16[256,256]{1,0:T(8,128)(2,1)} %slice_bitcast_fusion.4) | copy-start | bytes 393220
  280.6 37.8 %all-to-all-start.4 = ((bf16[8,484,256]{2,1,0:T(8,128)(2,1)}), bf16[8,484,256]{2,1,0:T(8,128)(2,1)}, u32[]{:S(2)}, u32[]{:S(2)}) async-start(bf16[8,484,256]{2,1,0:T(8,128)(2,1)} %pad_maximum_fusion.3), calls=%async_computation.4 | async-start | bytes 3997696 | tf_op jit(solution)/shard_map/all_to_all | solution.py:250
  286.2 2.5 copy-start.17
  286.2 2.5 copy-start.40
  319.8 2.9 copy-start.4
  334.9 3.5 slice-start.2
  (2 other events, 1.4 us)
Sparse Core Ops, SparseCore 0:
  11.1 56.1 all-gather.5
  102.0 55.8 all-gather.7
  168.4 51.9 all-gather.11
  242.4 72.6 all-gather.9
